TPU v7x, 128 devices: a whole 4x4x4 slice. The times are simulated.
128 devices in a mesh: dp: 4 (over z_hi, core), seq: 32 (over x, z_lo, y).
Axes of the slice: x: 4, y: 4, z: 4 (z_hi: 2, z_lo: 2; z = z_hi * 2 + z_lo), core: 2. Of those that a mesh axis runs over, the one named last changes fastest.
Arguments:
- frames_in: bfloat16 [4, 8192, 512], P('dp', 'seq'), may hold values from -6 to 6
- proj_weight: bfloat16 [512, 1536], replicated, may hold values from -0.25 to 0.25
- conv_taps: float32 [3, 1536], replicated, may hold values from -2.5 to 2.5
- long_filters: bfloat16 [8192, 2, 512], P('seq'), as said below
- out_grad: bfloat16 [4, 8192, 512], P('dp', 'seq'), may hold values from -6 to 6
Outputs:
- layer_out: bfloat16 [4, 8192, 512], P('dp', 'seq')
- grad_in: bfloat16 [4, 8192, 512], P('dp', 'seq')
- grad_proj: float32 [512, 1536], P(('dp', 'seq'))
- grad_taps: float32 [3, 1536], replicated
- grad_filters: float32 [8192, 2, 512], P('seq', None, 'dp')
Inputs may be any that keep to these rules, and one draw needn't show every extreme that they name: `long_filters`: taps of the two long filters for every channel.
All inputs are finite; a program needn't handle non-finite values.
Results may differ from a plain program's by a relative error of at most 0.013.
Values may be sent and summed in bfloat16 or wider, within the bound.
No kernel may reach another device: no remote copies, remote signals or barrier semaphores. Data moves between devices by JAX's collectives and lax.ppermute only.
A program may use at most 192 MiB of HBM per device.

v0:
```python
import math

import jax
import jax.numpy as jnp
from jax import lax
from jax.sharding import PartitionSpec as P

PRECISE = lax.Precision.HIGH
FULL_TURN = 2.0 * math.pi


def passed_along(value, axis, by):
    size = lax.axis_size(axis)
    pairs = [(i, i + by) for i in range(size) if 0 <= i + by < size]
    return lax.ppermute(value, axis, pairs)


def angle_table(row_count, col_count, period):
    products = (
        jnp.arange(row_count, dtype=jnp.int32)[:, None]
        * jnp.arange(col_count, dtype=jnp.int32)[None, :]
        % period
    )
    angles = products.astype(jnp.float32) * (FULL_TURN / period)
    return (jnp.cos(angles), jnp.sin(angles))


def rotate_stacked(stacked, cosine_table, sine_table, direction):
    return jnp.stack(
        [
            stacked[0] * cosine_table - direction * stacked[1] * sine_table,
            stacked[1] * cosine_table + direction * stacked[0] * sine_table,
        ]
    )


def dft_pair(cosine_table, sine_table, stacked, table_part, data_part, result_side, direction):
    block_table = jnp.stack(
        [
            jnp.stack([cosine_table, -direction * sine_table]),
            jnp.stack([direction * sine_table, cosine_table]),
        ]
    )
    return jnp.einsum(
        "yz" + table_part + ",z" + data_part + "->y" + result_side,
        block_table,
        stacked,
        precision=PRECISE,
    )


def spectral_product(left_side, right_side):
    return jnp.stack(
        [
            left_side[0] * right_side[0] - left_side[1] * right_side[1],
            left_side[0] * right_side[1] + left_side[1] * right_side[0],
        ]
    )


def adjoint_product(left_side, right_side):
    return jnp.stack(
        [
            left_side[0] * right_side[0] + left_side[1] * right_side[1],
            left_side[0] * right_side[1] - left_side[1] * right_side[0],
        ]
    )


def local_forward(stacked):
    local_freqs, frames, channels = (stacked.shape[1], stacked.shape[2], stacked.shape[3])
    inner_len = math.gcd(frames, 128)
    outer_len = frames // inner_len
    data = stacked.reshape(2, local_freqs, outer_len, inner_len, channels)
    cosine_table, sine_table = angle_table(outer_len, outer_len, outer_len)
    data = dft_pair(cosine_table, sine_table, data, "ga", "kabw", "kgbw", -1.0)
    cosine_table, sine_table = angle_table(outer_len, inner_len, frames)
    data = rotate_stacked(data, cosine_table[None, :, :, None], sine_table[None, :, :, None], -1.0)
    cosine_table, sine_table = angle_table(inner_len, inner_len, inner_len)
    data = dft_pair(cosine_table, sine_table, data, "fb", "kgbw", "kgfw", -1.0)
    return data.reshape(2, local_freqs, frames, channels)


def local_inverse(stacked):
    local_freqs, frames, channels = (stacked.shape[1], stacked.shape[2], stacked.shape[3])
    inner_len = math.gcd(frames, 128)
    outer_len = frames // inner_len
    data = stacked.reshape(2, local_freqs, outer_len, inner_len, channels)
    cosine_table, sine_table = angle_table(inner_len, inner_len, inner_len)
    data = dft_pair(cosine_table, sine_table, data, "bf", "kgfw", "kgbw", 1.0)
    cosine_table, sine_table = angle_table(outer_len, inner_len, frames)
    data = rotate_stacked(data, cosine_table[None, :, :, None], sine_table[None, :, :, None], 1.0)
    cosine_table, sine_table = angle_table(outer_len, outer_len, outer_len)
    data = dft_pair(cosine_table, sine_table, data, "ag", "kgbw", "kabw", 1.0)
    return data.reshape(2, local_freqs, frames, channels) / frames


def forward_transform(field):
    seq_devices = lax.axis_size("seq")
    frames, channels = field.shape
    block_rows = frames // seq_devices
    freq_rows = 2 * seq_devices
    fft_length = freq_rows * frames
    received = lax.all_to_all(
        field.reshape(seq_devices, block_rows, channels),
        "seq",
        split_axis=0,
        concat_axis=0,
        tiled=True,
    )
    values = received.astype(jnp.float32)
    cosine_table, sine_table = angle_table(freq_rows, seq_devices, freq_rows)
    part_table = jnp.stack([cosine_table, -sine_table])
    section = jnp.einsum("ykq,qrw->ykrw", part_table, values, precision=PRECISE)
    frame_ids = lax.axis_index("seq") * block_rows + jnp.arange(block_rows, dtype=jnp.int32)
    products = jnp.arange(freq_rows, dtype=jnp.int32)[:, None] * frame_ids[None, :] % fft_length
    angles = products.astype(jnp.float32) * (FULL_TURN / fft_length)
    stacked = rotate_stacked(
        section, jnp.cos(angles)[:, :, None], jnp.sin(angles)[:, :, None], -1.0
    ).astype(jnp.bfloat16)
    regrouped = lax.all_to_all(stacked, "seq", split_axis=1, concat_axis=2, tiled=True)
    return local_forward(regrouped.astype(jnp.float32))


def inverse_transform(spectra, keep_wide):
    seq_devices = lax.axis_size("seq")
    local_freqs, frames, channels = (spectra.shape[1], spectra.shape[2], spectra.shape[3])
    freq_rows = 2 * seq_devices
    fft_length = freq_rows * frames
    stacked = local_inverse(spectra)
    freq_ids = lax.axis_index("seq") * local_freqs + jnp.arange(local_freqs, dtype=jnp.int32)
    products = freq_ids[:, None] * jnp.arange(frames, dtype=jnp.int32)[None, :] % fft_length
    angles = products.astype(jnp.float32) * (FULL_TURN / fft_length)
    stacked = rotate_stacked(stacked, jnp.cos(angles)[:, :, None], jnp.sin(angles)[:, :, None], 1.0)
    if keep_wide:
        regrouped = lax.all_to_all(
            stacked.astype(jnp.bfloat16), "seq", split_axis=2, concat_axis=1, tiled=True
        ).astype(stacked.dtype)
    else:
        regrouped = lax.all_to_all(
            stacked.astype(jnp.bfloat16), "seq", split_axis=2, concat_axis=1, tiled=True
        ).astype(jnp.float32)
    cosine_table, sine_table = angle_table(seq_devices, freq_rows, freq_rows)
    part_table = jnp.stack([cosine_table, -sine_table])
    values = jnp.einsum("zqk,zkrw->qrw", part_table, regrouped, precision=PRECISE) / freq_rows
    if keep_wide:
        returned = lax.all_to_all(
            values.astype(jnp.bfloat16), "seq", split_axis=0, concat_axis=1, tiled=True
        ).astype(values.dtype)
    else:
        returned = lax.all_to_all(
            values.astype(jnp.bfloat16), "seq", split_axis=0, concat_axis=1, tiled=True
        )
    return returned.reshape(frames, channels)


def shards(frames_in, proj_weight, conv_taps, long_filters, out_grad):
    signal = frames_in[0]
    frames, channels = signal.shape
    seq_devices = lax.axis_size("seq")
    data_devices = lax.axis_size("dp")
    grad_scale = 1.0 / math.sqrt(data_devices * seq_devices * frames)
    margin_rows = conv_taps.shape[0] - 1
    tap_count = conv_taps.shape[0]
    projected = jnp.dot(signal, proj_weight, preferred_element_type=jnp.float32).astype(
        jnp.bfloat16
    )
    before = passed_along(projected[frames - margin_rows :], "seq", 1)
    extended = jnp.concatenate([before, projected], axis=0).astype(jnp.float32)
    mixed = sum(
        (
            conv_taps[tap_index][None, :]
            * extended[margin_rows - tap_index : margin_rows - tap_index + frames]
            for tap_index in range(tap_count)
        )
    ).astype(jnp.bfloat16)
    value = mixed[:, :channels]
    gate_one = mixed[:, channels : 2 * channels].astype(jnp.float32)
    gate_two = mixed[:, 2 * channels :].astype(jnp.float32)
    upstream = out_grad[0].astype(jnp.float32)
    grad_two = (upstream * gate_two).astype(jnp.bfloat16)
    filter_spectra = forward_transform(long_filters.reshape(frames, 2 * channels))
    filter_one = filter_spectra[..., :channels]
    filter_two = filter_spectra[..., channels:]
    value_spectra = forward_transform(value)
    conv_one = inverse_transform(spectral_product(filter_one, value_spectra), False)
    first = (gate_one * conv_one.astype(jnp.float32)).astype(jnp.bfloat16)
    first_spectra = forward_transform(first)
    conv_two = inverse_transform(spectral_product(filter_two, first_spectra), False)
    two_spectra = forward_transform(grad_two)
    grad_first = inverse_transform(adjoint_product(filter_two, two_spectra), False)
    grad_one = (grad_first.astype(jnp.float32) * gate_one).astype(jnp.bfloat16)
    one_spectra = forward_transform(grad_one)
    grad_value = inverse_transform(adjoint_product(filter_one, one_spectra), False)
    middle = (grad_first.astype(jnp.float32) * conv_one.astype(jnp.float32)).astype(jnp.bfloat16)
    grad_pair_one = adjoint_product(value_spectra, one_spectra)
    grad_pair_two = adjoint_product(first_spectra, two_spectra)
    stacked = jnp.concatenate([grad_pair_one, grad_pair_two], axis=3)
    tap_rows = inverse_transform(stacked, True)
    grad_filters = (
        lax.psum_scatter(
            tap_rows.reshape(frames, 2, channels).astype(jnp.bfloat16),
            "dp",
            scatter_dimension=2,
            tiled=True,
        ).astype(jnp.float32)
        * grad_scale
    )
    layer_out = (gate_two * conv_two.astype(jnp.float32)).astype(jnp.bfloat16)
    grad_mixed = jnp.concatenate(
        [
            grad_value.astype(jnp.float32),
            middle.astype(jnp.float32),
            upstream * conv_two.astype(jnp.float32),
        ],
        axis=1,
    ).astype(jnp.bfloat16)
    after_rows = passed_along(grad_mixed[:margin_rows], "seq", -1)
    grad_mixed_f = grad_mixed.astype(jnp.float32)
    grad_pad = jnp.concatenate([grad_mixed, after_rows], axis=0).astype(jnp.float32)
    grad_rows = sum(
        (
            conv_taps[tap_index][None, :] * grad_pad[tap_index : tap_index + frames]
            for tap_index in range(tap_count)
        )
    ).astype(jnp.bfloat16)
    taps_terms = jnp.stack(
        [
            jnp.sum(
                extended[margin_rows - tap_index : margin_rows - tap_index + frames] * grad_mixed_f,
                axis=0,
            )
            for tap_index in range(tap_count)
        ]
    )
    grad_taps = lax.psum(taps_terms, ("dp", "seq")) * grad_scale
    grad_proj = (
        lax.psum_scatter(
            jnp.einsum("tc,tj->cj", signal, grad_rows, preferred_element_type=jnp.float32),
            ("dp", "seq"),
            scatter_dimension=0,
            tiled=True,
        )
        * grad_scale
    )
    grad_in = jnp.einsum(
        "tj,dj->td", grad_rows, proj_weight, preferred_element_type=jnp.float32
    ).astype(jnp.bfloat16)
    return (layer_out[None], grad_in[None], grad_proj, grad_taps, grad_filters)


def solution(mesh):
    placed = (P("dp", "seq", None), P(), P(), P("seq", None, None), P("dp", "seq", None))
    return jax.shard_map(
        shards,
        mesh=mesh,
        in_specs=placed,
        out_specs=(
            P("dp", "seq", None),
            P("dp", "seq", None),
            P(("dp", "seq"), None),
            P(),
            P("seq", None, "dp"),
        ),
        check_vma=False,
    )
```

profile of v0, /device:TPU:1, one launch (start us, length us, event | category | flops | bytes accessed | tf_op | source)
XLA Modules:
  0.0 740.7 jit_solution(4199064908352546538)
XLA Ops:
  18.1 8.8 %all-to-all-start.10 = ((bf16[32,8,512]{2,1,0:T(8,128)(2,1)}), bf16[32,8,512]{2,1,0:T(8,128)(2,1)S(1)}, u32[]{:S(2)}, u32[]{:S(2)}) async-start(bf16[32,8,512]{2,1,0:T(8,128)(2,1)} %fusion.108), calls=%async_computation.10 | async-start | bytes 524288 | tf_op jit(solution)/shard_map/all_to_all | solution.py:104
  69.1 7.5 %all-to-all-done.11 = bf16[2,64,8,512]{3,2,0,1:T(8,128)(2,1)S(1)} async-done(((bf16[2,64,8,512]{3,2,0,1:T(8,128)(2,1)}), bf16[2,64,8,512]{3,2,0,1:T(8,128)(2,1)S(1)}, u32[]{:S(2)}, u32[]{:S(2)}) %all-to-all-start.11) | async-done | bytes 1048608 | tf_op jit(solution)/shard_map/all_to_all | solution.py:121
  118.9 9.8 %convolution_bitcast_fusion.1 = f32[2,2,2,128,1024]{4,2,0,3,1:T(2,128)S(1)} fusion(bf16[2,2,2,128,1024,1]{4,3,2,1,0,5:T(8,128)(2,1)S(1)} %bitcast.559, f32[1,2,2,2]{1,2,3,0:T(2,128)S(1)} %copy.176, f32[1,2,2,2]{1,2,3,0:T(2,128)S(1)} %copy.175), kind=kOutput, calls=%fused_computation.11 | convolution fusion | flops 25165840 | bytes 6291520 | tf_op jit(solution)/shard_map/yzga,zkabw->ykgbw/dot_general | solution.py:44
  190.8 12.3 %all-to-all-start.12 = ((bf16[2,2,256,512]{3,1,0,2:T(2,128)(2,1)}), bf16[2,2,256,512]{3,1,0,2:T(2,128)(2,1)}, u32[]{:S(2)}, u32[]{:S(2)}) async-start(bf16[2,2,256,512]{3,1,0,2:T(2,128)(2,1)} %copy.221), calls=%async_computation.12 | async-start | bytes 2097152 | tf_op jit(solution)/shard_map/all_to_all | solution.py:140
  206.5 10.6 %all-to-all-done.12 = bf16[2,2,256,512]{3,1,0,2:T(2,128)(2,1)} async-done(((bf16[2,2,256,512]{3,1,0,2:T(2,128)(2,1)}), bf16[2,2,256,512]{3,1,0,2:T(2,128)(2,1)}, u32[]{:S(2)}, u32[]{:S(2)}) %all-to-all-start.12) | async-done | bytes 1048608 | tf_op jit(solution)/shard_map/all_to_all | solution.py:140
  217.1 7.1 all-to-all-start.4
  238.4 6.8 all-to-all-start.13
  253.5 15.8 %all_to_all.238 = bf16[32,8,512]{2,1,0:T(8,128)(2,1)S(1)} all-to-all(bf16[32,8,512]{2,1,0:T(8,128)(2,1)} %copy.194), channel_id=1, replica_groups=mesh['dp'=4,'seq'=32] {'seq'}, dimensions={0} | all-to-all | bytes 524288 | tf_op jit(solution)/shard_map/all_to_all | solution.py:151
  271.2 11.8 %all_to_all.239 = bf16[32,8,512]{2,1,0:T(8,128)(2,1)} all-to-all(bf16[32,8,512]{2,1,0:T(8,128)(2,1)S(1)} %get-tuple-element.114), channel_id=1, replica_groups=mesh['dp'=4,'seq'=32] {'seq'}, dimensions={0} | all-to-all | bytes 524288 | tf_op jit(solution)/shard_map/all_to_all | solution.py:104
  308.4 8.8 %all-to-all-done.15 = bf16[2,64,8,512]{3,2,0,1:T(8,128)(2,1)} async-done(((bf16[2,64,8,512]{3,2,0,1:T(8,128)(2,1)}), bf16[2,64,8,512]{3,2,0,1:T(8,128)(2,1)}, u32[]{:S(2)}, u32[]{:S(2)}) %all-to-all-start.15) | async-done | bytes 1048608 | tf_op jit(solution)/shard_map/all_to_all | solution.py:121
  349.8 7.3 multiply_add_fusion.3
  412.0 7.4 copy.241
  426.6 8.0 %all-to-all-start.8 = ((bf16[2,2,256,512]{3,1,0,2:T(2,128)(2,1)}), bf16[2,2,256,512]{3,1,0,2:T(2,128)(2,1)}, u32[]{:S(2)}, u32[]{:S(2)}) async-start(bf16[2,2,256,512]{3,1,0,2:T(2,128)(2,1)} %copy.206), calls=%async_computation.8 | async-start | bytes 2097152 | tf_op jit(solution)/shard_map/all_to_all | solution.py:140
  434.7 11.4 %fusion = f32[2,2,2,128,1024]{4,2,0,3,1:T(2,128)S(1)} fusion(f32[1,2,2,128,1024]{4,2,0,3,1:T(2,128)} %get-tuple-element.40, f32[1,2,2,128,1024]{4,2,0,3,1:T(2,128)} %get-tuple-element.39, f32[1,2,2,2]{3,2,1,0:T(2,128)S(1)} %get-tuple-element.145, f32[1,2,2,2]{3,2,1,0:T(2,128)S(1)} %get-tuple-element.140), kind=kOutput, calls=%fused_computation.4 | convolution fusion | flops 27262992 | bytes 8388672 | tf_op jit(solution)/shard_map/yzag,zkgbw->ykabw/dot_general | solution.py:44
  462.8 7.8 %all-to-all-start.9 = ((bf16[32,8,512]{2,1,0:T(8,128)(2,1)}), bf16[32,8,512]{2,1,0:T(8,128)(2,1)S(1)}, u32[]{:S(2)}, u32[]{:S(2)}) async-start(bf16[32,8,512]{2,1,0:T(8,128)(2,1)} %copy.209), calls=%async_computation.9 | async-start | bytes 524288 | tf_op jit(solution)/shard_map/all_to_all | solution.py:151
  490.9 7.0 all-to-all-start.18
  499.4 9.0 %collective-permute-done.1 = bf16[2,1536]{1,0:T(2,128)(2,1)S(1)} collective-permute-done((bf16[2,1536]{1,0:T(2,128)(2,1)S(1)}, bf16[2,1536]{1,0:T(2,128)(2,1)S(1)}, u32[]{:S(2)}, u32[]{:S(2)}) %collective-permute-start.1) | collective-permute-done | bytes 6176 | tf_op jit(solution)/shard_map/ppermute | solution.py:15
  528.6 10.8 %all-to-all-start.19 = ((bf16[32,8,1024]{2,1,0:T(8,128)(2,1)}), bf16[32,8,1024]{2,1,0:T(8,128)(2,1)}, u32[]{:S(2)}, u32[]{:S(2)}) async-start(bf16[32,8,1024]{2,1,0:T(8,128)(2,1)} %copy.247), calls=%async_computation.19 | async-start | bytes 1048576 | tf_op jit(solution)/shard_map/all_to_all | solution.py:147
  541.1 8.1 %all-to-all-done.19 = bf16[32,8,1024]{2,1,0:T(8,128)(2,1)} async-done(((bf16[32,8,1024]{2,1,0:T(8,128)(2,1)}), bf16[32,8,1024]{2,1,0:T(8,128)(2,1)}, u32[]{:S(2)}, u32[]{:S(2)}) %all-to-all-start.19) | async-done | bytes 524320 | tf_op jit(solution)/shard_map/all_to_all | solution.py:147
  550.7 25.2 %copy.328 = bf16[256,2,512]{1,0,2:T(8,128)(2,1)} copy(bf16[256,2,512]{2,1,0:T(2,128)(2,1)S(1)} %all_to_all.217) | data formatting | bytes 1048576
  575.9 49.6 %reshape.827 = bf16[512,512]{1,0:T(8,128)(2,1)} reshape(bf16[512,256,2]{2,1,0:T(8,128)(2,1)} %bitcast.520) | data formatting | bytes 1048576
  625.6 74.0 %psum.7 = f32[3,1536]{1,0:T(4,128)S(1)} all-reduce(f32[3,1536]{1,0:T(4,128)S(1)} %pad_maximum_fusion.15), channel_id=1, replica_groups=mesh['dp'=4,'seq'=32] {'dp','seq'}, use_global_device_ids=true, to_apply=%region_4.5 | all-reduce | flops 4608 | bytes 36864 | tf_op jit(solution)/shard_map/psum | solution.py:236
  703.7 19.9 %reshape.828 = bf16[128,256,2]{2,1,0:T(8,128)(2,1)} reshape(bf16[128,512]{1,0:T(8,128)(2,1)} %reduce-scatter.5.cloned.1.call-done) | data formatting | bytes 262144
  723.6 8.4 %copy.329 = bf16[256,2,128]{2,1,0:T(2,128)(2,1)S(1)} copy(bf16[256,2,128]{1,0,2:T(8,128)(2,1)} %bitcast.524) | data formatting | bytes 262144
  (271 shorter events, 370.3 us)
Async XLA Ops:
  11.0 4.8 collective-permute-start
  17.2 23.8 %copy-start.14 = (bf16[256,1536]{1,0:T(8,128)(2,1)}, bf16[256,1536]{1,0:T(8,128)(2,1)S(1)}, u32[]{:S(2)}) copy-start(bf16[256,1536]{1,0:T(8,128)(2,1)S(1)} %add_convert_fusion.1) | copy-start | bytes 2359300
  18.1 16.9 %all-to-all-start.10 = ((bf16[32,8,512]{2,1,0:T(8,128)(2,1)}), bf16[32,8,512]{2,1,0:T(8,128)(2,1)S(1)}, u32[]{:S(2)}, u32[]{:S(2)}) async-start(bf16[32,8,512]{2,1,0:T(8,128)(2,1)} %fusion.108), calls=%async_computation.10 | async-start | bytes 524288 | tf_op jit(solution)/shard_map/all_to_all | solution.py:104
  35.0 12.1 %all-to-all-start.2 = ((bf16[32,8,512]{2,1,0:T(8,128)(2,1)}), bf16[32,8,512]{2,1,0:T(8,128)(2,1)S(1)}, u32[]{:S(2)}, u32[]{:S(2)}) async-start(bf16[32,8,512]{2,1,0:T(8,128)(2,1)} %slice_bitcast_fusion), calls=%async_computation.2 | async-start | bytes 524288 | tf_op jit(solution)/shard_map/all_to_all | solution.py:104
  47.1 13.1 %all-to-all-start = ((bf16[32,8,1024]{2,1,0:T(8,128)(2,1)}), bf16[32,8,1024]{2,1,0:T(8,128)(2,1)S(1)}, u32[]{:S(2)}, u32[]{:S(2)}) async-start(bf16[32,8,1024]{2,1,0:T(8,128)(2,1)} %reshape_reshape.4), calls=%async_computation | async-start | bytes 1048576 | tf_op jit(solution)/shard_map/all_to_all | solution.py:104
  61.0 15.6 %all-to-all-start.11 = ((bf16[2,64,8,512]{3,2,0,1:T(8,128)(2,1)}), bf16[2,64,8,512]{3,2,0,1:T(8,128)(2,1)S(1)}, u32[]{:S(2)}, u32[]{:S(2)}) async-start(bf16[2,64,8,512]{3,2,0,1:T(8,128)(2,1)} %copy.211), calls=%async_computation.11 | async-start | bytes 2097152 | tf_op jit(solution)/shard_map/all_to_all | solution.py:121
  76.6 16.4 %all-to-all-start.3 = ((bf16[2,64,8,512]{3,2,0,1:T(8,128)(2,1)}), bf16[2,64,8,512]{3,2,0,1:T(8,128)(2,1)}, u32[]{:S(2)}, u32[]{:S(2)}) async-start(bf16[2,64,8,512]{3,2,0,1:T(8,128)(2,1)} %copy.181), calls=%async_computation.3 | async-start | bytes 2097152 | tf_op jit(solution)/shard_map/all_to_all | solution.py:121
  93.0 24.0 %all-to-all-start.1 = ((bf16[2,64,8,1024]{3,2,0,1:T(8,128)(2,1)}), bf16[2,64,8,1024]{3,2,0,1:T(8,128)(2,1)}, u32[]{:S(2)}, u32[]{:S(2)}) async-start(bf16[2,64,8,1024]{3,2,0,1:T(8,128)(2,1)} %copy.172), calls=%async_computation.1 | async-start | bytes 4194304 | tf_op jit(solution)/shard_map/all_to_all | solution.py:121
  190.8 26.2 %all-to-all-start.12 = ((bf16[2,2,256,512]{3,1,0,2:T(2,128)(2,1)}), bf16[2,2,256,512]{3,1,0,2:T(2,128)(2,1)}, u32[]{:S(2)}, u32[]{:S(2)}) async-start(bf16[2,2,256,512]{3,1,0,2:T(2,128)(2,1)} %copy.221), calls=%async_computation.12 | async-start | bytes 2097152 | tf_op jit(solution)/shard_map/all_to_all | solution.py:140
  217.1 21.3 %all-to-all-start.4 = ((bf16[2,2,256,512]{3,1,0,2:T(2,128)(2,1)}), bf16[2,2,256,512]{3,1,0,2:T(2,128)(2,1)}, u32[]{:S(2)}, u32[]{:S(2)}) async-start(bf16[2,2,256,512]{3,1,0,2:T(2,128)(2,1)} %copy.191), calls=%async_computation.4 | async-start | bytes 2097152 | tf_op jit(solution)/shard_map/all_to_all | solution.py:140
  238.4 15.1 %all-to-all-start.13 = ((bf16[32,8,512]{2,1,0:T(8,128)(2,1)}), bf16[32,8,512]{2,1,0:T(8,128)(2,1)}, u32[]{:S(2)}, u32[]{:S(2)}) async-start(bf16[32,8,512]{2,1,0:T(8,128)(2,1)} %copy.224), calls=%async_computation.13 | async-start | bytes 524288 | tf_op jit(solution)/shard_map/all_to_all | solution.py:151
  283.1 12.7 %all-to-all-start.14 = ((bf16[32,8,512]{2,1,0:T(8,128)(2,1)}), bf16[32,8,512]{2,1,0:T(8,128)(2,1)}, u32[]{:S(2)}, u32[]{:S(2)}) async-start(bf16[32,8,512]{2,1,0:T(8,128)(2,1)} %get-tuple-element.113), calls=%async_computation.14 | async-start | bytes 524288 | tf_op jit(solution)/shard_map/all_to_all | solution.py:104
  300.8 16.5 %all-to-all-start.15 = ((bf16[2,64,8,512]{3,2,0,1:T(8,128)(2,1)}), bf16[2,64,8,512]{3,2,0,1:T(8,128)(2,1)}, u32[]{:S(2)}, u32[]{:S(2)}) async-start(bf16[2,64,8,512]{3,2,0,1:T(8,128)(2,1)} %copy.226), calls=%async_computation.15 | async-start | bytes 2097152 | tf_op jit(solution)/shard_map/all_to_all | solution.py:121
  317.3 16.2 %all-to-all-start.7 = ((bf16[2,64,8,512]{3,2,0,1:T(8,128)(2,1)}), bf16[2,64,8,512]{3,2,0,1:T(8,128)(2,1)}, u32[]{:S(2)}, u32[]{:S(2)}) async-start(bf16[2,64,8,512]{3,2,0,1:T(8,128)(2,1)} %copy.196), calls=%async_computation.7 | async-start | bytes 2097152 | tf_op jit(solution)/shard_map/all_to_all | solution.py:121
  400.3 26.3 %all-to-all-start.16 = ((bf16[2,2,256,512]{3,1,0,2:T(2,128)(2,1)}), bf16[2,2,256,512]{3,1,0,2:T(2,128)(2,1)S(1)}, u32[]{:S(2)}, u32[]{:S(2)}) async-start(bf16[2,2,256,512]{3,1,0,2:T(2,128)(2,1)} %copy.236), calls=%async_computation.16 | async-start | bytes 2097152 | tf_op jit(solution)/shard_map/all_to_all | solution.py:140
  426.6 28.0 %all-to-all-start.8 = ((bf16[2,2,256,512]{3,1,0,2:T(2,128)(2,1)}), bf16[2,2,256,512]{3,1,0,2:T(2,128)(2,1)}, u32[]{:S(2)}, u32[]{:S(2)}) async-start(bf16[2,2,256,512]{3,1,0,2:T(2,128)(2,1)} %copy.206), calls=%async_computation.8 | async-start | bytes 2097152 | tf_op jit(solution)/shard_map/all_to_all | solution.py:140
  462.8 15.9 %all-to-all-start.9 = ((bf16[32,8,512]{2,1,0:T(8,128)(2,1)}), bf16[32,8,512]{2,1,0:T(8,128)(2,1)S(1)}, u32[]{:S(2)}, u32[]{:S(2)}) async-start(bf16[32,8,512]{2,1,0:T(8,128)(2,1)} %copy.209), calls=%async_computation.9 | async-start | bytes 524288 | tf_op jit(solution)/shard_map/all_to_all | solution.py:151
  478.8 12.2 %all-to-all-start.17 = ((bf16[32,8,512]{2,1,0:T(8,128)(2,1)}), bf16[32,8,512]{2,1,0:T(8,128)(2,1)S(1)}, u32[]{:S(2)}, u32[]{:S(2)}) async-start(bf16[32,8,512]{2,1,0:T(8,128)(2,1)} %copy.239), calls=%async_computation.17 | async-start | bytes 524288 | tf_op jit(solution)/shard_map/all_to_all | solution.py:151
  490.9 24.3 %all-to-all-start.18 = ((bf16[2,2,256,1024]{3,1,0,2:T(2,128)(2,1)}), bf16[2,2,256,1024]{3,1,0,2:T(2,128)(2,1)}, u32[]{:S(2)}, u32[]{:S(2)}) async-start(bf16[2,2,256,1024]{3,1,0,2:T(2,128)(2,1)} %copy.244), calls=%async_computation.18 | async-start | bytes 4194304 | tf_op jit(solution)/shard_map/all_to_all | solution.py:136
  498.0 203.4 %all-reduce.3.cloned.1.call-start = ((), (), s32[]{:S(2)}) async-start(), calls=%async_computation.22 | async-start | bytes 6291456
  498.1 10.3 %collective-permute-start.1 = (bf16[2,1536]{1,0:T(2,128)(2,1)S(1)}, bf16[2,1536]{1,0:T(2,128)(2,1)S(1)}, u32[]{:S(2)}, u32[]{:S(2)}) collective-permute-start(bf16[2,1536]{1,0:T(2,128)(2,1)S(1)} %slice.455), channel_id=1, source_target_pairs={{1,0},{2,1},{3,2},{4,3},{5,4},{6,5},{7,6},{8,7},{9,8},{10,9},{11,1... | collective-permute-start | bytes 18440 | tf_op jit(solution)/shard_map/ppermute | solution.py:15
  528.6 20.6 %all-to-all-start.19 = ((bf16[32,8,1024]{2,1,0:T(8,128)(2,1)}), bf16[32,8,1024]{2,1,0:T(8,128)(2,1)}, u32[]{:S(2)}, u32[]{:S(2)}) async-start(bf16[32,8,1024]{2,1,0:T(8,128)(2,1)} %copy.247), calls=%async_computation.19 | async-start | bytes 1048576 | tf_op jit(solution)/shard_map/all_to_all | solution.py:147
  539.4 164.3 %reduce-scatter.5.cloned.1.call-start = ((), (), s32[]{:S(2)}) async-start(), calls=%async_computation.21 | async-start | bytes 655360
  575.9 124.3 %copy-start.20 = (bf16[256,1536]{1,0:T(8,128)(2,1)S(1)}, bf16[256,1536]{1,0:T(8,128)(2,1)}, u32[]{:S(2)}) copy-start(bf16[256,1536]{1,0:T(8,128)(2,1)} %copy-done.19) | copy-start | bytes 2359300
  (34 other events, 154.6 us)
Sparse Core Ops, SparseCore 0:
  512.4 172.1 all-reduce.2
Sparse Core Ops, SparseCore 1:
  625.6 37.0 reduce-scatter.4
where the time goes:
time: 751 us; the launch traced here: 741 us
  local copies, waits for them, and re-layouts  235 us (31%)
  starting transfers between devices  117 us (16%)
  matrix products  109 us (15%)
  blocking collectives  102 us (14%)
  waiting for transfers between devices  94.8 us (13%)
  other arithmetic  66.1 us (9%)
  between operations  17.1 us (2%)
    unnamed x77, local copies, waits for them, and re-layouts  113 us
    dot_general x20, matrix products, dft_pair(): jnp.einsum('yz' + table_part + ',z' + data_part + '->y' + result_side, bl...  85.7 us
    psum x1, blocking collectives, shards(): grad_taps = lax.psum(taps_terms, ('dp', 'seq')) * grad_scale  74 us
    all_to_all x5, starting transfers between devices, inverse_transform(): lax.all_to_all(stacked.astype(jnp.bfloat16), 'seq', split_axis=2, concat_...  38.4 us
    all_to_all x15, local copies, waits for them, and re-layouts, inverse_transform(): lax.all_to_all(stacked.astype(jnp.bfloat16), 'seq', split_axis=2, concat_...  30.8 us
    all_to_all x4, starting transfers between devices, inverse_transform(): lax.all_to_all(values.astype(jnp.bfloat16), 'seq', split_axis=0, concat_a...  29.5 us
    all_to_all x5, waiting for transfers between devices, forward_transform(): lax.all_to_all(stacked, 'seq', split_axis=1, concat_axis=2, tiled=True)  28.6 us
    dot_general x5, local copies, waits for them, and re-layouts, dft_pair(): jnp.einsum('yz' + table_part + ',z' + data_part + '->y' + result_side, bl...  24.1 us
  transfers between devices with their start and end apart: 22, of which 17 were waited for; matrix products, arithmetic and copies ran while one was open for 28% of the time, Pallas kernels for 0%

commit v1 on v0

--- a/solution.py
+++ b/solution.py
@@ -179,33 +179,52 @@
     gate_two = mixed[:, 2 * channels :].astype(jnp.float32)
     upstream = out_grad[0].astype(jnp.float32)
     grad_two = (upstream * gate_two).astype(jnp.bfloat16)
-    filter_spectra = forward_transform(long_filters.reshape(frames, 2 * channels))
-    filter_one = filter_spectra[..., :channels]
-    filter_two = filter_spectra[..., channels:]
-    value_spectra = forward_transform(value)
-    conv_one = inverse_transform(spectral_product(filter_one, value_spectra), False)
+    opening = forward_transform(
+        jnp.concatenate([long_filters.reshape(frames, 2 * channels), value, grad_two], axis=1)
+    )
+    filter_one = opening[..., :channels]
+    filter_two = opening[..., channels : 2 * channels]
+    value_spectra = opening[..., 2 * channels : 3 * channels]
+    two_spectra = opening[..., 3 * channels :]
+    middle_rows = inverse_transform(
+        jnp.concatenate(
+            [
+                spectral_product(filter_one, value_spectra),
+                adjoint_product(filter_two, two_spectra),
+            ],
+            axis=3,
+        ),
+        False,
+    )
+    conv_one = middle_rows[:, :channels]
+    grad_first = middle_rows[:, channels:]
     first = (gate_one * conv_one.astype(jnp.float32)).astype(jnp.bfloat16)
-    first_spectra = forward_transform(first)
-    conv_two = inverse_transform(spectral_product(filter_two, first_spectra), False)
-    two_spectra = forward_transform(grad_two)
-    grad_first = inverse_transform(adjoint_product(filter_two, two_spectra), False)
     grad_one = (grad_first.astype(jnp.float32) * gate_one).astype(jnp.bfloat16)
-    one_spectra = forward_transform(grad_one)
-    grad_value = inverse_transform(adjoint_product(filter_one, one_spectra), False)
+    second = forward_transform(jnp.concatenate([first, grad_one], axis=1))
+    first_spectra = second[..., :channels]
+    one_spectra = second[..., channels:]
+    closing = inverse_transform(
+        jnp.concatenate(
+            [
+                spectral_product(filter_two, first_spectra),
+                adjoint_product(filter_one, one_spectra),
+                adjoint_product(value_spectra, one_spectra),
+                adjoint_product(first_spectra, two_spectra),
+            ],
+            axis=3,
+        ),
+        False,
+    )
+    conv_two = closing[:, :channels]
+    grad_value = closing[:, channels : 2 * channels]
+    tap_rows = closing[:, 2 * channels :]
+    block = channels // data_devices
+    tap_blocks = tap_rows.reshape(frames, 2, data_devices, block).transpose(2, 1, 0, 3)
+    tap_parts = lax.all_to_all(tap_blocks, "dp", split_axis=0, concat_axis=0, tiled=True)
+    grad_filters = (
+        jnp.sum(tap_parts.astype(jnp.float32), axis=0).transpose(1, 0, 2) * grad_scale
+    )
     middle = (grad_first.astype(jnp.float32) * conv_one.astype(jnp.float32)).astype(jnp.bfloat16)
-    grad_pair_one = adjoint_product(value_spectra, one_spectra)
-    grad_pair_two = adjoint_product(first_spectra, two_spectra)
-    stacked = jnp.concatenate([grad_pair_one, grad_pair_two], axis=3)
-    tap_rows = inverse_transform(stacked, True)
-    grad_filters = (
-        lax.psum_scatter(
-            tap_rows.reshape(frames, 2, channels).astype(jnp.bfloat16),
-            "dp",
-            scatter_dimension=2,
-            tiled=True,
-        ).astype(jnp.float32)
-        * grad_scale
-    )
     layer_out = (gate_two * conv_two.astype(jnp.float32)).astype(jnp.bfloat16)
     grad_mixed = jnp.concatenate(
         [
@@ -234,15 +253,16 @@
         ]
     )
     grad_taps = lax.psum(taps_terms, ("dp", "seq")) * grad_scale
-    grad_proj = (
-        lax.psum_scatter(
-            jnp.einsum("tc,tj->cj", signal, grad_rows, preferred_element_type=jnp.float32),
-            ("dp", "seq"),
-            scatter_dimension=0,
-            tiled=True,
-        )
-        * grad_scale
-    )
+    proj_terms = jnp.einsum("tc,tj->cj", signal, grad_rows, preferred_element_type=jnp.float32)
+    all_devices = data_devices * seq_devices
+    proj_parts = lax.all_to_all(
+        proj_terms.reshape(all_devices, proj_terms.shape[0] // all_devices, proj_terms.shape[1]),
+        ("dp", "seq"),
+        split_axis=0,
+        concat_axis=0,
+        tiled=True,
+    )
+    grad_proj = jnp.sum(proj_parts, axis=0) * grad_scale
     grad_in = jnp.einsum(
         "tj,dj->td", grad_rows, proj_weight, preferred_element_type=jnp.float32
     ).astype(jnp.bfloat16)

time: 751 us -> 639 us (0.85)
  local copies, waits for them, and re-layouts: 235 us -> 114 us
  blocking collectives: 102 us -> 201 us
  starting transfers between devices: 117 us -> 50.8 us
  waiting for transfers between devices: 94.8 us -> 117 us
  other arithmetic: 66.1 us -> 47.7 us
  between operations: 17.1 us -> 1.62 us
  matrix products: 109 us -> 96.3 us
    unnamed x77 -> x42, local copies, waits for them, and re-layouts: 113 us -> 7.09 us
    all_to_all x0 -> x1, blocking collectives: none -> 56.3 us  [inverse_transform(): lax.all_to_all(stacked.astype(jnp.bfloat16), 'seq', split_axis=2, concat_...]
    all_to_all x5 -> x2, waiting for transfers between devices: 28.6 us -> 79 us  [forward_transform(): lax.all_to_all(stacked, 'seq', split_axis=1, concat_axis=2, tiled=True)]
    all_to_all x5 -> x1, starting transfers between devices: 38.4 us -> 7.7 us  [inverse_transform(): lax.all_to_all(stacked.astype(jnp.bfloat16), 'seq', split_axis=2, concat_...]
    all_to_all x1 -> x2, blocking collectives: 15.8 us -> 38.7 us  [inverse_transform(): lax.all_to_all(values.astype(jnp.bfloat16), 'seq', split_axis=0, concat_a...]
    another operation x9 -> x0, local copies, waits for them, and re-layouts: 19.2 us -> none  [the longest x4 9.02 us: spectral_product(): jnp.stack([left_side[0] * right_side[0] - left_side[1] * right_side[1], l...]
    psum x1, blocking collectives: 74 us -> 91.3 us  [shards(): grad_taps = lax.psum(taps_terms, ('dp', 'seq')) * grad_scale]
    all_to_all x4 -> x2, waiting for transfers between devices: 16 us -> 0.66 us  [the longest x1 0.66 us: shards(): lax.all_to_all(tap_blocks, 'dp', split_axis=0, concat_axis=0, tiled=True)]
  transfers between devices with their start and end apart: 22 -> 8, of which waited for: 17 -> 5; matrix products, arithmetic and copies ran while one was open for 28% -> 3% of each run, Pallas kernels for 0% -> 0%
where the time goes in v1:
time: 639 us; the launch traced here: 629 us
  blocking collectives  201 us (31%)
  waiting for transfers between devices  117 us (18%)
  local copies, waits for them, and re-layouts  114 us (18%)
  matrix products  96.3 us (15%)
  starting transfers between devices  50.8 us (8%)
  other arithmetic  47.7 us (7%)
    psum x1, blocking collectives, shards(): grad_taps = lax.psum(taps_terms, ('dp', 'seq')) * grad_scale  91.3 us
    all_to_all x2, waiting for transfers between devices, forward_transform(): lax.all_to_all(stacked, 'seq', split_axis=1, concat_axis=2, tiled=True)  79 us
    dot_general x8, matrix products, dft_pair(): jnp.einsum('yz' + table_part + ',z' + data_part + '->y' + result_side, bl...  78.6 us
    all_to_all x1, blocking collectives, inverse_transform(): lax.all_to_all(stacked.astype(jnp.bfloat16), 'seq', split_axis=2, concat_...  56.3 us
    all_to_all x2, blocking collectives, inverse_transform(): lax.all_to_all(values.astype(jnp.bfloat16), 'seq', split_axis=0, concat_a...  38.7 us
    all_to_all x6, local copies, waits for them, and re-layouts, inverse_transform(): lax.all_to_all(stacked.astype(jnp.bfloat16), 'seq', split_axis=2, concat_...  25.7 us
    another operation x5, local copies, waits for them, and re-layouts, rotate_stacked(): jnp.stack([stacked[0] * cosine_table - direction * stacked[1] * sine_tabl...  24.5 us
    all_to_all x1, waiting for transfers between devices, inverse_transform(): lax.all_to_all(stacked.astype(jnp.bfloat16), 'seq', split_axis=2, concat_...  23.7 us
  transfers between devices with their start and end apart: 8, of which 5 were waited for; matrix products, arithmetic and copies ran while one was open for 3% of the time, Pallas kernels for 0%

profile of v1, /device:TPU:1, one launch (start us, length us, event | category | flops | bytes accessed | tf_op | source)
XLA Modules:
  0.0 629.4 jit_solution(16466730857301243935)
XLA Ops:
  13.9 8.2 %all-to-all-start = ((bf16[32,8,2048]{2,1,0:T(8,128)(2,1)}), bf16[32,8,2048]{2,1,0:T(8,128)(2,1)}, u32[]{:S(2)}, u32[]{:S(2)}) async-start(bf16[32,8,2048]{2,1,0:T(8,128)(2,1)} %pad_maximum_fusion.4), calls=%async_computation | async-start | bytes 2097152 | tf_op jit(solution)/shard_map/all_to_all | solution.py:104
  22.4 14.0 %all-to-all-done = bf16[32,8,2048]{2,1,0:T(8,128)(2,1)} async-done(((bf16[32,8,2048]{2,1,0:T(8,128)(2,1)}), bf16[32,8,2048]{2,1,0:T(8,128)(2,1)}, u32[]{:S(2)}, u32[]{:S(2)}) %all-to-all-start) | async-done | bytes 1048608 | tf_op jit(solution)/shard_map/all_to_all | solution.py:104
  55.4 55.2 %all-to-all-done.1 = bf16[2,64,8,2048]{3,2,0,1:T(8,128)(2,1)} async-done(((bf16[2,64,8,2048]{3,2,0,1:T(8,128)(2,1)}), bf16[2,64,8,2048]{3,2,0,1:T(8,128)(2,1)}, u32[]{:S(2)}, u32[]{:S(2)}) %all-to-all-start.1) | async-done | bytes 4194336 | tf_op jit(solution)/shard_map/all_to_all | solution.py:121
  113.3 13.5 %convolution_bitcast_fusion = f32[2,2,2,128,2048]{4,2,0,3,1:T(2,128)S(1)} fusion(bf16[2,2,2,128,2048,1]{4,3,2,1,0,5:T(8,128)(2,1)S(1)} %bitcast.252, f32[1,2,2,2]{1,2,3,0:T(2,128)S(1)} %copy.142, f32[1,2,2,2]{1,2,3,0:T(2,128)S(1)} %copy.141), kind=kOutput, calls=%fused_computation.10 | convolution fusion | flops 50331664 | bytes 12582976 | tf_op jit(solution)/shard_map/yzga,zkabw->ykgbw/dot_general | solution.py:44
  137.3 11.2 %fusion.6 = f32[2,2,2,128,2048]{4,3,0,2,1:T(8,128)S(1)} fusion(f32[2,2,2,128,2048,1]{4,2,0,3,1,5:T(2,128)S(1)} %maximum_bitcast_fusion, f32[1,2,128,128]{3,2,1,0:T(8,128)S(1)} %get-tuple-element.49, f32[1,2,128,128]{3,2,1,0:T(8,128)S(1)} %get-tuple-element.52), kind=kOutput, calls=%fused_computation.11 | convolution fusion | flops 3221291008 | bytes 17039360 | tf_op jit(solution)/shard_map/yzfb,zkgbw->ykgfw/dot_general | solution.py:44
  159.9 7.3 %copy.187 = f32[2,2,2,128,1024,1]{4,0,2,5,3,1:T(2,128)} copy(f32[2,2,2,128,1024,1]{3,4,0,2,1,5:T(8,128)} %maximum_bitcast_fusion.5) | data formatting | bytes 8388608 | tf_op jit(solution)/shard_map/stack | solution.py:29
  167.3 11.6 %fusion.19 = f32[2,2,2,128,1024]{4,2,0,3,1:T(2,128)S(1)} fusion(f32[2,2,2,128,1024,1]{4,0,2,5,3,1:T(2,128)} %copy.187, f32[1,2,2,2]{1,2,3,0:T(2,128)S(1)} %copy.150, f32[1,2,2,2]{1,2,3,0:T(2,128)S(1)} %copy.149), kind=kOutput, calls=%fused_computation.30 | convolution fusion | flops 26214416 | bytes 8388672 | tf_op jit(solution)/shard_map/yzag,zkgbw->ykabw/dot_general | solution.py:44
  186.0 7.7 %all-to-all-start.2 = ((bf16[2,2,256,1024]{3,1,0,2:T(2,128)(2,1)}), bf16[2,2,256,1024]{3,1,0,2:T(2,128)(2,1)}, u32[]{:S(2)}, u32[]{:S(2)}) async-start(bf16[2,2,256,1024]{3,1,0,2:T(2,128)(2,1)} %copy.154), calls=%async_computation.2 | async-start | bytes 4194304 | tf_op jit(solution)/shard_map/all_to_all | solution.py:140
  193.8 23.7 %all-to-all-done.2 = bf16[2,2,256,1024]{3,1,0,2:T(2,128)(2,1)} async-done(((bf16[2,2,256,1024]{3,1,0,2:T(2,128)(2,1)}), bf16[2,2,256,1024]{3,1,0,2:T(2,128)(2,1)}, u32[]{:S(2)}, u32[]{:S(2)}) %all-to-all-start.2) | async-done | bytes 2097184 | tf_op jit(solution)/shard_map/all_to_all | solution.py:140
  230.1 18.2 %all_to_all.104 = bf16[32,8,1024]{2,1,0:T(8,128)(2,1)S(1)} all-to-all(bf16[32,8,1024]{2,1,0:T(8,128)(2,1)S(1)} %copy.157), channel_id=1, replica_groups=mesh['dp'=4,'seq'=32] {'seq'}, dimensions={0} | all-to-all | bytes 1048576 | tf_op jit(solution)/shard_map/all_to_all | solution.py:151
  249.2 14.8 %all_to_all.105 = bf16[32,8,1024]{2,1,0:T(8,128)(2,1)S(1)} all-to-all(bf16[32,8,1024]{2,1,0:T(8,128)(2,1)S(1)} %maximum_bitcast_fusion.10), channel_id=1, replica_groups=mesh['dp'=4,'seq'=32] {'seq'}, dimensions={0} | all-to-all | bytes 1048576 | tf_op jit(solution)/shard_map/all_to_all | solution.py:104
  274.8 23.8 %all-to-all-done.5 = bf16[2,64,8,1024]{3,2,0,1:T(8,128)(2,1)} async-done(((bf16[2,64,8,1024]{3,2,0,1:T(8,128)(2,1)}), bf16[2,64,8,1024]{3,2,0,1:T(8,128)(2,1)}, u32[]{:S(2)}, u32[]{:S(2)}) %all-to-all-start.5) | async-done | bytes 2097184 | tf_op jit(solution)/shard_map/all_to_all | solution.py:121
  307.4 7.2 %copy.163 = f32[2,128,1024,2,2]{1,2,3,4,0:T(8,128)} copy(f32[2,128,1024,2,2]{2,4,3,1,0:T(2,128)} %convolution_bitcast_fusion.2) | data formatting | bytes 8388608 | tf_op jit(solution)/shard_map/yzga,zkabw->ykgbw/dot_general | solution.py:44
  324.4 9.0 %fusion.9 = f32[2,2,2048,2,128]{4,2,3,1,0:T(8,128)} fusion(f32[2,2,2,128,2048,1]{4,3,2,1,0,5:T(8,128)S(1)} %bitcast.244, f32[1,2,128,128]{3,2,1,0:T(8,128)S(1)} %get-tuple-element.53, f32[1,2,128,128]{3,2,1,0:T(8,128)S(1)} %get-tuple-element.48), kind=kOutput, calls=%fused_computation.12 | convolution fusion | flops 3221291008 | bytes 17039360 | tf_op jit(solution)/shard_map/yzbf,zkgfw->ykgbw/dot_general | solution.py:44
  333.3 13.3 %copy.167 = f32[2,2,2048,2,128]{2,1,3,4,0:T(2,128)} copy(f32[2,2,2048,2,128]{4,2,3,1,0:T(8,128)} %fusion.9) | data formatting | bytes 16777216 | tf_op jit(solution)/shard_map/yzbf,zkgfw->ykgbw/dot_general | solution.py:44
  346.6 7.2 %multiply_subtract_fusion = (f32[1,2,2,128,2048]{4,2,0,3,1:T(2,128)S(1)}, f32[1,2,2,128,2048]{4,2,0,3,1:T(2,128)S(1)}) fusion(f32[2,2,2,128,2048]{4,2,0,3,1:T(2,128)} %bitcast.245, f32[2,128]{0,1:T(8,128)S(1)} %copy.168, f32[2,128]{0,1:T(8,128)S(1)} %copy.144), kind=kLoop, calls=%fused_computation.35 | loop fusion | flops 6291456 | bytes 16779264 | tf_op jit(solution)/shard_map/sub | solution.py:31
  353.8 20.8 %fusion = f32[2,2,2,128,2048]{4,2,0,3,1:T(2,128)} fusion(f32[2,2,2,2,1,1]{3,2,1,0,5,4:T(2,128)S(1)} %copy.198, f32[1,2,2,128,2048]{4,2,0,3,1:T(2,128)S(1)} %get-tuple-element.20, f32[1,2,2,128,2048]{4,2,0,3,1:T(2,128)S(1)} %get-tuple-element.19), kind=kOutput, calls=%fused_computation.4 | convolution fusion | flops 54525952 | bytes 16777280 | tf_op jit(solution)/shard_map/yzag,zkgbw->ykabw/dot_general | solution.py:44
  374.7 9.5 %fusion.122 = (f32[1,2,2,128,2048]{4,2,0,3,1:T(2,128)}, f32[1,2,2,128,2048]{4,2,0,3,1:T(2,128)S(1)}) fusion(f32[2,2,2,128,2048]{4,2,0,3,1:T(2,128)} %fusion), kind=kLoop, calls=%fused_computation.240 | loop fusion | bytes 16777216 | tf_op jit(solution)/shard_map/slice | solution.py:31
  400.5 56.3 %all_to_all.106 = bf16[2,2,256,2048]{3,1,0,2:T(2,128)(2,1)S(1)} all-to-all(bf16[2,2,256,2048]{3,1,0,2:T(2,128)(2,1)} %copy.172), channel_id=1, replica_groups=mesh['dp'=4,'seq'=32] {'seq'}, dimensions={2} | all-to-all | bytes 8388608 | tf_op jit(solution)/shard_map/all_to_all | solution.py:140
  465.4 7.2 %all_to_all.90 = bf16[2,64,8,2048]{3,1,0,2:T(8,128)(2,1)} reshape(bf16[2,32,2,8,2048]{4,2,1,0,3:T(2,128)(2,1)} %copy.174) | data formatting | bytes 8388608 | tf_op jit(solution)/shard_map/all_to_all | solution.py:140
  476.7 20.5 %all_to_all.107 = bf16[32,8,2048]{2,1,0:T(8,128)(2,1)S(1)} all-to-all(bf16[32,8,2048]{2,1,0:T(8,128)(2,1)S(1)} %copy.175), channel_id=1, replica_groups=mesh['dp'=4,'seq'=32] {'seq'}, dimensions={0} | all-to-all | bytes 2097152 | tf_op jit(solution)/shard_map/all_to_all | solution.py:151
  501.3 8.4 %all-to-all-start.9 = ((bf16[4,2,256,128]{3,1,2,0:T(2,128)(2,1)}), bf16[4,2,256,128]{3,1,2,0:T(2,128)(2,1)}, u32[]{:S(2)}, u32[]{:S(2)}) async-start(bf16[4,2,256,128]{3,1,2,0:T(2,128)(2,1)} %bitcast.235), calls=%async_computation.9 | async-start | bytes 1048576 | tf_op jit(solution)/shard_map/all_to_all | solution.py:223
  519.1 8.5 %all-to-all-start.8 = ((f32[128,4,1536]{2,1,0:T(4,128)}), f32[128,4,1536]{2,1,0:T(4,128)}, u32[]{:S(2)}, u32[]{:S(2)}) async-start(f32[128,4,1536]{2,1,0:T(4,128)} %reshape.528), calls=%async_computation.8 | async-start | bytes 6291456 | tf_op jit(solution)/shard_map/all_to_all | solution.py:258
  529.3 91.3 %psum.7 = f32[3,1536]{1,0:T(4,128)S(1)} all-reduce(f32[3,1536]{1,0:T(4,128)S(1)} %pad_maximum_fusion.10), channel_id=1, replica_groups=mesh['dp'=4,'seq'=32] {'dp','seq'}, use_global_device_ids=true, to_apply=%region_4.5 | all-reduce | flops 4608 | bytes 36864 | tf_op jit(solution)/shard_map/psum | solution.py:255
  (152 shorter events, 159.2 us)
Async XLA Ops:
  3.6 7.2 %collective-permute-start = (bf16[2,1536]{1,0:T(2,128)(2,1)S(1)}, bf16[2,1536]{1,0:T(2,128)(2,1)S(1)}, u32[]{:S(2)}, u32[]{:S(2)}) collective-permute-start(bf16[2,1536]{1,0:T(2,128)(2,1)S(1)} %slice.280), channel_id=1, source_target_pairs={{0,1},{1,2},{2,3},{3,4},{4,5},{5,6},{6,7},{7,8},{8,9},{9,10},{10,1... | collective-permute-start | bytes 18440 | tf_op jit(solution)/shard_map/ppermute | solution.py:15
  8.5 4.2 copy-start.13
  8.5 4.2 copy-start.15
  8.5 4.2 copy-start.17
  10.8 2.1 copy-start.9
  13.9 22.5 %all-to-all-start = ((bf16[32,8,2048]{2,1,0:T(8,128)(2,1)}), bf16[32,8,2048]{2,1,0:T(8,128)(2,1)}, u32[]{:S(2)}, u32[]{:S(2)}) async-start(bf16[32,8,2048]{2,1,0:T(8,128)(2,1)} %pad_maximum_fusion.4), calls=%async_computation | async-start | bytes 2097152 | tf_op jit(solution)/shard_map/all_to_all | solution.py:104
  47.0 63.6 %all-to-all-start.1 = ((bf16[2,64,8,2048]{3,2,0,1:T(8,128)(2,1)}), bf16[2,64,8,2048]{3,2,0,1:T(8,128)(2,1)}, u32[]{:S(2)}, u32[]{:S(2)}) async-start(bf16[2,64,8,2048]{3,2,0,1:T(8,128)(2,1)} %copy.138), calls=%async_computation.1 | async-start | bytes 8388608 | tf_op jit(solution)/shard_map/all_to_all | solution.py:121
  149.6 3.4 copy-start.1
  186.0 31.5 %all-to-all-start.2 = ((bf16[2,2,256,1024]{3,1,0,2:T(2,128)(2,1)}), bf16[2,2,256,1024]{3,1,0,2:T(2,128)(2,1)}, u32[]{:S(2)}, u32[]{:S(2)}) async-start(bf16[2,2,256,1024]{3,1,0,2:T(2,128)(2,1)} %copy.154), calls=%async_computation.2 | async-start | bytes 4194304 | tf_op jit(solution)/shard_map/all_to_all | solution.py:140
  268.8 29.8 %all-to-all-start.5 = ((bf16[2,64,8,1024]{3,2,0,1:T(8,128)(2,1)}), bf16[2,64,8,1024]{3,2,0,1:T(8,128)(2,1)}, u32[]{:S(2)}, u32[]{:S(2)}) async-start(bf16[2,64,8,1024]{3,2,0,1:T(8,128)(2,1)} %copy.159), calls=%async_computation.5 | async-start | bytes 4194304 | tf_op jit(solution)/shard_map/all_to_all | solution.py:121
  317.3 2.2 slice-start
  317.3 3.5 slice-start.1
  472.6 24.6 %copy-start.11 = (bf16[1,256,512]{2,1,0:T(8,128)(2,1)S(1)}, bf16[1,256,512]{2,1,0:T(8,128)(2,1)}, u32[]{:S(2)}) copy-start(bf16[1,256,512]{2,1,0:T(8,128)(2,1)} %param.9) | copy-start | bytes 786436
  476.1 22.0 %copy-start.7 = (bf16[256,512]{1,0:T(8,128)(2,1)S(1)}, bf16[256,512]{1,0:T(8,128)(2,1)}, u32[]{:S(2)}) copy-start(bf16[256,512]{1,0:T(8,128)(2,1)} %get-tuple-element.47) | copy-start | bytes 786436
  498.1 11.8 %copy-start.4 = (bf16[256,512]{1,0:T(8,128)(2,1)}, bf16[256,512]{1,0:T(8,128)(2,1)S(1)}, u32[]{:S(2)}) copy-start(bf16[256,512]{1,0:T(8,128)(2,1)S(1)} %get-tuple-element.45) | copy-start | bytes 786436
  498.1 12.3 %copy-start.6 = (bf16[256,512]{1,0:T(8,128)(2,1)}, bf16[256,512]{1,0:T(8,128)(2,1)S(1)}, u32[]{:S(2)}) copy-start(bf16[256,512]{1,0:T(8,128)(2,1)S(1)} %slice.318) | copy-start | bytes 786436
  498.1 11.8 %copy-start.14 = (f32[1536]{0:T(1024)S(1)}, f32[1536]{0:T(1024)}, u32[]{:S(2)}) copy-start(f32[1536]{0:T(1024)} %copy-done.13) | copy-start | bytes 18436
  498.1 11.8 %copy-start.16 = (f32[1536]{0:T(1024)S(1)}, f32[1536]{0:T(1024)}, u32[]{:S(2)}) copy-start(f32[1536]{0:T(1024)} %copy-done.15) | copy-start | bytes 18436
  498.1 11.8 %copy-start.18 = (f32[1536]{0:T(1024)S(1)}, f32[1536]{0:T(1024)}, u32[]{:S(2)}) copy-start(f32[1536]{0:T(1024)} %copy-done.17) | copy-start | bytes 18436
  498.2 11.5 %collective-permute-start.1 = (bf16[2,1536]{1,0:T(2,128)(2,1)S(1)}, bf16[2,1536]{1,0:T(2,128)(2,1)S(1)}, u32[]{:S(2)}, u32[]{:S(2)}) collective-permute-start(bf16[2,1536]{1,0:T(2,128)(2,1)S(1)} %slice.319), channel_id=1, source_target_pairs={{1,0},{2,1},{3,2},{4,3},{5,4},{6,5},{7,6},{8,7},{9,8},{10,9},{11,1... | collective-permute-start | bytes 18440 | tf_op jit(solution)/shard_map/ppermute | solution.py:15
  501.3 17.8 %all-to-all-start.9 = ((bf16[4,2,256,128]{3,1,2,0:T(2,128)(2,1)}), bf16[4,2,256,128]{3,1,2,0:T(2,128)(2,1)}, u32[]{:S(2)}, u32[]{:S(2)}) async-start(bf16[4,2,256,128]{3,1,2,0:T(2,128)(2,1)} %bitcast.235), calls=%async_computation.9 | async-start | bytes 1048576 | tf_op jit(solution)/shard_map/all_to_all | solution.py:223
  518.4 9.2 %copy-start.3 = (f32[258,1536]{1,0:T(8,128)S(1)}, f32[258,1536]{1,0:T(8,128)}, u32[]{:S(2)}) copy-start(f32[258,1536]{1,0:T(8,128)} %copy-done.2) | copy-start | bytes 4755460
  518.4 9.2 %copy-start.5 = (bf16[256,512]{1,0:T(8,128)(2,1)S(1)}, bf16[256,512]{1,0:T(8,128)(2,1)}, u32[]{:S(2)}) copy-start(bf16[256,512]{1,0:T(8,128)(2,1)} %copy-done.4) | copy-start | bytes 786436
  519.1 107.1 %all-to-all-start.8 = ((f32[128,4,1536]{2,1,0:T(4,128)}), f32[128,4,1536]{2,1,0:T(4,128)}, u32[]{:S(2)}, u32[]{:S(2)}) async-start(f32[128,4,1536]{2,1,0:T(4,128)} %reshape.528), calls=%async_computation.8 | async-start | bytes 6291456 | tf_op jit(solution)/shard_map/all_to_all | solution.py:258
  (5 other events, 7.1 us)

commit v2 on v1

--- a/solution.py
+++ b/solution.py
@@ -252,9 +252,20 @@
             for tap_index in range(tap_count)
         ]
     )
-    grad_taps = lax.psum(taps_terms, ("dp", "seq")) * grad_scale
+    all_devices = data_devices * seq_devices
+    taps_flat = taps_terms.reshape(all_devices, -1)
+    taps_share = jnp.sum(
+        lax.all_to_all(taps_flat, ("dp", "seq"), split_axis=0, concat_axis=0, tiled=True), axis=0
+    )
+    taps_whole = lax.all_to_all(
+        jnp.broadcast_to(taps_share[None], taps_flat.shape),
+        ("dp", "seq"),
+        split_axis=0,
+        concat_axis=0,
+        tiled=True,
+    )
+    grad_taps = taps_whole.reshape(taps_terms.shape) * grad_scale
     proj_terms = jnp.einsum("tc,tj->cj", signal, grad_rows, preferred_element_type=jnp.float32)
-    all_devices = data_devices * seq_devices
     proj_parts = lax.all_to_all(
         proj_terms.reshape(all_devices, proj_terms.shape[0] // all_devices, proj_terms.shape[1]),
         ("dp", "seq"),

time: 639 us -> 612 us (0.958)
  blocking collectives: 201 us -> 110 us
  waiting for transfers between devices: 117 us -> 165 us
  starting transfers between devices: 50.8 us -> 62.8 us
    psum x1 -> x0, blocking collectives: 91.3 us -> none  [shards(): grad_taps = lax.psum(taps_terms, ('dp', 'seq')) * grad_scale]
    all_to_all x1, waiting for transfers between devices: 0.01 us -> 36.1 us  [shards(): lax.all_to_all(proj_terms.reshape(all_devices, proj_terms.shape[0] // all...]
    all_to_all x0 -> x2, starting transfers between devices: none -> 17.8 us  [the longest x1 9.92 us: shards(): lax.all_to_all(taps_flat, ('dp', 'seq'), split_axis=0, concat_axis=0, til...]
    all_to_all x0 -> x2, waiting for transfers between devices: none -> 12.2 us  [the longest x1 8.51 us: shards(): lax.all_to_all(jnp.broadcast_to(taps_share[None], taps_flat.shape), ('dp'...]
  transfers between devices with their start and end apart: 8 -> 10, of which waited for: 5 -> 7; matrix products, arithmetic and copies ran while one was open for 3% -> 4% of each run, Pallas kernels for 0% -> 0%
where the time goes in v2:
time: 612 us; the launch traced here: 603 us
  waiting for transfers between devices  165 us (27%)
  local copies, waits for them, and re-layouts  118 us (19%)
  blocking collectives  110 us (18%)
  matrix products  96.1 us (16%)
  starting transfers between devices  62.8 us (10%)
  other arithmetic  48.6 us (8%)
    all_to_all x2, waiting for transfers between devices, forward_transform(): lax.all_to_all(stacked, 'seq', split_axis=1, concat_axis=2, tiled=True)  79.1 us
    dot_general x8, matrix products, dft_pair(): jnp.einsum('yz' + table_part + ',z' + data_part + '->y' + result_side, bl...  78.6 us
    all_to_all x1, blocking collectives, inverse_transform(): lax.all_to_all(stacked.astype(jnp.bfloat16), 'seq', split_axis=2, concat_...  56.3 us
    all_to_all x2, blocking collectives, inverse_transform(): lax.all_to_all(values.astype(jnp.bfloat16), 'seq', split_axis=0, concat_a...  38.8 us
    all_to_all x1, waiting for transfers between devices, shards(): lax.all_to_all(proj_terms.reshape(all_devices, proj_terms.shape[0] // all...  36.1 us
    all_to_all x6, local copies, waits for them, and re-layouts, inverse_transform(): lax.all_to_all(stacked.astype(jnp.bfloat16), 'seq', split_axis=2, concat_...  25.7 us
    another operation x5, local copies, waits for them, and re-layouts, rotate_stacked(): jnp.stack([stacked[0] * cosine_table - direction * stacked[1] * sine_tabl...  24.5 us
    all_to_all x1, waiting for transfers between devices, inverse_transform(): lax.all_to_all(stacked.astype(jnp.bfloat16), 'seq', split_axis=2, concat_...  23.7 us
  transfers between devices with their start and end apart: 10, of which 7 were waited for; matrix products, arithmetic and copies ran while one was open for 4% of the time, Pallas kernels for 0%

profile of v2, /device:TPU:1, one launch (start us, length us, event | category | flops | bytes accessed | tf_op | source)
XLA Modules:
  0.0 602.9 jit_solution(16305419852619392462)
XLA Ops:
  13.9 8.2 %all-to-all-start = ((bf16[32,8,2048]{2,1,0:T(8,128)(2,1)}), bf16[32,8,2048]{2,1,0:T(8,128)(2,1)}, u32[]{:S(2)}, u32[]{:S(2)}) async-start(bf16[32,8,2048]{2,1,0:T(8,128)(2,1)} %pad_maximum_fusion.4), calls=%async_computation | async-start | bytes 2097152 | tf_op jit(solution)/shard_map/all_to_all | solution.py:104
  22.4 14.0 %all-to-all-done = bf16[32,8,2048]{2,1,0:T(8,128)(2,1)} async-done(((bf16[32,8,2048]{2,1,0:T(8,128)(2,1)}), bf16[32,8,2048]{2,1,0:T(8,128)(2,1)}, u32[]{:S(2)}, u32[]{:S(2)}) %all-to-all-start) | async-done | bytes 1048608 | tf_op jit(solution)/shard_map/all_to_all | solution.py:104
  55.4 55.2 %all-to-all-done.1 = bf16[2,64,8,2048]{3,2,0,1:T(8,128)(2,1)} async-done(((bf16[2,64,8,2048]{3,2,0,1:T(8,128)(2,1)}), bf16[2,64,8,2048]{3,2,0,1:T(8,128)(2,1)}, u32[]{:S(2)}, u32[]{:S(2)}) %all-to-all-start.1) | async-done | bytes 4194336 | tf_op jit(solution)/shard_map/all_to_all | solution.py:121
  113.4 13.5 %convolution_bitcast_fusion = f32[2,2,2,128,2048]{4,2,0,3,1:T(2,128)S(1)} fusion(bf16[2,2,2,128,2048,1]{4,3,2,1,0,5:T(8,128)(2,1)S(1)} %bitcast.253, f32[1,2,2,2]{1,2,3,0:T(2,128)S(1)} %copy.144, f32[1,2,2,2]{1,2,3,0:T(2,128)S(1)} %copy.143), kind=kOutput, calls=%fused_computation.10 | convolution fusion | flops 50331664 | bytes 12582976 | tf_op jit(solution)/shard_map/yzga,zkabw->ykgbw/dot_general | solution.py:44
  137.4 11.2 %fusion.6 = f32[2,2,2,128,2048]{4,3,0,2,1:T(8,128)S(1)} fusion(f32[2,2,2,128,2048,1]{4,2,0,3,1,5:T(2,128)S(1)} %maximum_bitcast_fusion, f32[1,2,128,128]{3,2,1,0:T(8,128)S(1)} %get-tuple-element.49, f32[1,2,128,128]{3,2,1,0:T(8,128)S(1)} %get-tuple-element.52), kind=kOutput, calls=%fused_computation.11 | convolution fusion | flops 3221291008 | bytes 17039360 | tf_op jit(solution)/shard_map/yzfb,zkgbw->ykgfw/dot_general | solution.py:44
  160.0 7.3 %copy.190 = f32[2,2,2,128,1024,1]{4,0,2,5,3,1:T(2,128)} copy(f32[2,2,2,128,1024,1]{3,4,0,2,1,5:T(8,128)} %maximum_bitcast_fusion.5) | data formatting | bytes 8388608 | tf_op jit(solution)/shard_map/stack | solution.py:29
  167.4 11.6 %fusion.19 = f32[2,2,2,128,1024]{4,2,0,3,1:T(2,128)S(1)} fusion(f32[2,2,2,128,1024,1]{4,0,2,5,3,1:T(2,128)} %copy.190, f32[1,2,2,2]{1,2,3,0:T(2,128)S(1)} %copy.152, f32[1,2,2,2]{1,2,3,0:T(2,128)S(1)} %copy.151), kind=kOutput, calls=%fused_computation.30 | convolution fusion | flops 26214416 | bytes 8388672 | tf_op jit(solution)/shard_map/yzag,zkgbw->ykabw/dot_general | solution.py:44
  186.1 7.7 %all-to-all-start.2 = ((bf16[2,2,256,1024]{3,1,0,2:T(2,128)(2,1)}), bf16[2,2,256,1024]{3,1,0,2:T(2,128)(2,1)}, u32[]{:S(2)}, u32[]{:S(2)}) async-start(bf16[2,2,256,1024]{3,1,0,2:T(2,128)(2,1)} %copy.156), calls=%async_computation.2 | async-start | bytes 4194304 | tf_op jit(solution)/shard_map/all_to_all | solution.py:140
  193.9 23.7 %all-to-all-done.2 = bf16[2,2,256,1024]{3,1,0,2:T(2,128)(2,1)} async-done(((bf16[2,2,256,1024]{3,1,0,2:T(2,128)(2,1)}), bf16[2,2,256,1024]{3,1,0,2:T(2,128)(2,1)}, u32[]{:S(2)}, u32[]{:S(2)}) %all-to-all-start.2) | async-done | bytes 2097184 | tf_op jit(solution)/shard_map/all_to_all | solution.py:140
  230.2 18.3 %all_to_all.119 = bf16[32,8,1024]{2,1,0:T(8,128)(2,1)S(1)} all-to-all(bf16[32,8,1024]{2,1,0:T(8,128)(2,1)S(1)} %copy.159), channel_id=1, replica_groups=mesh['dp'=4,'seq'=32] {'seq'}, dimensions={0} | all-to-all | bytes 1048576 | tf_op jit(solution)/shard_map/all_to_all | solution.py:151
  249.4 15.0 %all_to_all.120 = bf16[32,8,1024]{2,1,0:T(8,128)(2,1)S(1)} all-to-all(bf16[32,8,1024]{2,1,0:T(8,128)(2,1)S(1)} %maximum_bitcast_fusion.10), channel_id=1, replica_groups=mesh['dp'=4,'seq'=32] {'seq'}, dimensions={0} | all-to-all | bytes 1048576 | tf_op jit(solution)/shard_map/all_to_all | solution.py:104
  275.2 23.8 %all-to-all-done.5 = bf16[2,64,8,1024]{3,2,0,1:T(8,128)(2,1)} async-done(((bf16[2,64,8,1024]{3,2,0,1:T(8,128)(2,1)}), bf16[2,64,8,1024]{3,2,0,1:T(8,128)(2,1)}, u32[]{:S(2)}, u32[]{:S(2)}) %all-to-all-start.5) | async-done | bytes 2097184 | tf_op jit(solution)/shard_map/all_to_all | solution.py:121
  307.8 7.2 %copy.165 = f32[2,128,1024,2,2]{1,2,3,4,0:T(8,128)} copy(f32[2,128,1024,2,2]{2,4,3,1,0:T(2,128)} %convolution_bitcast_fusion.2) | data formatting | bytes 8388608 | tf_op jit(solution)/shard_map/yzga,zkabw->ykgbw/dot_general | solution.py:44
  324.8 8.9 %fusion.9 = f32[2,2,2048,2,128]{4,2,3,1,0:T(8,128)} fusion(f32[2,2,2,128,2048,1]{4,3,2,1,0,5:T(8,128)S(1)} %bitcast.245, f32[1,2,128,128]{3,2,1,0:T(8,128)S(1)} %get-tuple-element.53, f32[1,2,128,128]{3,2,1,0:T(8,128)S(1)} %get-tuple-element.48), kind=kOutput, calls=%fused_computation.12 | convolution fusion | flops 3221291008 | bytes 17039360 | tf_op jit(solution)/shard_map/yzbf,zkgfw->ykgbw/dot_general | solution.py:44
  333.7 13.3 %copy.169 = f32[2,2,2048,2,128]{2,1,3,4,0:T(2,128)} copy(f32[2,2,2048,2,128]{4,2,3,1,0:T(8,128)} %fusion.9) | data formatting | bytes 16777216 | tf_op jit(solution)/shard_map/yzbf,zkgfw->ykgbw/dot_general | solution.py:44
  347.0 7.2 %multiply_subtract_fusion = (f32[1,2,2,128,2048]{4,2,0,3,1:T(2,128)S(1)}, f32[1,2,2,128,2048]{4,2,0,3,1:T(2,128)S(1)}) fusion(f32[2,2,2,128,2048]{4,2,0,3,1:T(2,128)} %bitcast.246, f32[2,128]{0,1:T(8,128)S(1)} %copy.170, f32[2,128]{0,1:T(8,128)S(1)} %copy.146), kind=kLoop, calls=%fused_computation.35 | loop fusion | flops 6291456 | bytes 16779264 | tf_op jit(solution)/shard_map/sub | solution.py:31
  354.2 20.8 %fusion = f32[2,2,2,128,2048]{4,2,0,3,1:T(2,128)} fusion(f32[2,2,2,2,1,1]{3,2,1,0,5,4:T(2,128)S(1)} %copy.201, f32[1,2,2,128,2048]{4,2,0,3,1:T(2,128)S(1)} %get-tuple-element.20, f32[1,2,2,128,2048]{4,2,0,3,1:T(2,128)S(1)} %get-tuple-element.19), kind=kOutput, calls=%fused_computation.4 | convolution fusion | flops 54525952 | bytes 16777280 | tf_op jit(solution)/shard_map/yzag,zkgbw->ykabw/dot_general | solution.py:44
  375.1 9.5 %fusion.122 = (f32[1,2,2,128,2048]{4,2,0,3,1:T(2,128)}, f32[1,2,2,128,2048]{4,2,0,3,1:T(2,128)S(1)}) fusion(f32[2,2,2,128,2048]{4,2,0,3,1:T(2,128)} %fusion), kind=kLoop, calls=%fused_computation.240 | loop fusion | bytes 16777216 | tf_op jit(solution)/shard_map/slice | solution.py:31
  400.9 56.3 %all_to_all.121 = bf16[2,2,256,2048]{3,1,0,2:T(2,128)(2,1)S(1)} all-to-all(bf16[2,2,256,2048]{3,1,0,2:T(2,128)(2,1)} %copy.174), channel_id=1, replica_groups=mesh['dp'=4,'seq'=32] {'seq'}, dimensions={2} | all-to-all | bytes 8388608 | tf_op jit(solution)/shard_map/all_to_all | solution.py:140
  477.2 20.5 %all_to_all.122 = bf16[32,8,2048]{2,1,0:T(8,128)(2,1)S(1)} all-to-all(bf16[32,8,2048]{2,1,0:T(8,128)(2,1)S(1)} %copy.177), channel_id=1, replica_groups=mesh['dp'=4,'seq'=32] {'seq'}, dimensions={0} | all-to-all | bytes 2097152 | tf_op jit(solution)/shard_map/all_to_all | solution.py:151
  500.2 9.9 %all-to-all-start.9 = ((f32[128,1,36]{2,1,0:T(1,128)}), f32[128,1,36]{2,1,0:T(1,128)S(1)}, u32[]{:S(2)}, u32[]{:S(2)}) async-start(f32[128,1,36]{2,1,0:T(1,128)} %bitcast.95), calls=%async_computation.9 | async-start | bytes 131072 | tf_op jit(solution)/shard_map/all_to_all | solution.py:258
  520.7 7.9 %all-to-all-start.10 = ((f32[128,1,36]{2,1,0:T(1,128)}), f32[128,1,36]{2,1,0:T(1,128)S(1)}, u32[]{:S(2)}, u32[]{:S(2)}) async-start(f32[128,1,36]{2,1,0:T(1,128)} %broadcast_in_dim.8), calls=%async_computation.10 | async-start | bytes 131072 | tf_op jit(solution)/shard_map/all_to_all | solution.py:260
  529.9 8.5 %all-to-all-done.10 = f32[128,1,36]{2,1,0:T(1,128)S(1)} async-done(((f32[128,1,36]{2,1,0:T(1,128)}), f32[128,1,36]{2,1,0:T(1,128)S(1)}, u32[]{:S(2)}, u32[]{:S(2)}) %all-to-all-start.10) | async-done | bytes 18464 | tf_op jit(solution)/shard_map/all_to_all | solution.py:260
  563.6 36.1 %all-to-all-done.8 = f32[128,4,1536]{2,1,0:T(4,128)} async-done(((f32[128,4,1536]{2,1,0:T(4,128)}), f32[128,4,1536]{2,1,0:T(4,128)}, u32[]{:S(2)}, u32[]{:S(2)}) %all-to-all-start.8) | async-done | bytes 3145760 | tf_op jit(solution)/shard_map/all_to_all | solution.py:269
  (163 shorter events, 185.4 us)
Async XLA Ops:
  3.6 7.2 %collective-permute-start = (bf16[2,1536]{1,0:T(2,128)(2,1)S(1)}, bf16[2,1536]{1,0:T(2,128)(2,1)S(1)}, u32[]{:S(2)}, u32[]{:S(2)}) collective-permute-start(bf16[2,1536]{1,0:T(2,128)(2,1)S(1)} %slice.280), channel_id=1, source_target_pairs={{0,1},{1,2},{2,3},{3,4},{4,5},{5,6},{6,7},{7,8},{8,9},{9,10},{10,1... | collective-permute-start | bytes 18440 | tf_op jit(solution)/shard_map/ppermute | solution.py:15
  8.5 4.2 copy-start.15
  8.5 4.2 copy-start.17
  8.5 4.2 copy-start.19
  13.9 22.5 %all-to-all-start = ((bf16[32,8,2048]{2,1,0:T(8,128)(2,1)}), bf16[32,8,2048]{2,1,0:T(8,128)(2,1)}, u32[]{:S(2)}, u32[]{:S(2)}) async-start(bf16[32,8,2048]{2,1,0:T(8,128)(2,1)} %pad_maximum_fusion.4), calls=%async_computation | async-start | bytes 2097152 | tf_op jit(solution)/shard_map/all_to_all | solution.py:104
  47.0 63.6 %all-to-all-start.1 = ((bf16[2,64,8,2048]{3,2,0,1:T(8,128)(2,1)}), bf16[2,64,8,2048]{3,2,0,1:T(8,128)(2,1)}, u32[]{:S(2)}, u32[]{:S(2)}) async-start(bf16[2,64,8,2048]{3,2,0,1:T(8,128)(2,1)} %copy.140), calls=%async_computation.1 | async-start | bytes 8388608 | tf_op jit(solution)/shard_map/all_to_all | solution.py:121
  186.1 31.5 %all-to-all-start.2 = ((bf16[2,2,256,1024]{3,1,0,2:T(2,128)(2,1)}), bf16[2,2,256,1024]{3,1,0,2:T(2,128)(2,1)}, u32[]{:S(2)}, u32[]{:S(2)}) async-start(bf16[2,2,256,1024]{3,1,0,2:T(2,128)(2,1)} %copy.156), calls=%async_computation.2 | async-start | bytes 4194304 | tf_op jit(solution)/shard_map/all_to_all | solution.py:140
  269.2 29.9 %all-to-all-start.5 = ((bf16[2,64,8,1024]{3,2,0,1:T(8,128)(2,1)}), bf16[2,64,8,1024]{3,2,0,1:T(8,128)(2,1)}, u32[]{:S(2)}, u32[]{:S(2)}) async-start(bf16[2,64,8,1024]{3,2,0,1:T(8,128)(2,1)} %copy.161), calls=%async_computation.5 | async-start | bytes 4194304 | tf_op jit(solution)/shard_map/all_to_all | solution.py:121
  317.7 3.5 slice-start.1
  473.1 24.6 %copy-start.14 = (bf16[1,256,512]{2,1,0:T(8,128)(2,1)S(1)}, bf16[1,256,512]{2,1,0:T(8,128)(2,1)}, u32[]{:S(2)}) copy-start(bf16[1,256,512]{2,1,0:T(8,128)(2,1)} %param.9) | copy-start | bytes 786436
  476.6 22.2 %copy-start.3 = (f32[258,1536]{1,0:T(8,128)S(1)}, f32[258,1536]{1,0:T(8,128)}, u32[]{:S(2)}) copy-start(f32[258,1536]{1,0:T(8,128)} %copy-done.2) | copy-start | bytes 4755460
  476.6 22.2 %copy-start.9 = (bf16[256,512]{1,0:T(8,128)(2,1)S(1)}, bf16[256,512]{1,0:T(8,128)(2,1)}, u32[]{:S(2)}) copy-start(bf16[256,512]{1,0:T(8,128)(2,1)} %get-tuple-element.47) | copy-start | bytes 786436
  498.8 14.9 %copy-start.8 = (bf16[256,512]{1,0:T(8,128)(2,1)}, bf16[256,512]{1,0:T(8,128)(2,1)S(1)}, u32[]{:S(2)}) copy-start(bf16[256,512]{1,0:T(8,128)(2,1)S(1)} %slice.318) | copy-start | bytes 786436
  498.8 14.0 %copy-start.5 = (bf16[32,8,2048]{2,1,0:T(8,128)(2,1)S(1)}, bf16[32,8,2048]{2,1,0:T(8,128)(2,1)}, u32[]{:S(2)}) copy-start(bf16[32,8,2048]{2,1,0:T(8,128)(2,1)} %copy-done.4) | copy-start | bytes 3145732
  499.4 29.2 %copy-start.7 = (bf16[256,512]{1,0:T(8,128)(2,1)S(1)}, bf16[256,512]{1,0:T(8,128)(2,1)}, u32[]{:S(2)}) copy-start(bf16[256,512]{1,0:T(8,128)(2,1)} %copy-done.6) | copy-start | bytes 786436
  500.2 19.7 %all-to-all-start.9 = ((f32[128,1,36]{2,1,0:T(1,128)}), f32[128,1,36]{2,1,0:T(1,128)S(1)}, u32[]{:S(2)}, u32[]{:S(2)}) async-start(f32[128,1,36]{2,1,0:T(1,128)} %bitcast.95), calls=%async_computation.9 | async-start | bytes 131072 | tf_op jit(solution)/shard_map/all_to_all | solution.py:258
  510.2 33.2 %copy-start.16 = (f32[1536]{0:T(1024)S(1)}, f32[1536]{0:T(1024)}, u32[]{:S(2)}) copy-start(f32[1536]{0:T(1024)} %copy-done.15) | copy-start | bytes 18436
  510.2 33.2 %copy-start.18 = (f32[1536]{0:T(1024)S(1)}, f32[1536]{0:T(1024)}, u32[]{:S(2)}) copy-start(f32[1536]{0:T(1024)} %copy-done.17) | copy-start | bytes 18436
  510.2 33.2 %copy-start.20 = (f32[1536]{0:T(1024)S(1)}, f32[1536]{0:T(1024)}, u32[]{:S(2)}) copy-start(f32[1536]{0:T(1024)} %copy-done.19) | copy-start | bytes 18436
  511.3 17.3 %collective-permute-start.1 = (bf16[2,1536]{1,0:T(2,128)(2,1)S(1)}, bf16[2,1536]{1,0:T(2,128)(2,1)S(1)}, u32[]{:S(2)}, u32[]{:S(2)}) collective-permute-start(bf16[2,1536]{1,0:T(2,128)(2,1)S(1)} %slice.319), channel_id=1, source_target_pairs={{1,0},{2,1},{3,2},{4,3},{5,4},{6,5},{7,6},{8,7},{9,8},{10,9},{11,1... | collective-permute-start | bytes 18440 | tf_op jit(solution)/shard_map/ppermute | solution.py:15
  520.7 17.7 %all-to-all-start.10 = ((f32[128,1,36]{2,1,0:T(1,128)}), f32[128,1,36]{2,1,0:T(1,128)S(1)}, u32[]{:S(2)}, u32[]{:S(2)}) async-start(f32[128,1,36]{2,1,0:T(1,128)} %broadcast_in_dim.8), calls=%async_computation.10 | async-start | bytes 131072 | tf_op jit(solution)/shard_map/all_to_all | solution.py:260
  538.4 14.4 %all-to-all-start.11 = ((bf16[4,2,256,128]{3,1,2,0:T(2,128)(2,1)}), bf16[4,2,256,128]{3,1,2,0:T(2,128)(2,1)}, u32[]{:S(2)}, u32[]{:S(2)}) async-start(bf16[4,2,256,128]{3,1,2,0:T(2,128)(2,1)} %bitcast.256), calls=%async_computation.11 | async-start | bytes 1048576 | tf_op jit(solution)/shard_map/all_to_all | solution.py:223
  552.8 6.0 copy-start.11
  552.8 46.8 %all-to-all-start.8 = ((f32[128,4,1536]{2,1,0:T(4,128)}), f32[128,4,1536]{2,1,0:T(4,128)}, u32[]{:S(2)}, u32[]{:S(2)}) async-start(f32[128,4,1536]{2,1,0:T(4,128)} %reshape.542), calls=%async_computation.8 | async-start | bytes 6291456 | tf_op jit(solution)/shard_map/all_to_all | solution.py:269
  (9 other events, 14.9 us)

commit v3 on v2

--- a/solution.py
+++ b/solution.py
@@ -109,48 +109,59 @@
         tiled=True,
     )
     values = received.astype(jnp.float32)
-    cosine_table, sine_table = angle_table(freq_rows, seq_devices, freq_rows)
-    part_table = jnp.stack([cosine_table, -sine_table])
+    cosine_table, sine_table = angle_table(seq_devices, seq_devices, freq_rows)
+    alternating = jnp.where(jnp.arange(seq_devices) % 2 == 0, 1.0, -1.0).astype(jnp.float32)
+    part_table = jnp.stack([cosine_table, (-sine_table).at[0].set(alternating)])
     section = jnp.einsum("ykq,qrw->ykrw", part_table, values, precision=PRECISE)
     frame_ids = lax.axis_index("seq") * block_rows + jnp.arange(block_rows, dtype=jnp.int32)
-    products = jnp.arange(freq_rows, dtype=jnp.int32)[:, None] * frame_ids[None, :] % fft_length
+    products = (
+        jnp.arange(seq_devices, dtype=jnp.int32)[:, None] * frame_ids[None, :] % fft_length
+    )
     angles = products.astype(jnp.float32) * (FULL_TURN / fft_length)
     stacked = rotate_stacked(
         section, jnp.cos(angles)[:, :, None], jnp.sin(angles)[:, :, None], -1.0
     ).astype(jnp.bfloat16)
     regrouped = lax.all_to_all(stacked, "seq", split_axis=1, concat_axis=2, tiled=True)
-    return local_forward(regrouped.astype(jnp.float32))
+    data = regrouped[:, 0].astype(jnp.float32)
+    first_device = lax.axis_index("seq") == 0
+    products = seq_devices * jnp.arange(frames, dtype=jnp.int32) % fft_length
+    angles = (products.astype(jnp.float32) * (FULL_TURN / fft_length))[:, None]
+    zeros = jnp.zeros_like(data[0])
+    row_low = jnp.where(first_device, jnp.stack([data[0], zeros]), data)
+    row_high = jnp.where(
+        first_device,
+        jnp.stack([jnp.cos(angles) * data[1], -jnp.sin(angles) * data[1]]),
+        jnp.zeros_like(data),
+    )
+    return local_forward(jnp.stack([row_low, row_high], axis=1))
 
 
 def inverse_transform(spectra, keep_wide):
     seq_devices = lax.axis_size("seq")
     local_freqs, frames, channels = (spectra.shape[1], spectra.shape[2], spectra.shape[3])
+    block_rows = frames // seq_devices
     freq_rows = 2 * seq_devices
     fft_length = freq_rows * frames
     stacked = local_inverse(spectra)
-    freq_ids = lax.axis_index("seq") * local_freqs + jnp.arange(local_freqs, dtype=jnp.int32)
+    device = lax.axis_index("seq")
+    freq_ids = jnp.stack([device, jnp.int32(seq_devices)]).astype(jnp.int32)
     products = freq_ids[:, None] * jnp.arange(frames, dtype=jnp.int32)[None, :] % fft_length
     angles = products.astype(jnp.float32) * (FULL_TURN / fft_length)
     stacked = rotate_stacked(stacked, jnp.cos(angles)[:, :, None], jnp.sin(angles)[:, :, None], 1.0)
-    if keep_wide:
-        regrouped = lax.all_to_all(
-            stacked.astype(jnp.bfloat16), "seq", split_axis=2, concat_axis=1, tiled=True
-        ).astype(stacked.dtype)
-    else:
-        regrouped = lax.all_to_all(
-            stacked.astype(jnp.bfloat16), "seq", split_axis=2, concat_axis=1, tiled=True
-        ).astype(jnp.float32)
-    cosine_table, sine_table = angle_table(seq_devices, freq_rows, freq_rows)
-    part_table = jnp.stack([cosine_table, -sine_table])
-    values = jnp.einsum("zqk,zkrw->qrw", part_table, regrouped, precision=PRECISE) / freq_rows
-    if keep_wide:
-        returned = lax.all_to_all(
-            values.astype(jnp.bfloat16), "seq", split_axis=0, concat_axis=1, tiled=True
-        ).astype(values.dtype)
-    else:
-        returned = lax.all_to_all(
-            values.astype(jnp.bfloat16), "seq", split_axis=0, concat_axis=1, tiled=True
-        )
+    back = stacked.astype(jnp.bfloat16)
+    packed = jnp.where(device == 0, jnp.stack([back[0, 0], back[0, 1]]), back[:, 0])
+    regrouped = lax.all_to_all(
+        packed[:, None], "seq", split_axis=2, concat_axis=1, tiled=True
+    ).astype(jnp.float32)
+    cosine_table, sine_table = angle_table(seq_devices, seq_devices, freq_rows)
+    alternating = jnp.where(jnp.arange(seq_devices) % 2 == 0, 1.0, -1.0).astype(jnp.float32)
+    real_table = (2.0 * cosine_table).at[:, 0].set(1.0)
+    imag_table = (-2.0 * sine_table).at[:, 0].set(alternating)
+    part_table = jnp.stack([real_table, imag_table]) / freq_rows
+    values = jnp.einsum("zqk,zkrw->qrw", part_table, regrouped, precision=PRECISE)
+    returned = lax.all_to_all(
+        values.astype(jnp.bfloat16), "seq", split_axis=0, concat_axis=1, tiled=True
+    )
     return returned.reshape(frames, channels)
 
 

time: 612 us -> 516 us (0.84)
  waiting for transfers between devices: 165 us -> 108 us
  blocking collectives: 110 us -> 82.3 us
  local copies, waits for them, and re-layouts: 118 us -> 91.3 us
  other arithmetic: 48.6 us -> 65.8 us
    all_to_all x2, waiting for transfers between devices: 79.1 us -> 35 us  [forward_transform(): lax.all_to_all(stacked, 'seq', split_axis=1, concat_axis=2, tiled=True)]
    all_to_all x6 -> x0, local copies, waits for them, and re-layouts: 25.7 us -> none  [inverse_transform(): lax.all_to_all(stacked.astype(jnp.bfloat16), 'seq', split_axis=2, concat_...]
    all_to_all x1, blocking collectives: 56.3 us -> 31.7 us  [inverse_transform(): lax.all_to_all(packed[:, None], 'seq', split_axis=2, concat_axis=1, tiled...]
    all_to_all x1, waiting for transfers between devices: 23.7 us -> 7.4 us  [inverse_transform(): lax.all_to_all(packed[:, None], 'seq', split_axis=2, concat_axis=1, tiled...]
    another operation x5 -> x3, local copies, waits for them, and re-layouts: 24.5 us -> 11.4 us  [rotate_stacked(): jnp.stack([stacked[0] * cosine_table - direction * stacked[1] * sine_tabl...]
    select_n x0 -> x7, other arithmetic: none -> 12.6 us  [the longest x2 6.63 us: forward_transform(): jnp.where(first_device, jnp.stack([jnp.cos(angles) * data[1], -jnp.sin(an...]
    dot_general x8, matrix products: 78.6 us -> 87.8 us  [dft_pair(): jnp.einsum('yz' + table_part + ',z' + data_part + '->y' + result_side, bl...]
    another operation x0 -> x6, local copies, waits for them, and re-layouts: none -> 8.55 us  [the longest x4 6.47 us: forward_transform(): jnp.stack([jnp.cos(angles) * data[1], -jnp.sin(angles) * data[1]])]
  transfers between devices with their start and end apart: 10 -> 10, of which waited for: 7 -> 8; matrix products, arithmetic and copies ran while one was open for 4% -> 6% of each run, Pallas kernels for 0% -> 0%
where the time goes in v3:
time: 516 us; the launch traced here: 508 us
  waiting for transfers between devices  108 us (21%)
  matrix products  101 us (20%)
  local copies, waits for them, and re-layouts  91.3 us (18%)
  blocking collectives  82.3 us (16%)
  other arithmetic  65.8 us (13%)
  starting transfers between devices  58.2 us (11%)
    dot_general x8, matrix products, dft_pair(): jnp.einsum('yz' + table_part + ',z' + data_part + '->y' + result_side, bl...  87.8 us
    all_to_all x1, waiting for transfers between devices, shards(): lax.all_to_all(proj_terms.reshape(all_devices, proj_terms.shape[0] // all...  36.2 us
    all_to_all x2, blocking collectives, inverse_transform(): lax.all_to_all(values.astype(jnp.bfloat16), 'seq', split_axis=0, concat_a...  36.1 us
    all_to_all x2, waiting for transfers between devices, forward_transform(): lax.all_to_all(stacked, 'seq', split_axis=1, concat_axis=2, tiled=True)  35 us
    all_to_all x1, blocking collectives, inverse_transform(): lax.all_to_all(packed[:, None], 'seq', split_axis=2, concat_axis=1, tiled...  31.7 us
    dot_general x2, local copies, waits for them, and re-layouts, dft_pair(): jnp.einsum('yz' + table_part + ',z' + data_part + '->y' + result_side, bl...  20.9 us
    slice x4, local copies, waits for them, and re-layouts, rotate_stacked(): stacked[0] * cosine_table - direction * stacked[1] * sine_table  16.5 us
    sub x4, other arithmetic, rotate_stacked(): stacked[0] * cosine_table - direction * stacked[1] * sine_table  15.1 us
  transfers between devices with their start and end apart: 10, of which 8 were waited for; matrix products, arithmetic and copies ran while one was open for 6% of the time, Pallas kernels for 0%

profile of v3, /device:TPU:1, one launch (start us, length us, event | category | flops | bytes accessed | tf_op | source)
XLA Modules:
  0.0 508.1 jit_solution(7284474090291778342)
XLA Ops:
  12.0 8.3 %all-to-all-start = ((bf16[32,8,2048]{2,1,0:T(8,128)(2,1)}), bf16[32,8,2048]{2,1,0:T(8,128)(2,1)S(1)}, u32[]{:S(2)}, u32[]{:S(2)}) async-start(bf16[32,8,2048]{2,1,0:T(8,128)(2,1)} %pad_maximum_fusion.3), calls=%async_computation | async-start | bytes 2097152 | tf_op jit(solution)/shard_map/all_to_all | solution.py:104
  20.6 13.9 %all-to-all-done = bf16[32,8,2048]{2,1,0:T(8,128)(2,1)S(1)} async-done(((bf16[32,8,2048]{2,1,0:T(8,128)(2,1)}), bf16[32,8,2048]{2,1,0:T(8,128)(2,1)S(1)}, u32[]{:S(2)}, u32[]{:S(2)}) %all-to-all-start) | async-done | bytes 1048608 | tf_op jit(solution)/shard_map/all_to_all | solution.py:104
  40.4 6.9 %all-to-all-start.1 = ((bf16[2,32,8,2048]{3,2,0,1:T(8,128)(2,1)}), bf16[2,32,8,2048]{3,2,0,1:T(8,128)(2,1)}, u32[]{:S(2)}, u32[]{:S(2)}) async-start(bf16[2,32,8,2048]{3,2,0,1:T(8,128)(2,1)} %copy.174), calls=%async_computation.1 | async-start | bytes 4194304 | tf_op jit(solution)/shard_map/all_to_all | solution.py:124
  49.3 24.8 %all-to-all-done.1 = bf16[2,32,8,2048]{3,2,0,1:T(8,128)(2,1)} async-done(((bf16[2,32,8,2048]{3,2,0,1:T(8,128)(2,1)}), bf16[2,32,8,2048]{3,2,0,1:T(8,128)(2,1)}, u32[]{:S(2)}, u32[]{:S(2)}) %all-to-all-start.1) | async-done | bytes 2097184 | tf_op jit(solution)/shard_map/all_to_all | solution.py:124
  90.4 19.8 %fusion.7 = f32[2,2,2,128,2048]{4,2,0,3,1:T(2,128)S(1)} fusion(f32[2,1,2,128,2048]{4,0,2,3,1:T(2,128)S(1)} %maximum_select_fusion, f32[2,1,2,128,2048]{4,0,2,3,1:T(2,128)S(1)} %select_select_fusion, f32[1,2,2,2]{1,2,3,0:T(2,128)S(1)} %copy.182, f32[1,2,2,2]{1,2,3,0:T(2,128)S(1)} %copy.181), kind=kOutput, calls=%fused_computation.12 | convolution fusion | flops 52428816 | bytes 16777280 | tf_op jit(solution)/shard_map/yzga,zkabw->ykgbw/dot_general | solution.py:44
  120.2 11.2 %fusion.8 = f32[2,2,2,128,2048]{4,3,0,2,1:T(8,128)S(1)} fusion(f32[2,2,2,128,2048,1]{4,2,0,3,1,5:T(2,128)S(1)} %maximum_bitcast_fusion.1, f32[1,2,128,128]{3,2,1,0:T(8,128)S(1)} %get-tuple-element.117, f32[1,2,128,128]{3,2,1,0:T(8,128)S(1)} %get-tuple-element.120), kind=kOutput, calls=%fused_computation.14 | convolution fusion | flops 3221291008 | bytes 17039360 | tf_op jit(solution)/shard_map/yzfb,zkgbw->ykgfw/dot_general | solution.py:44
  143.2 7.4 %copy.230 = f32[2,2,2,128,1024,1]{4,0,2,5,3,1:T(2,128)} copy(f32[2,2,2,128,1024,1]{3,4,0,2,1,5:T(8,128)} %maximum_bitcast_fusion.9) | data formatting | bytes 8388608 | tf_op jit(solution)/shard_map/stack | solution.py:29
  150.6 11.3 %fusion.21 = f32[2,2,2,128,1024]{4,2,0,3,1:T(2,128)S(1)} fusion(f32[2,2,2,128,1024,1]{4,0,2,5,3,1:T(2,128)} %copy.230, f32[1,2,2,2]{1,2,3,0:T(2,128)S(1)} %copy.189, f32[1,2,2,2]{1,2,3,0:T(2,128)S(1)} %copy.188), kind=kOutput, calls=%fused_computation.33 | convolution fusion | flops 26214416 | bytes 8388672 | tf_op jit(solution)/shard_map/yzag,zkgbw->ykabw/dot_general | solution.py:44
  180.8 7.4 %all-to-all-done.2 = bf16[2,1,256,1024]{3,0,1,2:T(2,128)(2,1)S(1)} async-done(((bf16[2,1,256,1024]{3,0,1,2:T(2,128)(2,1)}), bf16[2,1,256,1024]{3,0,1,2:T(2,128)(2,1)S(1)}, u32[]{:S(2)}, u32[]{:S(2)}) %all-to-all-start.2) | async-done | bytes 1048608 | tf_op jit(solution)/shard_map/all_to_all | solution.py:153
  190.2 15.5 %all_to_all.95 = bf16[32,8,1024]{2,1,0:T(8,128)(2,1)S(1)} all-to-all(bf16[32,8,1024]{2,1,0:T(8,128)(2,1)S(1)} %copy.196), channel_id=1, replica_groups=mesh['dp'=4,'seq'=32] {'seq'}, dimensions={0} | all-to-all | bytes 1048576 | tf_op jit(solution)/shard_map/all_to_all | solution.py:162
  206.6 14.5 %all_to_all.96 = bf16[32,8,1024]{2,1,0:T(8,128)(2,1)S(1)} all-to-all(bf16[32,8,1024]{2,1,0:T(8,128)(2,1)S(1)} %maximum_bitcast_fusion.18), channel_id=1, replica_groups=mesh['dp'=4,'seq'=32] {'seq'}, dimensions={0} | all-to-all | bytes 1048576 | tf_op jit(solution)/shard_map/all_to_all | solution.py:104
  233.6 10.2 %all-to-all-done.5 = bf16[2,32,8,1024]{3,2,0,1:T(8,128)(2,1)S(1)} async-done(((bf16[2,32,8,1024]{3,2,0,1:T(8,128)(2,1)}), bf16[2,32,8,1024]{3,2,0,1:T(8,128)(2,1)S(1)}, u32[]{:S(2)}, u32[]{:S(2)}) %all-to-all-start.5) | async-done | bytes 1048608 | tf_op jit(solution)/shard_map/all_to_all | solution.py:124
  251.7 9.6 %fusion.25 = f32[2,128,1024,2,2]{2,4,3,1,0:T(2,128)} fusion(f32[2,1,2,128,1024]{4,0,2,3,1:T(2,128)S(1)} %maximum_select_fusion.1, f32[2,1,2,128,1024]{4,0,2,3,1:T(2,128)S(1)} %select_select_fusion.1, f32[1,2,2,2]{1,2,3,0:T(2,128)S(1)} %copy-done.59, f32[1,2,2,2]{1,2,3,0:T(2,128)S(1)} %copy-done.57), kind=kOutput, calls=%fused_computation.41 | convolution fusion | flops 26214416 | bytes 8388672 | tf_op jit(solution)/shard_map/yzga,zkabw->ykgbw/dot_general | solution.py:44
  261.4 7.6 %copy.205 = f32[2,128,1024,2,2]{1,2,3,4,0:T(8,128)} copy(f32[2,128,1024,2,2]{2,4,3,1,0:T(2,128)} %fusion.25) | data formatting | bytes 8388608 | tf_op jit(solution)/shard_map/yzga,zkabw->ykgbw/dot_general | solution.py:44
  277.9 9.0 %fusion.11 = f32[2,2,2048,2,128]{4,2,3,1,0:T(8,128)} fusion(f32[2,2,2,128,2048,1]{4,3,2,1,0,5:T(8,128)S(1)} %bitcast.256, f32[1,2,128,128]{3,2,1,0:T(8,128)S(1)} %copy-done.13, f32[1,2,128,128]{3,2,1,0:T(8,128)S(1)} %get-tuple-element.116), kind=kOutput, calls=%fused_computation.15 | convolution fusion | flops 3221291008 | bytes 17039360 | tf_op jit(solution)/shard_map/yzbf,zkgfw->ykgbw/dot_general | solution.py:44
  286.8 13.3 %copy.209 = f32[2,2,2048,2,128]{2,1,3,4,0:T(2,128)} copy(f32[2,2,2048,2,128]{4,2,3,1,0:T(8,128)} %fusion.11) | data formatting | bytes 16777216 | tf_op jit(solution)/shard_map/yzbf,zkgfw->ykgbw/dot_general | solution.py:44
  300.1 7.1 %multiply_subtract_fusion = (f32[1,2,2,128,2048]{4,2,0,3,1:T(2,128)S(1)}, f32[1,2,2,128,2048]{4,2,0,3,1:T(2,128)S(1)}) fusion(f32[2,2,2,128,2048]{4,2,0,3,1:T(2,128)} %bitcast.257, f32[2,128]{0,1:T(8,128)S(1)} %copy-done.24, f32[2,128]{0,1:T(8,128)S(1)} %copy-done.22), kind=kLoop, calls=%fused_computation.37 | loop fusion | flops 6291456 | bytes 16779264 | tf_op jit(solution)/shard_map/sub | solution.py:31
  307.2 21.0 %fusion = f32[2,2,2,128,2048]{4,2,0,3,1:T(2,128)} fusion(f32[2,2,2,2,1,1]{3,2,1,0,5,4:T(2,128)S(1)} %copy-done.53, f32[1,2,2,128,2048]{4,2,0,3,1:T(2,128)S(1)} %get-tuple-element.80, f32[1,2,2,128,2048]{4,2,0,3,1:T(2,128)S(1)} %get-tuple-element.79), kind=kOutput, calls=%fused_computation.5 | convolution fusion | flops 54525952 | bytes 16777280 | tf_op jit(solution)/shard_map/yzag,zkgbw->ykabw/dot_general | solution.py:44
  328.2 9.6 %fusion.140 = (f32[1,2,2,128,2048]{4,2,0,3,1:T(2,128)}, f32[1,2,2,128,2048]{4,2,0,3,1:T(2,128)S(1)}) fusion(f32[2,2,2,128,2048]{4,2,0,3,1:T(2,128)} %fusion), kind=kLoop, calls=%fused_computation.275 | loop fusion | bytes 16777216 | tf_op jit(solution)/shard_map/slice | solution.py:31
  350.1 31.7 %all_to_all.97 = bf16[2,1,256,2048]{3,0,1,2:T(2,128)(2,1)S(1)} all-to-all(bf16[2,1,256,2048]{3,0,1,2:T(2,128)(2,1)S(1)} %copy.214), channel_id=1, replica_groups=mesh['dp'=4,'seq'=32] {'seq'}, dimensions={2} | all-to-all | bytes 4194304 | tf_op jit(solution)/shard_map/all_to_all | solution.py:153
  385.0 20.6 %all_to_all.98 = bf16[32,8,2048]{2,1,0:T(8,128)(2,1)S(1)} all-to-all(bf16[32,8,2048]{2,1,0:T(8,128)(2,1)S(1)} %copy.217), channel_id=1, replica_groups=mesh['dp'=4,'seq'=32] {'seq'}, dimensions={0} | all-to-all | bytes 2097152 | tf_op jit(solution)/shard_map/all_to_all | solution.py:162
  407.9 9.8 %all-to-all-start.9 = ((f32[128,1,36]{2,1,0:T(1,128)}), f32[128,1,36]{2,1,0:T(1,128)S(1)}, u32[]{:S(2)}, u32[]{:S(2)}) async-start(f32[128,1,36]{2,1,0:T(1,128)} %bitcast.102), calls=%async_computation.9 | async-start | bytes 131072 | tf_op jit(solution)/shard_map/all_to_all | solution.py:269
  435.5 8.5 %all-to-all-done.10 = f32[128,1,36]{2,1,0:T(1,128)S(1)} async-done(((f32[128,1,36]{2,1,0:T(1,128)}), f32[128,1,36]{2,1,0:T(1,128)S(1)}, u32[]{:S(2)}, u32[]{:S(2)}) %all-to-all-start.10) | async-done | bytes 18464 | tf_op jit(solution)/shard_map/all_to_all | solution.py:271
  468.6 36.2 %all-to-all-done.8 = f32[128,4,1536]{2,1,0:T(4,128)} async-done(((f32[128,4,1536]{2,1,0:T(4,128)}), f32[128,4,1536]{2,1,0:T(4,128)}, u32[]{:S(2)}, u32[]{:S(2)}) %all-to-all-start.8) | async-done | bytes 3145760 | tf_op jit(solution)/shard_map/all_to_all | solution.py:280
  (261 shorter events, 170.5 us)
Async XLA Ops:
  3.6 5.3 %collective-permute-start = (bf16[2,1536]{1,0:T(2,128)(2,1)S(1)}, bf16[2,1536]{1,0:T(2,128)(2,1)S(1)}, u32[]{:S(2)}, u32[]{:S(2)}) collective-permute-start(bf16[2,1536]{1,0:T(2,128)(2,1)S(1)} %slice.415), channel_id=1, source_target_pairs={{0,1},{1,2},{2,3},{3,4},{4,5},{5,6},{6,7},{7,8},{8,9},{9,10},{10,1... | collective-permute-start | bytes 18440 | tf_op jit(solution)/shard_map/ppermute | solution.py:15
  12.0 22.5 %all-to-all-start = ((bf16[32,8,2048]{2,1,0:T(8,128)(2,1)}), bf16[32,8,2048]{2,1,0:T(8,128)(2,1)S(1)}, u32[]{:S(2)}, u32[]{:S(2)}) async-start(bf16[32,8,2048]{2,1,0:T(8,128)(2,1)} %pad_maximum_fusion.3), calls=%async_computation | async-start | bytes 2097152 | tf_op jit(solution)/shard_map/all_to_all | solution.py:104
  40.4 33.7 %all-to-all-start.1 = ((bf16[2,32,8,2048]{3,2,0,1:T(8,128)(2,1)}), bf16[2,32,8,2048]{3,2,0,1:T(8,128)(2,1)}, u32[]{:S(2)}, u32[]{:S(2)}) async-start(bf16[2,32,8,2048]{3,2,0,1:T(8,128)(2,1)} %copy.174), calls=%async_computation.1 | async-start | bytes 4194304 | tf_op jit(solution)/shard_map/all_to_all | solution.py:124
  47.6 42.8 %copy-start.56 = (f32[1,2,2,2]{1,2,3,0:T(2,128)}, f32[1,2,2,2]{1,2,3,0:T(2,128)S(1)}, u32[]{:S(2)}) copy-start(f32[1,2,2,2]{1,2,3,0:T(2,128)S(1)} %copy.181) | copy-start | bytes 100
  47.7 42.7 %copy-start.58 = (f32[1,2,2,2]{1,2,3,0:T(2,128)}, f32[1,2,2,2]{1,2,3,0:T(2,128)S(1)}, u32[]{:S(2)}) copy-start(f32[1,2,2,2]{1,2,3,0:T(2,128)S(1)} %copy.182) | copy-start | bytes 100
  47.7 92.7 %copy-start.45 = (f32[2,128]{1,0:T(2,128)}, f32[2,128]{1,0:T(2,128)S(1)}, u32[]{:S(2)}) copy-start(f32[2,128]{1,0:T(2,128)S(1)} %get-tuple-element.141) | copy-start | bytes 3076
  47.7 92.7 %copy-start.48 = (f32[2,128]{1,0:T(2,128)}, f32[2,128]{1,0:T(2,128)S(1)}, u32[]{:S(2)}) copy-start(f32[2,128]{1,0:T(2,128)S(1)} %get-tuple-element.140) | copy-start | bytes 3076
  47.8 62.4 %copy-start.21 = (f32[2,128]{0,1:T(8,128)}, f32[2,128]{0,1:T(8,128)S(1)}, u32[]{:S(2)}) copy-start(f32[2,128]{0,1:T(8,128)S(1)} %copy.183) | copy-start | bytes 3076
  48.1 102.5 %copy-start.43 = (f32[1,2,2,2]{1,2,3,0:T(2,128)}, f32[1,2,2,2]{1,2,3,0:T(2,128)S(1)}, u32[]{:S(2)}) copy-start(f32[1,2,2,2]{1,2,3,0:T(2,128)S(1)} %copy.188) | copy-start | bytes 100
  48.2 102.4 %copy-start.44 = (f32[1,2,2,2]{1,2,3,0:T(2,128)}, f32[1,2,2,2]{1,2,3,0:T(2,128)S(1)}, u32[]{:S(2)}) copy-start(f32[1,2,2,2]{1,2,3,0:T(2,128)S(1)} %copy.189) | copy-start | bytes 100
  48.5 27.1 %copy-start.49 = (f32[256]{0:T(256)}, f32[256]{0:T(256)S(1)}, u32[]{:S(2)}) copy-start(f32[256]{0:T(256)S(1)} %get-tuple-element.136) | copy-start | bytes 3076
  48.5 27.1 %copy-start.50 = (f32[256]{0:T(256)}, f32[256]{0:T(256)S(1)}, u32[]{:S(2)}) copy-start(f32[256]{0:T(256)S(1)} %get-tuple-element.137) | copy-start | bytes 3076
  49.1 71.1 %copy-start.14 = (f32[1,2,128,128]{3,2,1,0:T(8,128)}, f32[1,2,128,128]{3,2,1,0:T(8,128)S(1)}, u32[]{:S(2)}) copy-start(f32[1,2,128,128]{3,2,1,0:T(8,128)S(1)} %get-tuple-element.117) | copy-start | bytes 393220
  49.1 71.1 %copy-start.16 = (f32[1,2,128,128]{3,2,1,0:T(8,128)}, f32[1,2,128,128]{3,2,1,0:T(8,128)S(1)}, u32[]{:S(2)}) copy-start(f32[1,2,128,128]{3,2,1,0:T(8,128)S(1)} %get-tuple-element.120) | copy-start | bytes 393220
  49.1 87.2 %copy-start.12 = (f32[1,2,128,128]{3,2,1,0:T(8,128)}, f32[1,2,128,128]{3,2,1,0:T(8,128)S(1)}, u32[]{:S(2)}) copy-start(f32[1,2,128,128]{3,2,1,0:T(8,128)S(1)} %get-tuple-element.121) | copy-start | bytes 393220
  49.3 115.6 %copy-start.39 = (f32[2,256]{1,0:T(2,128)}, f32[2,256]{1,0:T(2,128)S(1)}, u32[]{:S(2)}) copy-start(f32[2,256]{1,0:T(2,128)S(1)} %get-tuple-element.130) | copy-start | bytes 6148
  49.3 115.6 %copy-start.41 = (f32[2,256]{1,0:T(2,128)}, f32[2,256]{1,0:T(2,128)S(1)}, u32[]{:S(2)}) copy-start(f32[2,256]{1,0:T(2,128)S(1)} %get-tuple-element.131) | copy-start | bytes 6148
  167.8 20.4 %all-to-all-start.2 = ((bf16[2,1,256,1024]{3,0,1,2:T(2,128)(2,1)}), bf16[2,1,256,1024]{3,0,1,2:T(2,128)(2,1)S(1)}, u32[]{:S(2)}, u32[]{:S(2)}) async-start(bf16[2,1,256,1024]{3,0,1,2:T(2,128)(2,1)} %copy.193), calls=%async_computation.2 | async-start | bytes 2097152 | tf_op jit(solution)/shard_map/all_to_all | solution.py:153
  224.3 19.5 %all-to-all-start.5 = ((bf16[2,32,8,1024]{3,2,0,1:T(8,128)(2,1)}), bf16[2,32,8,1024]{3,2,0,1:T(8,128)(2,1)S(1)}, u32[]{:S(2)}, u32[]{:S(2)}) async-start(bf16[2,32,8,1024]{3,2,0,1:T(8,128)(2,1)} %copy.198), calls=%async_computation.5 | async-start | bytes 2097152 | tf_op jit(solution)/shard_map/all_to_all | solution.py:124
  407.9 19.6 %all-to-all-start.9 = ((f32[128,1,36]{2,1,0:T(1,128)}), f32[128,1,36]{2,1,0:T(1,128)S(1)}, u32[]{:S(2)}, u32[]{:S(2)}) async-start(f32[128,1,36]{2,1,0:T(1,128)} %bitcast.102), calls=%async_computation.9 | async-start | bytes 131072 | tf_op jit(solution)/shard_map/all_to_all | solution.py:269
  418.8 15.5 %collective-permute-start.1 = (bf16[2,1536]{1,0:T(2,128)(2,1)S(1)}, bf16[2,1536]{1,0:T(2,128)(2,1)S(1)}, u32[]{:S(2)}, u32[]{:S(2)}) collective-permute-start(bf16[2,1536]{1,0:T(2,128)(2,1)S(1)} %slice.462), channel_id=1, source_target_pairs={{1,0},{2,1},{3,2},{4,3},{5,4},{6,5},{7,6},{8,7},{9,8},{10,9},{11,1... | collective-permute-start | bytes 18440 | tf_op jit(solution)/shard_map/ppermute | solution.py:15
  428.3 15.8 %all-to-all-start.10 = ((f32[128,1,36]{2,1,0:T(1,128)}), f32[128,1,36]{2,1,0:T(1,128)S(1)}, u32[]{:S(2)}, u32[]{:S(2)}) async-start(f32[128,1,36]{2,1,0:T(1,128)} %broadcast_in_dim.24), calls=%async_computation.10 | async-start | bytes 131072 | tf_op jit(solution)/shard_map/all_to_all | solution.py:271
  444.0 14.3 %all-to-all-start.11 = ((bf16[4,2,256,128]{3,1,2,0:T(2,128)(2,1)}), bf16[4,2,256,128]{3,1,2,0:T(2,128)(2,1)}, u32[]{:S(2)}, u32[]{:S(2)}) async-start(bf16[4,2,256,128]{3,1,2,0:T(2,128)(2,1)} %bitcast.271), calls=%async_computation.11 | async-start | bytes 1048576 | tf_op jit(solution)/shard_map/all_to_all | solution.py:234
  458.4 46.4 %all-to-all-start.8 = ((f32[128,4,1536]{2,1,0:T(4,128)}), f32[128,4,1536]{2,1,0:T(4,128)}, u32[]{:S(2)}, u32[]{:S(2)}) async-start(f32[128,4,1536]{2,1,0:T(4,128)} %reshape.820), calls=%async_computation.8 | async-start | bytes 6291456 | tf_op jit(solution)/shard_map/all_to_all | solution.py:280
  (48 other events, 427.3 us)

commit v4 on v3

--- a/solution.py
+++ b/solution.py
@@ -236,24 +236,54 @@
         jnp.sum(tap_parts.astype(jnp.float32), axis=0).transpose(1, 0, 2) * grad_scale
     )
     middle = (grad_first.astype(jnp.float32) * conv_one.astype(jnp.float32)).astype(jnp.bfloat16)
-    layer_out = (gate_two * conv_two.astype(jnp.float32)).astype(jnp.bfloat16)
-    grad_mixed = jnp.concatenate(
-        [
-            grad_value.astype(jnp.float32),
-            middle.astype(jnp.float32),
-            upstream * conv_two.astype(jnp.float32),
-        ],
-        axis=1,
-    ).astype(jnp.bfloat16)
-    after_rows = passed_along(grad_mixed[:margin_rows], "seq", -1)
-    grad_mixed_f = grad_mixed.astype(jnp.float32)
-    grad_pad = jnp.concatenate([grad_mixed, after_rows], axis=0).astype(jnp.float32)
-    grad_rows = sum(
+    all_devices = data_devices * seq_devices
+    row_block = signal.shape[1] // all_devices
+
+    def short_rows(block):
+        after_rows = passed_along(block[:margin_rows], "seq", -1)
+        padded = jnp.concatenate([block, after_rows], axis=0).astype(jnp.float32)
+        return padded
+
+    def taps_slice(tap_index, lo, hi):
+        return conv_taps[tap_index][None, lo:hi]
+
+    middle_pad = short_rows(middle)
+    middle_rows_grad = sum(
         (
-            conv_taps[tap_index][None, :] * grad_pad[tap_index : tap_index + frames]
+            taps_slice(tap_index, channels, 2 * channels)
+            * middle_pad[tap_index : tap_index + frames]
             for tap_index in range(tap_count)
         )
     ).astype(jnp.bfloat16)
+    middle_terms = jnp.einsum(
+        "tc,tj->cj", signal, middle_rows_grad, preferred_element_type=jnp.float32
+    )
+    middle_parts = lax.all_to_all(
+        middle_terms.reshape(all_devices, row_block, channels),
+        ("dp", "seq"),
+        split_axis=0,
+        concat_axis=0,
+        tiled=True,
+    )
+    layer_out = (gate_two * conv_two.astype(jnp.float32)).astype(jnp.bfloat16)
+    outer_mixed = jnp.concatenate(
+        [grad_value.astype(jnp.float32), upstream * conv_two.astype(jnp.float32)], axis=1
+    ).astype(jnp.bfloat16)
+    grad_mixed = jnp.concatenate(
+        [outer_mixed[:, :channels], middle, outer_mixed[:, channels:]], axis=1
+    )
+    outer_pad = short_rows(outer_mixed)
+    outer_taps = jnp.concatenate([conv_taps[:, :channels], conv_taps[:, 2 * channels :]], axis=1)
+    outer_rows = sum(
+        (
+            outer_taps[tap_index][None, :] * outer_pad[tap_index : tap_index + frames]
+            for tap_index in range(tap_count)
+        )
+    ).astype(jnp.bfloat16)
+    grad_rows = jnp.concatenate(
+        [outer_rows[:, :channels], middle_rows_grad, outer_rows[:, channels:]], axis=1
+    )
+    grad_mixed_f = grad_mixed.astype(jnp.float32)
     taps_terms = jnp.stack(
         [
             jnp.sum(
@@ -263,11 +293,23 @@
             for tap_index in range(tap_count)
         ]
     )
-    all_devices = data_devices * seq_devices
     taps_flat = taps_terms.reshape(all_devices, -1)
-    taps_share = jnp.sum(
-        lax.all_to_all(taps_flat, ("dp", "seq"), split_axis=0, concat_axis=0, tiled=True), axis=0
-    )
+    lane = 128
+    outer_terms = jnp.einsum("tc,tj->cj", signal, outer_rows, preferred_element_type=jnp.float32)
+    outer_flat = outer_terms.reshape(all_devices, row_block * 2 * channels // lane, lane)
+    taps_row = jnp.pad(taps_flat, ((0, 0), (0, lane - taps_flat.shape[1])))[:, None, :]
+    outer_parts = jnp.sum(
+        lax.all_to_all(
+            jnp.concatenate([outer_flat, taps_row], axis=1),
+            ("dp", "seq"),
+            split_axis=0,
+            concat_axis=0,
+            tiled=True,
+        ),
+        axis=0,
+    )
+    taps_share = outer_parts[-1, : taps_flat.shape[1]]
+    outer_sum = outer_parts[:-1].reshape(row_block, 2 * channels)
     taps_whole = lax.all_to_all(
         jnp.broadcast_to(taps_share[None], taps_flat.shape),
         ("dp", "seq"),
@@ -276,15 +318,13 @@
         tiled=True,
     )
     grad_taps = taps_whole.reshape(taps_terms.shape) * grad_scale
-    proj_terms = jnp.einsum("tc,tj->cj", signal, grad_rows, preferred_element_type=jnp.float32)
-    proj_parts = lax.all_to_all(
-        proj_terms.reshape(all_devices, proj_terms.shape[0] // all_devices, proj_terms.shape[1]),
-        ("dp", "seq"),
-        split_axis=0,
-        concat_axis=0,
-        tiled=True,
-    )
-    grad_proj = jnp.sum(proj_parts, axis=0) * grad_scale
+    grad_proj = (
+        jnp.concatenate(
+            [outer_sum[:, :channels], jnp.sum(middle_parts, axis=0), outer_sum[:, channels:]],
+            axis=1,
+        )
+        * grad_scale
+    )
     grad_in = jnp.einsum(
         "tj,dj->td", grad_rows, proj_weight, preferred_element_type=jnp.float32
     ).astype(jnp.bfloat16)

time: 516 us -> 518 us (level)
  blocking collectives: 82.3 us -> 61.8 us
  waiting for transfers between devices: 108 us -> 121 us
  starting transfers between devices: 58.2 us -> 67.9 us
    all_to_all x2 -> x1, blocking collectives: 36.1 us -> 15.5 us  [inverse_transform(): lax.all_to_all(values.astype(jnp.bfloat16), 'seq', split_axis=0, concat_a...]
    all_to_all x2 -> x3, starting transfers between devices: 15.2 us -> 24.4 us  [the longest x1 11.5 us: shards(): lax.all_to_all(middle_terms.reshape(all_devices, row_block, channels), ('...]
    all_to_all x2 -> x3, waiting for transfers between devices: 41.9 us -> 46.3 us  [the longest x1 30.9 us: shards(): lax.all_to_all(jnp.concatenate([outer_flat, taps_row], axis=1), ('dp', 's...]
  transfers between devices with their start and end apart: 10 -> 12, of which waited for: 8 -> 10; matrix products, arithmetic and copies ran while one was open for 6% -> 7% of each run, Pallas kernels for 0% -> 0%
where the time goes in v4:
time: 518 us; the launch traced here: 511 us
  waiting for transfers between devices  121 us (23%)
  matrix products  100 us (19%)
  local copies, waits for them, and re-layouts  91.5 us (18%)
  starting transfers between devices  67.9 us (13%)
  other arithmetic  66.3 us (13%)
  blocking collectives  61.8 us (12%)
    dot_general x8, matrix products, dft_pair(): jnp.einsum('yz' + table_part + ',z' + data_part + '->y' + result_side, bl...  87.7 us
    all_to_all x2, waiting for transfers between devices, forward_transform(): lax.all_to_all(stacked, 'seq', split_axis=1, concat_axis=2, tiled=True)  38.8 us
    all_to_all x1, blocking collectives, inverse_transform(): lax.all_to_all(packed[:, None], 'seq', split_axis=2, concat_axis=1, tiled...  31.7 us
    all_to_all x1, waiting for transfers between devices, shards(): lax.all_to_all(jnp.concatenate([outer_flat, taps_row], axis=1), ('dp', 's...  30.9 us
    dot_general x2, local copies, waits for them, and re-layouts, dft_pair(): jnp.einsum('yz' + table_part + ',z' + data_part + '->y' + result_side, bl...  21 us
    slice x4, local copies, waits for them, and re-layouts, rotate_stacked(): stacked[0] * cosine_table - direction * stacked[1] * sine_table  16.5 us
    all_to_all x1, blocking collectives, inverse_transform(): lax.all_to_all(values.astype(jnp.bfloat16), 'seq', split_axis=0, concat_a...  15.5 us
    sub x4, other arithmetic, rotate_stacked(): stacked[0] * cosine_table - direction * stacked[1] * sine_table  15.1 us
  transfers between devices with their start and end apart: 12, of which 10 were waited for; matrix products, arithmetic and copies ran while one was open for 7% of the time, Pallas kernels for 0%

profile of v4, /device:TPU:1, one launch (start us, length us, event | category | flops | bytes accessed | tf_op | source)
XLA Modules:
  0.0 510.8 jit_solution(11382146019746302573)
XLA Ops:
  11.0 8.8 %all-to-all-start = ((bf16[32,8,2048]{2,1,0:T(8,128)(2,1)}), bf16[32,8,2048]{2,1,0:T(8,128)(2,1)S(1)}, u32[]{:S(2)}, u32[]{:S(2)}) async-start(bf16[32,8,2048]{2,1,0:T(8,128)(2,1)} %pad_maximum_fusion.4), calls=%async_computation | async-start | bytes 2097152 | tf_op jit(solution)/shard_map/all_to_all | solution.py:104
  20.2 13.9 %all-to-all-done = bf16[32,8,2048]{2,1,0:T(8,128)(2,1)S(1)} async-done(((bf16[32,8,2048]{2,1,0:T(8,128)(2,1)}), bf16[32,8,2048]{2,1,0:T(8,128)(2,1)S(1)}, u32[]{:S(2)}, u32[]{:S(2)}) %all-to-all-start) | async-done | bytes 1048608 | tf_op jit(solution)/shard_map/all_to_all | solution.py:104
  40.0 7.0 %all-to-all-start.1 = ((bf16[2,32,8,2048]{3,2,0,1:T(8,128)(2,1)}), bf16[2,32,8,2048]{3,2,0,1:T(8,128)(2,1)}, u32[]{:S(2)}, u32[]{:S(2)}) async-start(bf16[2,32,8,2048]{3,2,0,1:T(8,128)(2,1)} %copy.175), calls=%async_computation.1 | async-start | bytes 4194304 | tf_op jit(solution)/shard_map/all_to_all | solution.py:124
  49.0 24.8 %all-to-all-done.1 = bf16[2,32,8,2048]{3,2,0,1:T(8,128)(2,1)} async-done(((bf16[2,32,8,2048]{3,2,0,1:T(8,128)(2,1)}), bf16[2,32,8,2048]{3,2,0,1:T(8,128)(2,1)}, u32[]{:S(2)}, u32[]{:S(2)}) %all-to-all-start.1) | async-done | bytes 2097184 | tf_op jit(solution)/shard_map/all_to_all | solution.py:124
  90.0 19.8 %fusion.7 = f32[2,2,2,128,2048]{4,2,0,3,1:T(2,128)S(1)} fusion(f32[2,1,2,128,2048]{4,0,2,3,1:T(2,128)S(1)} %maximum_select_fusion, f32[2,1,2,128,2048]{4,0,2,3,1:T(2,128)S(1)} %select_select_fusion, f32[1,2,2,2]{1,2,3,0:T(2,128)S(1)} %copy.183, f32[1,2,2,2]{1,2,3,0:T(2,128)S(1)} %copy.182), kind=kOutput, calls=%fused_computation.12 | convolution fusion | flops 52428816 | bytes 16777280 | tf_op jit(solution)/shard_map/yzga,zkabw->ykgbw/dot_general | solution.py:44
  119.9 11.2 %fusion.8 = f32[2,2,2,128,2048]{4,3,0,2,1:T(8,128)S(1)} fusion(f32[2,2,2,128,2048,1]{4,2,0,3,1,5:T(2,128)S(1)} %maximum_bitcast_fusion.1, f32[1,2,128,128]{3,2,1,0:T(8,128)S(1)} %get-tuple-element.119, f32[1,2,128,128]{3,2,1,0:T(8,128)S(1)} %get-tuple-element.122), kind=kOutput, calls=%fused_computation.14 | convolution fusion | flops 3221291008 | bytes 17039360 | tf_op jit(solution)/shard_map/yzfb,zkgbw->ykgfw/dot_general | solution.py:44
  142.9 7.4 %copy.231 = f32[2,2,2,128,1024,1]{4,0,2,5,3,1:T(2,128)} copy(f32[2,2,2,128,1024,1]{3,4,0,2,1,5:T(8,128)} %maximum_bitcast_fusion.9) | data formatting | bytes 8388608 | tf_op jit(solution)/shard_map/stack | solution.py:29
  150.3 11.3 %fusion.21 = f32[2,2,2,128,1024]{4,2,0,3,1:T(2,128)S(1)} fusion(f32[2,2,2,128,1024,1]{4,0,2,5,3,1:T(2,128)} %copy.231, f32[1,2,2,2]{1,2,3,0:T(2,128)S(1)} %copy.190, f32[1,2,2,2]{1,2,3,0:T(2,128)S(1)} %copy.189), kind=kOutput, calls=%fused_computation.33 | convolution fusion | flops 26214416 | bytes 8388672 | tf_op jit(solution)/shard_map/yzag,zkgbw->ykabw/dot_general | solution.py:44
  180.4 7.4 %all-to-all-done.2 = bf16[2,1,256,1024]{3,0,1,2:T(2,128)(2,1)S(1)} async-done(((bf16[2,1,256,1024]{3,0,1,2:T(2,128)(2,1)}), bf16[2,1,256,1024]{3,0,1,2:T(2,128)(2,1)S(1)}, u32[]{:S(2)}, u32[]{:S(2)}) %all-to-all-start.2) | async-done | bytes 1048608 | tf_op jit(solution)/shard_map/all_to_all | solution.py:153
  189.8 15.5 %all_to_all.91 = bf16[32,8,1024]{2,1,0:T(8,128)(2,1)S(1)} all-to-all(bf16[32,8,1024]{2,1,0:T(8,128)(2,1)S(1)} %copy.197), channel_id=1, replica_groups=mesh['dp'=4,'seq'=32] {'seq'}, dimensions={0} | all-to-all | bytes 1048576 | tf_op jit(solution)/shard_map/all_to_all | solution.py:162
  205.6 14.5 %all_to_all.92 = bf16[32,8,1024]{2,1,0:T(8,128)(2,1)S(1)} all-to-all(bf16[32,8,1024]{2,1,0:T(8,128)(2,1)S(1)} %maximum_bitcast_fusion.18), channel_id=1, replica_groups=mesh['dp'=4,'seq'=32] {'seq'}, dimensions={0} | all-to-all | bytes 1048576 | tf_op jit(solution)/shard_map/all_to_all | solution.py:104
  228.9 14.0 %all-to-all-done.5 = bf16[2,32,8,1024]{3,2,0,1:T(8,128)(2,1)S(1)} async-done(((bf16[2,32,8,1024]{3,2,0,1:T(8,128)(2,1)}), bf16[2,32,8,1024]{3,2,0,1:T(8,128)(2,1)S(1)}, u32[]{:S(2)}, u32[]{:S(2)}) %all-to-all-start.5) | async-done | bytes 1048608 | tf_op jit(solution)/shard_map/all_to_all | solution.py:124
  250.2 9.6 %fusion.25 = f32[2,128,1024,2,2]{2,4,3,1,0:T(2,128)} fusion(f32[2,1,2,128,1024]{4,0,2,3,1:T(2,128)S(1)} %maximum_select_fusion.1, f32[2,1,2,128,1024]{4,0,2,3,1:T(2,128)S(1)} %select_select_fusion.1, f32[1,2,2,2]{1,2,3,0:T(2,128)S(1)} %copy-done.55, f32[1,2,2,2]{1,2,3,0:T(2,128)S(1)} %copy-done.53), kind=kOutput, calls=%fused_computation.41 | convolution fusion | flops 26214416 | bytes 8388672 | tf_op jit(solution)/shard_map/yzga,zkabw->ykgbw/dot_general | solution.py:44
  259.8 7.6 %copy.206 = f32[2,128,1024,2,2]{1,2,3,4,0:T(8,128)} copy(f32[2,128,1024,2,2]{2,4,3,1,0:T(2,128)} %fusion.25) | data formatting | bytes 8388608 | tf_op jit(solution)/shard_map/yzga,zkabw->ykgbw/dot_general | solution.py:44
  276.3 8.9 %fusion.11 = f32[2,2,2048,2,128]{4,2,3,1,0:T(8,128)} fusion(f32[2,2,2,128,2048,1]{4,3,2,1,0,5:T(8,128)S(1)} %bitcast.268, f32[1,2,128,128]{3,2,1,0:T(8,128)S(1)} %copy-done.11, f32[1,2,128,128]{3,2,1,0:T(8,128)S(1)} %get-tuple-element.118), kind=kOutput, calls=%fused_computation.15 | convolution fusion | flops 3221291008 | bytes 17039360 | tf_op jit(solution)/shard_map/yzbf,zkgfw->ykgbw/dot_general | solution.py:44
  285.2 13.3 %copy.210 = f32[2,2,2048,2,128]{2,1,3,4,0:T(2,128)} copy(f32[2,2,2048,2,128]{4,2,3,1,0:T(8,128)} %fusion.11) | data formatting | bytes 16777216 | tf_op jit(solution)/shard_map/yzbf,zkgfw->ykgbw/dot_general | solution.py:44
  298.5 7.1 %multiply_subtract_fusion = (f32[1,2,2,128,2048]{4,2,0,3,1:T(2,128)S(1)}, f32[1,2,2,128,2048]{4,2,0,3,1:T(2,128)S(1)}) fusion(f32[2,2,2,128,2048]{4,2,0,3,1:T(2,128)} %bitcast.269, f32[2,128]{0,1:T(8,128)S(1)} %copy.211, f32[2,128]{0,1:T(8,128)S(1)} %copy-done.20), kind=kLoop, calls=%fused_computation.37 | loop fusion | flops 6291456 | bytes 16779264 | tf_op jit(solution)/shard_map/sub | solution.py:31
  305.6 21.0 %fusion = f32[2,2,2,128,2048]{4,2,0,3,1:T(2,128)} fusion(f32[2,2,2,2,1,1]{3,2,1,0,5,4:T(2,128)S(1)} %copy.242, f32[1,2,2,128,2048]{4,2,0,3,1:T(2,128)S(1)} %get-tuple-element.80, f32[1,2,2,128,2048]{4,2,0,3,1:T(2,128)S(1)} %get-tuple-element.79), kind=kOutput, calls=%fused_computation.5 | convolution fusion | flops 54525952 | bytes 16777280 | tf_op jit(solution)/shard_map/yzag,zkgbw->ykabw/dot_general | solution.py:44
  326.6 9.6 %fusion.150 = (f32[1,2,2,128,2048]{4,2,0,3,1:T(2,128)}, f32[1,2,2,128,2048]{4,2,0,3,1:T(2,128)S(1)}) fusion(f32[2,2,2,128,2048]{4,2,0,3,1:T(2,128)} %fusion), kind=kLoop, calls=%fused_computation.296 | loop fusion | bytes 16777216 | tf_op jit(solution)/shard_map/slice | solution.py:31
  348.4 31.7 %all_to_all.93 = bf16[2,1,256,2048]{3,0,1,2:T(2,128)(2,1)S(1)} all-to-all(bf16[2,1,256,2048]{3,0,1,2:T(2,128)(2,1)S(1)} %copy.215), channel_id=1, replica_groups=mesh['dp'=4,'seq'=32] {'seq'}, dimensions={2} | all-to-all | bytes 4194304 | tf_op jit(solution)/shard_map/all_to_all | solution.py:153
  405.2 11.5 %all-to-all-start.9 = ((f32[128,4,512]{2,1,0:T(4,128)}), f32[128,4,512]{2,1,0:T(4,128)}, u32[]{:S(2)}, u32[]{:S(2)}) async-start(f32[128,4,512]{2,1,0:T(4,128)} %reshape.834), calls=%async_computation.9 | async-start | bytes 2097152 | tf_op jit(solution)/shard_map/all_to_all | solution.py:261
  425.9 9.5 %all-to-all-done.9 = f32[128,4,512]{2,1,0:T(4,128)} async-done(((f32[128,4,512]{2,1,0:T(4,128)}), f32[128,4,512]{2,1,0:T(4,128)}, u32[]{:S(2)}, u32[]{:S(2)}) %all-to-all-start.9) | async-done | bytes 1048608 | tf_op jit(solution)/shard_map/all_to_all | solution.py:261
  461.3 30.9 %all-to-all-done.8 = f32[128,33,128]{2,1,0:T(8,128)} async-done(((f32[128,33,128]{2,1,0:T(8,128)}), f32[128,33,128]{2,1,0:T(8,128)}, u32[]{:S(2)}, u32[]{:S(2)}) %all-to-all-start.8) | async-done | bytes 2162720 | tf_op jit(solution)/shard_map/all_to_all | solution.py:302
  500.4 9.2 %all-to-all-done.10 = f32[128,1,36]{2,1,0:T(1,128)S(1)} async-done(((f32[128,1,36]{2,1,0:T(1,128)}), f32[128,1,36]{2,1,0:T(1,128)S(1)}, u32[]{:S(2)}, u32[]{:S(2)}) %all-to-all-start.10) | async-done | bytes 18464 | tf_op jit(solution)/shard_map/all_to_all | solution.py:313
  (271 shorter events, 182.8 us)
Async XLA Ops:
  3.6 4.8 collective-permute-start
  9.8 195.6 %copy-start.4 = (bf16[256,1536]{1,0:T(8,128)(2,1)}, bf16[256,1536]{1,0:T(8,128)(2,1)S(1)}, u32[]{:S(2)}) copy-start(bf16[256,1536]{1,0:T(8,128)(2,1)S(1)} %add_convert_fusion.1) | copy-start | bytes 2359300
  11.0 23.1 %all-to-all-start = ((bf16[32,8,2048]{2,1,0:T(8,128)(2,1)}), bf16[32,8,2048]{2,1,0:T(8,128)(2,1)S(1)}, u32[]{:S(2)}, u32[]{:S(2)}) async-start(bf16[32,8,2048]{2,1,0:T(8,128)(2,1)} %pad_maximum_fusion.4), calls=%async_computation | async-start | bytes 2097152 | tf_op jit(solution)/shard_map/all_to_all | solution.py:104
  40.0 33.8 %all-to-all-start.1 = ((bf16[2,32,8,2048]{3,2,0,1:T(8,128)(2,1)}), bf16[2,32,8,2048]{3,2,0,1:T(8,128)(2,1)}, u32[]{:S(2)}, u32[]{:S(2)}) async-start(bf16[2,32,8,2048]{3,2,0,1:T(8,128)(2,1)} %copy.175), calls=%async_computation.1 | async-start | bytes 4194304 | tf_op jit(solution)/shard_map/all_to_all | solution.py:124
  47.4 92.7 %copy-start.40 = (f32[2,128]{1,0:T(2,128)}, f32[2,128]{1,0:T(2,128)S(1)}, u32[]{:S(2)}) copy-start(f32[2,128]{1,0:T(2,128)S(1)} %get-tuple-element.153) | copy-start | bytes 3076
  47.4 92.7 %copy-start.42 = (f32[2,128]{1,0:T(2,128)}, f32[2,128]{1,0:T(2,128)S(1)}, u32[]{:S(2)}) copy-start(f32[2,128]{1,0:T(2,128)S(1)} %get-tuple-element.152) | copy-start | bytes 3076
  47.5 62.4 %copy-start.19 = (f32[2,128]{0,1:T(8,128)}, f32[2,128]{0,1:T(8,128)S(1)}, u32[]{:S(2)}) copy-start(f32[2,128]{0,1:T(8,128)S(1)} %copy.184) | copy-start | bytes 3076
  47.8 102.5 %copy-start.36 = (f32[1,2,2,2]{1,2,3,0:T(2,128)}, f32[1,2,2,2]{1,2,3,0:T(2,128)S(1)}, u32[]{:S(2)}) copy-start(f32[1,2,2,2]{1,2,3,0:T(2,128)S(1)} %copy.189) | copy-start | bytes 100
  47.9 102.4 %copy-start.38 = (f32[1,2,2,2]{1,2,3,0:T(2,128)}, f32[1,2,2,2]{1,2,3,0:T(2,128)S(1)}, u32[]{:S(2)}) copy-start(f32[1,2,2,2]{1,2,3,0:T(2,128)S(1)} %copy.190) | copy-start | bytes 100
  48.8 71.1 %copy-start.12 = (f32[1,2,128,128]{3,2,1,0:T(8,128)}, f32[1,2,128,128]{3,2,1,0:T(8,128)S(1)}, u32[]{:S(2)}) copy-start(f32[1,2,128,128]{3,2,1,0:T(8,128)S(1)} %get-tuple-element.119) | copy-start | bytes 393220
  48.8 71.1 %copy-start.14 = (f32[1,2,128,128]{3,2,1,0:T(8,128)}, f32[1,2,128,128]{3,2,1,0:T(8,128)S(1)}, u32[]{:S(2)}) copy-start(f32[1,2,128,128]{3,2,1,0:T(8,128)S(1)} %get-tuple-element.122) | copy-start | bytes 393220
  48.8 87.2 %copy-start.10 = (f32[1,2,128,128]{3,2,1,0:T(8,128)}, f32[1,2,128,128]{3,2,1,0:T(8,128)S(1)}, u32[]{:S(2)}) copy-start(f32[1,2,128,128]{3,2,1,0:T(8,128)S(1)} %get-tuple-element.123) | copy-start | bytes 393220
  48.9 115.6 %copy-start.32 = (f32[2,256]{1,0:T(2,128)}, f32[2,256]{1,0:T(2,128)S(1)}, u32[]{:S(2)}) copy-start(f32[2,256]{1,0:T(2,128)S(1)} %get-tuple-element.142) | copy-start | bytes 6148
  48.9 115.6 %copy-start.34 = (f32[2,256]{1,0:T(2,128)}, f32[2,256]{1,0:T(2,128)S(1)}, u32[]{:S(2)}) copy-start(f32[2,256]{1,0:T(2,128)S(1)} %get-tuple-element.143) | copy-start | bytes 6148
  167.5 20.4 %all-to-all-start.2 = ((bf16[2,1,256,1024]{3,0,1,2:T(2,128)(2,1)}), bf16[2,1,256,1024]{3,0,1,2:T(2,128)(2,1)S(1)}, u32[]{:S(2)}, u32[]{:S(2)}) async-start(bf16[2,1,256,1024]{3,0,1,2:T(2,128)(2,1)} %copy.194), calls=%async_computation.2 | async-start | bytes 2097152 | tf_op jit(solution)/shard_map/all_to_all | solution.py:153
  205.5 191.5 %copy-start.7 = (bf16[256,512]{1,0:T(8,128)(2,1)}, bf16[256,512]{1,0:T(8,128)(2,1)S(1)}, u32[]{:S(2)}) copy-start(bf16[256,512]{1,0:T(8,128)(2,1)S(1)} %get-tuple-element.117) | copy-start | bytes 786436
  223.4 19.5 %all-to-all-start.5 = ((bf16[2,32,8,1024]{3,2,0,1:T(8,128)(2,1)}), bf16[2,32,8,1024]{3,2,0,1:T(8,128)(2,1)S(1)}, u32[]{:S(2)}, u32[]{:S(2)}) async-start(bf16[2,32,8,1024]{3,2,0,1:T(8,128)(2,1)} %copy.199), calls=%async_computation.5 | async-start | bytes 2097152 | tf_op jit(solution)/shard_map/all_to_all | solution.py:124
  384.3 20.9 %all-to-all-start.7 = ((bf16[32,8,2048]{2,1,0:T(8,128)(2,1)}), bf16[32,8,2048]{2,1,0:T(8,128)(2,1)}, u32[]{:S(2)}, u32[]{:S(2)}) async-start(bf16[32,8,2048]{2,1,0:T(8,128)(2,1)} %copy.218), calls=%async_computation.7 | async-start | bytes 2097152 | tf_op jit(solution)/shard_map/all_to_all | solution.py:162
  391.0 6.1 %collective-permute-start.2 = (bf16[2,512]{1,0:T(2,128)(2,1)S(1)}, bf16[2,512]{1,0:T(2,128)(2,1)S(1)}, u32[]{:S(2)}, u32[]{:S(2)}) collective-permute-start(bf16[2,512]{1,0:T(2,128)(2,1)S(1)} %slice.552), channel_id=1, source_target_pairs={{1,0},{2,1},{3,2},{4,3},{5,4},{6,5},{7,6},{8,7},{9,8},{10,9},{11,1... | collective-permute-start | bytes 6152 | tf_op jit(solution)/shard_map/ppermute | solution.py:15
  405.2 30.2 %all-to-all-start.9 = ((f32[128,4,512]{2,1,0:T(4,128)}), f32[128,4,512]{2,1,0:T(4,128)}, u32[]{:S(2)}, u32[]{:S(2)}) async-start(f32[128,4,512]{2,1,0:T(4,128)} %reshape.834), calls=%async_computation.9 | async-start | bytes 2097152 | tf_op jit(solution)/shard_map/all_to_all | solution.py:261
  419.7 5.8 %collective-permute-start.1 = (bf16[2,1024]{1,0:T(2,128)(2,1)S(1)}, bf16[2,1024]{1,0:T(2,128)(2,1)S(1)}, u32[]{:S(2)}, u32[]{:S(2)}) collective-permute-start(bf16[2,1024]{1,0:T(2,128)(2,1)S(1)} %pad_maximum_fusion.14), channel_id=1, source_target_pairs={{1,0},{2,1},{3,2},{4,3},{5,4},{6,5},{7,6},{8,7},{9,8},{10,9},{11,1... | collective-permute-start | bytes 12296 | tf_op jit(solution)/shard_map/ppermute | solution.py:15
  435.4 15.5 %all-to-all-start.11 = ((bf16[4,2,256,128]{3,1,2,0:T(2,128)(2,1)}), bf16[4,2,256,128]{3,1,2,0:T(2,128)(2,1)S(1)}, u32[]{:S(2)}, u32[]{:S(2)}) async-start(bf16[4,2,256,128]{3,1,2,0:T(2,128)(2,1)} %bitcast.259), calls=%async_computation.11 | async-start | bytes 1048576 | tf_op jit(solution)/shard_map/all_to_all | solution.py:234
  450.9 41.3 %all-to-all-start.8 = ((f32[128,33,128]{2,1,0:T(8,128)}), f32[128,33,128]{2,1,0:T(8,128)}, u32[]{:S(2)}, u32[]{:S(2)}) async-start(f32[128,33,128]{2,1,0:T(8,128)} %pad_maximum_fusion), calls=%async_computation.8 | async-start | bytes 5242880 | tf_op jit(solution)/shard_map/all_to_all | solution.py:302
  494.9 14.8 %all-to-all-start.10 = ((f32[128,1,36]{2,1,0:T(1,128)}), f32[128,1,36]{2,1,0:T(1,128)S(1)}, u32[]{:S(2)}, u32[]{:S(2)}) async-start(f32[128,1,36]{2,1,0:T(1,128)} %broadcast_in_dim.27), calls=%async_computation.10 | async-start | bytes 131072 | tf_op jit(solution)/shard_map/all_to_all | solution.py:313
  (46 other events, 473.6 us)

commit v5 on v4

--- a/solution.py
+++ b/solution.py
@@ -211,7 +211,38 @@
     grad_first = middle_rows[:, channels:]
     first = (gate_one * conv_one.astype(jnp.float32)).astype(jnp.bfloat16)
     grad_one = (grad_first.astype(jnp.float32) * gate_one).astype(jnp.bfloat16)
+    middle = (grad_first.astype(jnp.float32) * conv_one.astype(jnp.float32)).astype(jnp.bfloat16)
+    all_devices = data_devices * seq_devices
+    row_block = signal.shape[1] // all_devices
+
+    def short_rows(block):
+        after_rows = passed_along(block[:margin_rows], "seq", -1)
+        padded = jnp.concatenate([block, after_rows], axis=0).astype(jnp.float32)
+        return padded
+
+    def taps_slice(tap_index, lo, hi):
+        return conv_taps[tap_index][None, lo:hi]
+
+    middle_pad = short_rows(middle)
+    middle_rows_grad = sum(
+        (
+            taps_slice(tap_index, channels, 2 * channels)
+            * middle_pad[tap_index : tap_index + frames]
+            for tap_index in range(tap_count)
+        )
+    ).astype(jnp.bfloat16)
+    middle_terms = jnp.einsum(
+        "tc,tj->cj", signal, middle_rows_grad, preferred_element_type=jnp.float32
+    )
+    middle_parts = lax.all_to_all(
+        middle_terms.reshape(all_devices, row_block, channels),
+        ("dp", "seq"),
+        split_axis=0,
+        concat_axis=0,
+        tiled=True,
+    )
     second = forward_transform(jnp.concatenate([first, grad_one], axis=1))
+    middle_parts, second = lax.optimization_barrier((middle_parts, second))
     first_spectra = second[..., :channels]
     one_spectra = second[..., channels:]
     closing = inverse_transform(
@@ -234,36 +265,6 @@
     tap_parts = lax.all_to_all(tap_blocks, "dp", split_axis=0, concat_axis=0, tiled=True)
     grad_filters = (
         jnp.sum(tap_parts.astype(jnp.float32), axis=0).transpose(1, 0, 2) * grad_scale
-    )
-    middle = (grad_first.astype(jnp.float32) * conv_one.astype(jnp.float32)).astype(jnp.bfloat16)
-    all_devices = data_devices * seq_devices
-    row_block = signal.shape[1] // all_devices
-
-    def short_rows(block):
-        after_rows = passed_along(block[:margin_rows], "seq", -1)
-        padded = jnp.concatenate([block, after_rows], axis=0).astype(jnp.float32)
-        return padded
-
-    def taps_slice(tap_index, lo, hi):
-        return conv_taps[tap_index][None, lo:hi]
-
-    middle_pad = short_rows(middle)
-    middle_rows_grad = sum(
-        (
-            taps_slice(tap_index, channels, 2 * channels)
-            * middle_pad[tap_index : tap_index + frames]
-            for tap_index in range(tap_count)
-        )
-    ).astype(jnp.bfloat16)
-    middle_terms = jnp.einsum(
-        "tc,tj->cj", signal, middle_rows_grad, preferred_element_type=jnp.float32
-    )
-    middle_parts = lax.all_to_all(
-        middle_terms.reshape(all_devices, row_block, channels),
-        ("dp", "seq"),
-        split_axis=0,
-        concat_axis=0,
-        tiled=True,
     )
     layer_out = (gate_two * conv_two.astype(jnp.float32)).astype(jnp.bfloat16)
     outer_mixed = jnp.concatenate(

time: 518 us -> 535 us (1.033)
  waiting for transfers between devices: 121 us -> 112 us
  starting transfers between devices: 67.9 us -> 76.4 us
  other arithmetic: 66.3 us -> 73.2 us
  local copies, waits for them, and re-layouts: 91.5 us -> 97.1 us
    all_to_all x1, waiting for transfers between devices: 9.46 us -> 0.01 us  [shards(): lax.all_to_all(middle_terms.reshape(all_devices, row_block, channels), ('...]
    all_to_all x2, waiting for transfers between devices: 38.8 us -> 30.1 us  [forward_transform(): lax.all_to_all(stacked, 'seq', split_axis=1, concat_axis=2, tiled=True)]
    all_to_all x1, waiting for transfers between devices: 5.9 us -> 14.2 us  [inverse_transform(): lax.all_to_all(values.astype(jnp.bfloat16), 'seq', split_axis=0, concat_a...]
  transfers between devices with their start and end apart: 12 -> 12, of which waited for: 10 -> 10; matrix products, arithmetic and copies ran while one was open for 7% -> 11% of each run, Pallas kernels for 0% -> 0%
where the time goes in v5:
time: 535 us; the launch traced here: 527 us
  waiting for transfers between devices  112 us (21%)
  matrix products  101 us (19%)
  local copies, waits for them, and re-layouts  97.1 us (18%)
  starting transfers between devices  76.4 us (14%)
  other arithmetic  73.2 us (14%)
  blocking collectives  64.2 us (12%)
    dot_general x8, matrix products, dft_pair(): jnp.einsum('yz' + table_part + ',z' + data_part + '->y' + result_side, bl...  87.6 us
    all_to_all x1, blocking collectives, inverse_transform(): lax.all_to_all(packed[:, None], 'seq', split_axis=2, concat_axis=1, tiled...  34.2 us
    all_to_all x1, waiting for transfers between devices, shards(): lax.all_to_all(jnp.concatenate([outer_flat, taps_row], axis=1), ('dp', 's...  31.1 us
    all_to_all x2, waiting for transfers between devices, forward_transform(): lax.all_to_all(stacked, 'seq', split_axis=1, concat_axis=2, tiled=True)  30.1 us
    dot_general x2, local copies, waits for them, and re-layouts, dft_pair(): jnp.einsum('yz' + table_part + ',z' + data_part + '->y' + result_side, bl...  21 us
    slice x4, local copies, waits for them, and re-layouts, rotate_stacked(): stacked[0] * cosine_table - direction * stacked[1] * sine_table  16.5 us
    all_to_all x1, blocking collectives, inverse_transform(): lax.all_to_all(values.astype(jnp.bfloat16), 'seq', split_axis=0, concat_a...  15.5 us
    sub x4, other arithmetic, rotate_stacked(): stacked[0] * cosine_table - direction * stacked[1] * sine_table  15 us
  transfers between devices with their start and end apart: 12, of which 10 were waited for; matrix products, arithmetic and copies ran while one was open for 11% of the time, Pallas kernels for 0%

profile of v5, /device:TPU:1, one launch (start us, length us, event | category | flops | bytes accessed | tf_op | source)
XLA Modules:
  0.0 526.8 jit_solution(9258440156218201901)
XLA Ops:
  11.0 8.8 %all-to-all-start = ((bf16[32,8,2048]{2,1,0:T(8,128)(2,1)}), bf16[32,8,2048]{2,1,0:T(8,128)(2,1)S(1)}, u32[]{:S(2)}, u32[]{:S(2)}) async-start(bf16[32,8,2048]{2,1,0:T(8,128)(2,1)} %pad_maximum_fusion.4), calls=%async_computation | async-start | bytes 2097152 | tf_op jit(solution)/shard_map/all_to_all | solution.py:104
  20.2 13.9 %all-to-all-done = bf16[32,8,2048]{2,1,0:T(8,128)(2,1)S(1)} async-done(((bf16[32,8,2048]{2,1,0:T(8,128)(2,1)}), bf16[32,8,2048]{2,1,0:T(8,128)(2,1)S(1)}, u32[]{:S(2)}, u32[]{:S(2)}) %all-to-all-start) | async-done | bytes 1048608 | tf_op jit(solution)/shard_map/all_to_all | solution.py:104
  49.2 24.5 %all-to-all-done.1 = bf16[2,32,8,2048]{3,2,0,1:T(8,128)(2,1)} async-done(((bf16[2,32,8,2048]{3,2,0,1:T(8,128)(2,1)}), bf16[2,32,8,2048]{3,2,0,1:T(8,128)(2,1)}, u32[]{:S(2)}, u32[]{:S(2)}) %all-to-all-start.1) | async-done | bytes 2097184 | tf_op jit(solution)/shard_map/all_to_all | solution.py:124
  90.0 19.7 %fusion.7 = f32[2,2,2,128,2048]{4,2,0,3,1:T(2,128)S(1)} fusion(f32[2,1,2,128,2048]{4,0,2,3,1:T(2,128)S(1)} %maximum_select_fusion, f32[2,1,2,128,2048]{4,0,2,3,1:T(2,128)S(1)} %select_select_fusion, f32[1,2,2,2]{1,2,3,0:T(2,128)S(1)} %copy.183, f32[1,2,2,2]{1,2,3,0:T(2,128)S(1)} %copy.182), kind=kOutput, calls=%fused_computation.12 | convolution fusion | flops 52428816 | bytes 16777280 | tf_op jit(solution)/shard_map/yzga,zkabw->ykgbw/dot_general | solution.py:44
  119.7 11.2 %fusion.8 = f32[2,2,2,128,2048]{4,3,0,2,1:T(8,128)S(1)} fusion(f32[2,2,2,128,2048,1]{4,2,0,3,1,5:T(2,128)S(1)} %maximum_bitcast_fusion.1, f32[1,2,128,128]{3,2,1,0:T(8,128)S(1)} %get-tuple-element.123, f32[1,2,128,128]{3,2,1,0:T(8,128)S(1)} %get-tuple-element.126), kind=kOutput, calls=%fused_computation.14 | convolution fusion | flops 3221291008 | bytes 17039360 | tf_op jit(solution)/shard_map/yzfb,zkgbw->ykgfw/dot_general | solution.py:44
  142.7 7.4 %copy.231 = f32[2,2,2,128,1024,1]{4,0,2,5,3,1:T(2,128)} copy(f32[2,2,2,128,1024,1]{3,4,0,2,1,5:T(8,128)} %maximum_bitcast_fusion.9) | data formatting | bytes 8388608 | tf_op jit(solution)/shard_map/stack | solution.py:29
  150.1 11.4 %fusion.21 = f32[2,2,2,128,1024]{4,2,0,3,1:T(2,128)S(1)} fusion(f32[2,2,2,128,1024,1]{4,0,2,5,3,1:T(2,128)} %copy.231, f32[1,2,2,2]{1,2,3,0:T(2,128)S(1)} %copy.190, f32[1,2,2,2]{1,2,3,0:T(2,128)S(1)} %copy.189), kind=kOutput, calls=%fused_computation.33 | convolution fusion | flops 26214416 | bytes 8388672 | tf_op jit(solution)/shard_map/yzag,zkgbw->ykabw/dot_general | solution.py:44
  180.2 7.4 %all-to-all-done.2 = bf16[2,1,256,1024]{3,0,1,2:T(2,128)(2,1)S(1)} async-done(((bf16[2,1,256,1024]{3,0,1,2:T(2,128)(2,1)}), bf16[2,1,256,1024]{3,0,1,2:T(2,128)(2,1)S(1)}, u32[]{:S(2)}, u32[]{:S(2)}) %all-to-all-start.2) | async-done | bytes 1048608 | tf_op jit(solution)/shard_map/all_to_all | solution.py:153
  189.6 15.5 %all_to_all.91 = bf16[32,8,1024]{2,1,0:T(8,128)(2,1)S(1)} all-to-all(bf16[32,8,1024]{2,1,0:T(8,128)(2,1)S(1)} %copy.197), channel_id=1, replica_groups=mesh['dp'=4,'seq'=32] {'seq'}, dimensions={0} | all-to-all | bytes 1048576 | tf_op jit(solution)/shard_map/all_to_all | solution.py:162
  205.4 14.5 %all_to_all.92 = bf16[32,8,1024]{2,1,0:T(8,128)(2,1)S(1)} all-to-all(bf16[32,8,1024]{2,1,0:T(8,128)(2,1)S(1)} %maximum_bitcast_fusion.18), channel_id=1, replica_groups=mesh['dp'=4,'seq'=32] {'seq'}, dimensions={0} | all-to-all | bytes 1048576 | tf_op jit(solution)/shard_map/all_to_all | solution.py:104
  242.8 13.9 %all-to-all-start.4 = ((f32[128,4,512]{2,1,0:T(4,128)}), f32[128,4,512]{2,1,0:T(4,128)}, u32[]{:S(2)}, u32[]{:S(2)}) async-start(f32[128,4,512]{2,1,0:T(4,128)} %reshape.827), calls=%async_computation.4 | async-start | bytes 2097152 | tf_op jit(solution)/shard_map/all_to_all | solution.py:237
  264.0 9.6 %fusion.25 = f32[2,128,1024,2,2]{2,4,3,1,0:T(2,128)} fusion(f32[2,1,2,128,1024]{4,0,2,3,1:T(2,128)S(1)} %maximum_select_fusion.1, f32[2,1,2,128,1024]{4,0,2,3,1:T(2,128)S(1)} %select_select_fusion.1, f32[1,2,2,2]{1,2,3,0:T(2,128)S(1)} %copy-done.56, f32[1,2,2,2]{1,2,3,0:T(2,128)S(1)} %copy-done.54), kind=kOutput, calls=%fused_computation.41 | convolution fusion | flops 26214416 | bytes 8388672 | tf_op jit(solution)/shard_map/yzga,zkabw->ykgbw/dot_general | solution.py:44
  273.7 7.6 %copy.206 = f32[2,128,1024,2,2]{1,2,3,4,0:T(8,128)} copy(f32[2,128,1024,2,2]{2,4,3,1,0:T(2,128)} %fusion.25) | data formatting | bytes 8388608 | tf_op jit(solution)/shard_map/yzga,zkabw->ykgbw/dot_general | solution.py:44
  299.0 8.9 %fusion.11 = f32[2,2,2048,2,128]{4,2,3,1,0:T(8,128)} fusion(f32[2,2,2,128,2048,1]{4,3,2,1,0,5:T(8,128)S(1)} %bitcast.266, f32[1,2,128,128]{3,2,1,0:T(8,128)S(1)} %copy-done.12, f32[1,2,128,128]{3,2,1,0:T(8,128)S(1)} %get-tuple-element.122), kind=kOutput, calls=%fused_computation.15 | convolution fusion | flops 3221291008 | bytes 17039360 | tf_op jit(solution)/shard_map/yzbf,zkgfw->ykgbw/dot_general | solution.py:44
  308.0 13.3 %copy.210 = f32[2,2,2048,2,128]{2,1,3,4,0:T(2,128)} copy(f32[2,2,2048,2,128]{4,2,3,1,0:T(8,128)} %fusion.11) | data formatting | bytes 16777216 | tf_op jit(solution)/shard_map/yzbf,zkgfw->ykgbw/dot_general | solution.py:44
  321.3 7.1 %multiply_subtract_fusion = (f32[1,2,2,128,2048]{4,2,0,3,1:T(2,128)S(1)}, f32[1,2,2,128,2048]{4,2,0,3,1:T(2,128)S(1)}) fusion(f32[2,2,2,128,2048]{4,2,0,3,1:T(2,128)} %bitcast.267, f32[2,128]{0,1:T(8,128)S(1)} %copy.211, f32[2,128]{0,1:T(8,128)S(1)} %copy-done.21), kind=kLoop, calls=%fused_computation.37 | loop fusion | flops 6291456 | bytes 16779264 | tf_op jit(solution)/shard_map/sub | solution.py:31
  328.4 21.0 %fusion = f32[2,2,2,128,2048]{4,2,0,3,1:T(2,128)} fusion(f32[2,2,2,2,1,1]{3,2,1,0,5,4:T(2,128)S(1)} %copy.242, f32[1,2,2,128,2048]{4,2,0,3,1:T(2,128)S(1)} %get-tuple-element.84, f32[1,2,2,128,2048]{4,2,0,3,1:T(2,128)S(1)} %get-tuple-element.83), kind=kOutput, calls=%fused_computation.5 | convolution fusion | flops 54525952 | bytes 16777280 | tf_op jit(solution)/shard_map/yzag,zkgbw->ykabw/dot_general | solution.py:44
  349.4 9.6 %fusion.150 = (f32[1,2,2,128,2048]{4,2,0,3,1:T(2,128)}, f32[1,2,2,128,2048]{4,2,0,3,1:T(2,128)S(1)}) fusion(f32[2,2,2,128,2048]{4,2,0,3,1:T(2,128)} %fusion), kind=kLoop, calls=%fused_computation.296 | loop fusion | bytes 16777216 | tf_op jit(solution)/shard_map/slice | solution.py:31
  371.2 34.2 %all_to_all.93 = bf16[2,1,256,2048]{3,0,1,2:T(2,128)(2,1)S(1)} all-to-all(bf16[2,1,256,2048]{3,0,1,2:T(2,128)(2,1)S(1)} %copy.215), channel_id=1, replica_groups=mesh['dp'=4,'seq'=32] {'seq'}, dimensions={2} | all-to-all | bytes 4194304 | tf_op jit(solution)/shard_map/all_to_all | solution.py:153
  415.5 14.2 %all-to-all-done.8 = bf16[32,8,2048]{2,1,0:T(8,128)(2,1)} async-done(((bf16[32,8,2048]{2,1,0:T(8,128)(2,1)}), bf16[32,8,2048]{2,1,0:T(8,128)(2,1)}, u32[]{:S(2)}, u32[]{:S(2)}) %all-to-all-start.8) | async-done | bytes 1048608 | tf_op jit(solution)/shard_map/all_to_all | solution.py:162
  438.8 7.7 %all-to-all-start.11 = ((bf16[4,2,256,128]{3,1,2,0:T(2,128)(2,1)}), bf16[4,2,256,128]{3,1,2,0:T(2,128)(2,1)S(1)}, u32[]{:S(2)}, u32[]{:S(2)}) async-start(bf16[4,2,256,128]{3,1,2,0:T(2,128)(2,1)} %bitcast.259), calls=%async_computation.11 | async-start | bytes 1048576 | tf_op jit(solution)/shard_map/all_to_all | solution.py:265
  462.9 10.0 %all-to-all-start.9 = ((f32[128,33,128]{2,1,0:T(8,128)}), f32[128,33,128]{2,1,0:T(8,128)}, u32[]{:S(2)}, u32[]{:S(2)}) async-start(f32[128,33,128]{2,1,0:T(8,128)} %pad_maximum_fusion), calls=%async_computation.9 | async-start | bytes 5242880 | tf_op jit(solution)/shard_map/all_to_all | solution.py:303
  477.1 31.1 %all-to-all-done.9 = f32[128,33,128]{2,1,0:T(8,128)} async-done(((f32[128,33,128]{2,1,0:T(8,128)}), f32[128,33,128]{2,1,0:T(8,128)}, u32[]{:S(2)}, u32[]{:S(2)}) %all-to-all-start.9) | async-done | bytes 2162720 | tf_op jit(solution)/shard_map/all_to_all | solution.py:303
  516.4 9.2 %all-to-all-done.10 = f32[128,1,36]{2,1,0:T(1,128)S(1)} async-done(((f32[128,1,36]{2,1,0:T(1,128)}), f32[128,1,36]{2,1,0:T(1,128)S(1)}, u32[]{:S(2)}, u32[]{:S(2)}) %all-to-all-start.10) | async-done | bytes 18464 | tf_op jit(solution)/shard_map/all_to_all | solution.py:314
  (268 shorter events, 192.8 us)
Async XLA Ops:
  3.6 4.8 collective-permute-start
  9.8 195.4 %copy-start.5 = (bf16[256,1536]{1,0:T(8,128)(2,1)}, bf16[256,1536]{1,0:T(8,128)(2,1)S(1)}, u32[]{:S(2)}) copy-start(bf16[256,1536]{1,0:T(8,128)(2,1)S(1)} %add_convert_fusion.1) | copy-start | bytes 2359300
  11.0 23.1 %all-to-all-start = ((bf16[32,8,2048]{2,1,0:T(8,128)(2,1)}), bf16[32,8,2048]{2,1,0:T(8,128)(2,1)S(1)}, u32[]{:S(2)}, u32[]{:S(2)}) async-start(bf16[32,8,2048]{2,1,0:T(8,128)(2,1)} %pad_maximum_fusion.4), calls=%async_computation | async-start | bytes 2097152 | tf_op jit(solution)/shard_map/all_to_all | solution.py:104
  40.0 33.7 %all-to-all-start.1 = ((bf16[2,32,8,2048]{3,2,0,1:T(8,128)(2,1)}), bf16[2,32,8,2048]{3,2,0,1:T(8,128)(2,1)}, u32[]{:S(2)}, u32[]{:S(2)}) async-start(bf16[2,32,8,2048]{3,2,0,1:T(8,128)(2,1)} %copy.175), calls=%async_computation.1 | async-start | bytes 4194304 | tf_op jit(solution)/shard_map/all_to_all | solution.py:124
  47.2 42.8 %copy-start.53 = (f32[1,2,2,2]{1,2,3,0:T(2,128)}, f32[1,2,2,2]{1,2,3,0:T(2,128)S(1)}, u32[]{:S(2)}) copy-start(f32[1,2,2,2]{1,2,3,0:T(2,128)S(1)} %copy.182) | copy-start | bytes 100
  47.3 102.8 %copy-start.37 = (f32[1,2,2,2]{1,2,3,0:T(2,128)}, f32[1,2,2,2]{1,2,3,0:T(2,128)S(1)}, u32[]{:S(2)}) copy-start(f32[1,2,2,2]{1,2,3,0:T(2,128)S(1)} %copy.190) | copy-start | bytes 100
  47.4 102.7 %copy-start.39 = (f32[1,2,2,2]{1,2,3,0:T(2,128)}, f32[1,2,2,2]{1,2,3,0:T(2,128)S(1)}, u32[]{:S(2)}) copy-start(f32[1,2,2,2]{1,2,3,0:T(2,128)S(1)} %copy.189) | copy-start | bytes 100
  47.5 92.3 %copy-start.41 = (f32[2,128]{1,0:T(2,128)}, f32[2,128]{1,0:T(2,128)S(1)}, u32[]{:S(2)}) copy-start(f32[2,128]{1,0:T(2,128)S(1)} %get-tuple-element.157) | copy-start | bytes 3076
  47.5 92.3 %copy-start.47 = (f32[2,128]{1,0:T(2,128)}, f32[2,128]{1,0:T(2,128)S(1)}, u32[]{:S(2)}) copy-start(f32[2,128]{1,0:T(2,128)S(1)} %get-tuple-element.156) | copy-start | bytes 3076
  47.7 62.0 %copy-start.20 = (f32[2,128]{0,1:T(8,128)}, f32[2,128]{0,1:T(8,128)S(1)}, u32[]{:S(2)}) copy-start(f32[2,128]{0,1:T(8,128)S(1)} %copy.184) | copy-start | bytes 3076
  49.0 70.7 %copy-start.13 = (f32[1,2,128,128]{3,2,1,0:T(8,128)}, f32[1,2,128,128]{3,2,1,0:T(8,128)S(1)}, u32[]{:S(2)}) copy-start(f32[1,2,128,128]{3,2,1,0:T(8,128)S(1)} %get-tuple-element.123) | copy-start | bytes 393220
  49.0 70.7 %copy-start.15 = (f32[1,2,128,128]{3,2,1,0:T(8,128)}, f32[1,2,128,128]{3,2,1,0:T(8,128)S(1)}, u32[]{:S(2)}) copy-start(f32[1,2,128,128]{3,2,1,0:T(8,128)S(1)} %get-tuple-element.126) | copy-start | bytes 393220
  49.0 86.8 %copy-start.11 = (f32[1,2,128,128]{3,2,1,0:T(8,128)}, f32[1,2,128,128]{3,2,1,0:T(8,128)S(1)}, u32[]{:S(2)}) copy-start(f32[1,2,128,128]{3,2,1,0:T(8,128)S(1)} %get-tuple-element.127) | copy-start | bytes 393220
  49.2 115.1 %copy-start.33 = (f32[2,256]{1,0:T(2,128)}, f32[2,256]{1,0:T(2,128)S(1)}, u32[]{:S(2)}) copy-start(f32[2,256]{1,0:T(2,128)S(1)} %get-tuple-element.146) | copy-start | bytes 6148
  49.2 115.1 %copy-start.35 = (f32[2,256]{1,0:T(2,128)}, f32[2,256]{1,0:T(2,128)S(1)}, u32[]{:S(2)}) copy-start(f32[2,256]{1,0:T(2,128)S(1)} %get-tuple-element.147) | copy-start | bytes 6148
  167.2 20.4 %all-to-all-start.2 = ((bf16[2,1,256,1024]{3,0,1,2:T(2,128)(2,1)}), bf16[2,1,256,1024]{3,0,1,2:T(2,128)(2,1)S(1)}, u32[]{:S(2)}, u32[]{:S(2)}) async-start(bf16[2,1,256,1024]{3,0,1,2:T(2,128)(2,1)} %copy.194), calls=%async_computation.2 | async-start | bytes 2097152 | tf_op jit(solution)/shard_map/all_to_all | solution.py:153
  223.1 19.7 %all-to-all-start.6 = ((bf16[2,32,8,1024]{3,2,0,1:T(8,128)(2,1)}), bf16[2,32,8,1024]{3,2,0,1:T(8,128)(2,1)S(1)}, u32[]{:S(2)}, u32[]{:S(2)}) async-start(bf16[2,32,8,1024]{3,2,0,1:T(8,128)(2,1)} %copy.199), calls=%async_computation.6 | async-start | bytes 2097152 | tf_op jit(solution)/shard_map/all_to_all | solution.py:124
  228.6 4.5 collective-permute-start.1
  242.8 45.6 %all-to-all-start.4 = ((f32[128,4,512]{2,1,0:T(4,128)}), f32[128,4,512]{2,1,0:T(4,128)}, u32[]{:S(2)}, u32[]{:S(2)}) async-start(f32[128,4,512]{2,1,0:T(4,128)} %reshape.827), calls=%async_computation.4 | async-start | bytes 2097152 | tf_op jit(solution)/shard_map/all_to_all | solution.py:237
  409.5 20.2 %all-to-all-start.8 = ((bf16[32,8,2048]{2,1,0:T(8,128)(2,1)}), bf16[32,8,2048]{2,1,0:T(8,128)(2,1)}, u32[]{:S(2)}, u32[]{:S(2)}) async-start(bf16[32,8,2048]{2,1,0:T(8,128)(2,1)} %copy.218), calls=%async_computation.8 | async-start | bytes 2097152 | tf_op jit(solution)/shard_map/all_to_all | solution.py:162
  438.8 24.1 %all-to-all-start.11 = ((bf16[4,2,256,128]{3,1,2,0:T(2,128)(2,1)}), bf16[4,2,256,128]{3,1,2,0:T(2,128)(2,1)S(1)}, u32[]{:S(2)}, u32[]{:S(2)}) async-start(bf16[4,2,256,128]{3,1,2,0:T(2,128)(2,1)} %bitcast.259), calls=%async_computation.11 | async-start | bytes 1048576 | tf_op jit(solution)/shard_map/all_to_all | solution.py:265
  446.5 4.6 collective-permute-start.2
  462.9 45.3 %all-to-all-start.9 = ((f32[128,33,128]{2,1,0:T(8,128)}), f32[128,33,128]{2,1,0:T(8,128)}, u32[]{:S(2)}, u32[]{:S(2)}) async-start(f32[128,33,128]{2,1,0:T(8,128)} %pad_maximum_fusion), calls=%async_computation.9 | async-start | bytes 5242880 | tf_op jit(solution)/shard_map/all_to_all | solution.py:303
  510.8 14.8 %all-to-all-start.10 = ((f32[128,1,36]{2,1,0:T(1,128)}), f32[128,1,36]{2,1,0:T(1,128)S(1)}, u32[]{:S(2)}, u32[]{:S(2)}) async-start(f32[128,1,36]{2,1,0:T(1,128)} %broadcast_in_dim.27), calls=%async_computation.10 | async-start | bytes 131072 | tf_op jit(solution)/shard_map/all_to_all | solution.py:314
  (45 other events, 468.0 us)

commit v6 on v3

--- a/solution.py
+++ b/solution.py
@@ -265,9 +265,22 @@
     )
     all_devices = data_devices * seq_devices
     taps_flat = taps_terms.reshape(all_devices, -1)
-    taps_share = jnp.sum(
-        lax.all_to_all(taps_flat, ("dp", "seq"), split_axis=0, concat_axis=0, tiled=True), axis=0
-    )
+    lane = 128
+    proj_terms = jnp.einsum("tc,tj->cj", signal, grad_rows, preferred_element_type=jnp.float32)
+    row_block = proj_terms.shape[0] // all_devices
+    proj_flat = proj_terms.reshape(all_devices, row_block * proj_terms.shape[1] // lane, lane)
+    taps_row = jnp.pad(taps_flat, ((0, 0), (0, lane - taps_flat.shape[1])))[:, None, :]
+    proj_parts = jnp.sum(
+        lax.all_to_all(
+            jnp.concatenate([proj_flat, taps_row], axis=1),
+            ("dp", "seq"),
+            split_axis=0,
+            concat_axis=0,
+            tiled=True,
+        ),
+        axis=0,
+    )
+    taps_share = proj_parts[-1, : taps_flat.shape[1]]
     taps_whole = lax.all_to_all(
         jnp.broadcast_to(taps_share[None], taps_flat.shape),
         ("dp", "seq"),
@@ -276,15 +289,7 @@
         tiled=True,
     )
     grad_taps = taps_whole.reshape(taps_terms.shape) * grad_scale
-    proj_terms = jnp.einsum("tc,tj->cj", signal, grad_rows, preferred_element_type=jnp.float32)
-    proj_parts = lax.all_to_all(
-        proj_terms.reshape(all_devices, proj_terms.shape[0] // all_devices, proj_terms.shape[1]),
-        ("dp", "seq"),
-        split_axis=0,
-        concat_axis=0,
-        tiled=True,
-    )
-    grad_proj = jnp.sum(proj_parts, axis=0) * grad_scale
+    grad_proj = proj_parts[:-1].reshape(row_block, proj_terms.shape[1]) * grad_scale
     grad_in = jnp.einsum(
         "tj,dj->td", grad_rows, proj_weight, preferred_element_type=jnp.float32
     ).astype(jnp.bfloat16)

time: 516 us -> 517 us (level)
    all_to_all x2 -> x1, starting transfers between devices: 15.2 us -> 9.27 us  [shards(): lax.all_to_all(jnp.concatenate([proj_flat, taps_row], axis=1), ('dp', 'se...]
    all_to_all x2 -> x1, waiting for transfers between devices: 41.9 us -> 44.6 us  [shards(): lax.all_to_all(jnp.concatenate([proj_flat, taps_row], axis=1), ('dp', 'se...]
  transfers between devices with their start and end apart: 10 -> 9, of which waited for: 8 -> 6; matrix products, arithmetic and copies ran while one was open for 6% -> 7% of each run, Pallas kernels for 0% -> 0%
where the time goes in v6:
time: 517 us; the launch traced here: 510 us
  waiting for transfers between devices  110 us (21%)
  matrix products  101 us (20%)
  local copies, waits for them, and re-layouts  94.4 us (18%)
  blocking collectives  82.4 us (16%)
  other arithmetic  65.8 us (13%)
  starting transfers between devices  54.1 us (10%)
    dot_general x8, matrix products, dft_pair(): jnp.einsum('yz' + table_part + ',z' + data_part + '->y' + result_side, bl...  87.7 us
    all_to_all x1, waiting for transfers between devices, shards(): lax.all_to_all(jnp.concatenate([proj_flat, taps_row], axis=1), ('dp', 'se...  44.6 us
    all_to_all x2, blocking collectives, inverse_transform(): lax.all_to_all(values.astype(jnp.bfloat16), 'seq', split_axis=0, concat_a...  36.2 us
    all_to_all x2, waiting for transfers between devices, forward_transform(): lax.all_to_all(stacked, 'seq', split_axis=1, concat_axis=2, tiled=True)  35.1 us
    all_to_all x1, blocking collectives, inverse_transform(): lax.all_to_all(packed[:, None], 'seq', split_axis=2, concat_axis=1, tiled...  31.7 us
    dot_general x2, local copies, waits for them, and re-layouts, dft_pair(): jnp.einsum('yz' + table_part + ',z' + data_part + '->y' + result_side, bl...  21 us
    slice x4, local copies, waits for them, and re-layouts, rotate_stacked(): stacked[0] * cosine_table - direction * stacked[1] * sine_table  16.4 us
    sub x4, other arithmetic, rotate_stacked(): stacked[0] * cosine_table - direction * stacked[1] * sine_table  15.1 us
  transfers between devices with their start and end apart: 9, of which 6 were waited for; matrix products, arithmetic and copies ran while one was open for 7% of the time, Pallas kernels for 0%

profile of v6, /device:TPU:1, one launch (start us, length us, event | category | flops | bytes accessed | tf_op | source)
XLA Modules:
  0.0 509.6 jit_solution(8383822124044337764)
XLA Ops:
  12.0 8.2 %all-to-all-start = ((bf16[32,8,2048]{2,1,0:T(8,128)(2,1)}), bf16[32,8,2048]{2,1,0:T(8,128)(2,1)S(1)}, u32[]{:S(2)}, u32[]{:S(2)}) async-start(bf16[32,8,2048]{2,1,0:T(8,128)(2,1)} %pad_maximum_fusion.4), calls=%async_computation | async-start | bytes 2097152 | tf_op jit(solution)/shard_map/all_to_all | solution.py:104
  20.6 13.9 %all-to-all-done = bf16[32,8,2048]{2,1,0:T(8,128)(2,1)S(1)} async-done(((bf16[32,8,2048]{2,1,0:T(8,128)(2,1)}), bf16[32,8,2048]{2,1,0:T(8,128)(2,1)S(1)}, u32[]{:S(2)}, u32[]{:S(2)}) %all-to-all-start) | async-done | bytes 1048608 | tf_op jit(solution)/shard_map/all_to_all | solution.py:104
  49.3 24.9 %all-to-all-done.1 = bf16[2,32,8,2048]{3,2,0,1:T(8,128)(2,1)} async-done(((bf16[2,32,8,2048]{3,2,0,1:T(8,128)(2,1)}), bf16[2,32,8,2048]{3,2,0,1:T(8,128)(2,1)}, u32[]{:S(2)}, u32[]{:S(2)}) %all-to-all-start.1) | async-done | bytes 2097184 | tf_op jit(solution)/shard_map/all_to_all | solution.py:124
  90.4 19.8 %fusion.7 = f32[2,2,2,128,2048]{4,2,0,3,1:T(2,128)S(1)} fusion(f32[2,1,2,128,2048]{4,0,2,3,1:T(2,128)S(1)} %maximum_select_fusion, f32[2,1,2,128,2048]{4,0,2,3,1:T(2,128)S(1)} %select_select_fusion, f32[1,2,2,2]{1,2,3,0:T(2,128)S(1)} %copy.183, f32[1,2,2,2]{1,2,3,0:T(2,128)S(1)} %copy.182), kind=kOutput, calls=%fused_computation.12 | convolution fusion | flops 52428816 | bytes 16777280 | tf_op jit(solution)/shard_map/yzga,zkabw->ykgbw/dot_general | solution.py:44
  120.3 11.2 %fusion.8 = f32[2,2,2,128,2048]{4,3,0,2,1:T(8,128)S(1)} fusion(f32[2,2,2,128,2048,1]{4,2,0,3,1,5:T(2,128)S(1)} %maximum_bitcast_fusion.1, f32[1,2,128,128]{3,2,1,0:T(8,128)S(1)} %get-tuple-element.117, f32[1,2,128,128]{3,2,1,0:T(8,128)S(1)} %get-tuple-element.120), kind=kOutput, calls=%fused_computation.14 | convolution fusion | flops 3221291008 | bytes 17039360 | tf_op jit(solution)/shard_map/yzfb,zkgbw->ykgfw/dot_general | solution.py:44
  143.2 7.4 %copy.231 = f32[2,2,2,128,1024,1]{4,0,2,5,3,1:T(2,128)} copy(f32[2,2,2,128,1024,1]{3,4,0,2,1,5:T(8,128)} %maximum_bitcast_fusion.9) | data formatting | bytes 8388608 | tf_op jit(solution)/shard_map/stack | solution.py:29
  150.6 11.3 %fusion.21 = f32[2,2,2,128,1024]{4,2,0,3,1:T(2,128)S(1)} fusion(f32[2,2,2,128,1024,1]{4,0,2,5,3,1:T(2,128)} %copy.231, f32[1,2,2,2]{1,2,3,0:T(2,128)S(1)} %copy.190, f32[1,2,2,2]{1,2,3,0:T(2,128)S(1)} %copy.189), kind=kOutput, calls=%fused_computation.33 | convolution fusion | flops 26214416 | bytes 8388672 | tf_op jit(solution)/shard_map/yzag,zkgbw->ykabw/dot_general | solution.py:44
  180.7 7.4 %all-to-all-done.2 = bf16[2,1,256,1024]{3,0,1,2:T(2,128)(2,1)S(1)} async-done(((bf16[2,1,256,1024]{3,0,1,2:T(2,128)(2,1)}), bf16[2,1,256,1024]{3,0,1,2:T(2,128)(2,1)S(1)}, u32[]{:S(2)}, u32[]{:S(2)}) %all-to-all-start.2) | async-done | bytes 1048608 | tf_op jit(solution)/shard_map/all_to_all | solution.py:153
  190.1 15.6 %all_to_all.86 = bf16[32,8,1024]{2,1,0:T(8,128)(2,1)S(1)} all-to-all(bf16[32,8,1024]{2,1,0:T(8,128)(2,1)S(1)} %copy.197), channel_id=1, replica_groups=mesh['dp'=4,'seq'=32] {'seq'}, dimensions={0} | all-to-all | bytes 1048576 | tf_op jit(solution)/shard_map/all_to_all | solution.py:162
  206.6 14.5 %all_to_all.87 = bf16[32,8,1024]{2,1,0:T(8,128)(2,1)S(1)} all-to-all(bf16[32,8,1024]{2,1,0:T(8,128)(2,1)S(1)} %maximum_bitcast_fusion.18), channel_id=1, replica_groups=mesh['dp'=4,'seq'=32] {'seq'}, dimensions={0} | all-to-all | bytes 1048576 | tf_op jit(solution)/shard_map/all_to_all | solution.py:104
  233.6 10.2 %all-to-all-done.5 = bf16[2,32,8,1024]{3,2,0,1:T(8,128)(2,1)S(1)} async-done(((bf16[2,32,8,1024]{3,2,0,1:T(8,128)(2,1)}), bf16[2,32,8,1024]{3,2,0,1:T(8,128)(2,1)S(1)}, u32[]{:S(2)}, u32[]{:S(2)}) %all-to-all-start.5) | async-done | bytes 1048608 | tf_op jit(solution)/shard_map/all_to_all | solution.py:124
  251.7 9.6 %fusion.25 = f32[2,128,1024,2,2]{2,4,3,1,0:T(2,128)} fusion(f32[2,1,2,128,1024]{4,0,2,3,1:T(2,128)S(1)} %maximum_select_fusion.1, f32[2,1,2,128,1024]{4,0,2,3,1:T(2,128)S(1)} %select_select_fusion.1, f32[1,2,2,2]{1,2,3,0:T(2,128)S(1)} %copy-done.53, f32[1,2,2,2]{1,2,3,0:T(2,128)S(1)} %copy-done.51), kind=kOutput, calls=%fused_computation.42 | convolution fusion | flops 26214416 | bytes 8388672 | tf_op jit(solution)/shard_map/yzga,zkabw->ykgbw/dot_general | solution.py:44
  261.3 7.7 %copy.206 = f32[2,128,1024,2,2]{1,2,3,4,0:T(8,128)} copy(f32[2,128,1024,2,2]{2,4,3,1,0:T(2,128)} %fusion.25) | data formatting | bytes 8388608 | tf_op jit(solution)/shard_map/yzga,zkabw->ykgbw/dot_general | solution.py:44
  277.9 8.9 %fusion.11 = f32[2,2,2048,2,128]{4,2,3,1,0:T(8,128)} fusion(f32[2,2,2,128,2048,1]{4,3,2,1,0,5:T(8,128)S(1)} %bitcast.258, f32[1,2,128,128]{3,2,1,0:T(8,128)S(1)} %copy-done.7, f32[1,2,128,128]{3,2,1,0:T(8,128)S(1)} %get-tuple-element.116), kind=kOutput, calls=%fused_computation.15 | convolution fusion | flops 3221291008 | bytes 17039360 | tf_op jit(solution)/shard_map/yzbf,zkgfw->ykgbw/dot_general | solution.py:44
  286.8 13.3 %copy.210 = f32[2,2,2048,2,128]{2,1,3,4,0:T(2,128)} copy(f32[2,2,2048,2,128]{4,2,3,1,0:T(8,128)} %fusion.11) | data formatting | bytes 16777216 | tf_op jit(solution)/shard_map/yzbf,zkgfw->ykgbw/dot_general | solution.py:44
  300.1 7.1 %multiply_subtract_fusion = (f32[1,2,2,128,2048]{4,2,0,3,1:T(2,128)S(1)}, f32[1,2,2,128,2048]{4,2,0,3,1:T(2,128)S(1)}) fusion(f32[2,2,2,128,2048]{4,2,0,3,1:T(2,128)} %bitcast.259, f32[2,128]{0,1:T(8,128)S(1)} %copy-done.18, f32[2,128]{0,1:T(8,128)S(1)} %copy-done.16), kind=kLoop, calls=%fused_computation.37 | loop fusion | flops 6291456 | bytes 16779264 | tf_op jit(solution)/shard_map/sub | solution.py:31
  307.2 21.0 %fusion = f32[2,2,2,128,2048]{4,2,0,3,1:T(2,128)} fusion(f32[2,2,2,2,1,1]{3,2,1,0,5,4:T(2,128)S(1)} %copy-done.47, f32[1,2,2,128,2048]{4,2,0,3,1:T(2,128)S(1)} %get-tuple-element.80, f32[1,2,2,128,2048]{4,2,0,3,1:T(2,128)S(1)} %get-tuple-element.79), kind=kOutput, calls=%fused_computation.5 | convolution fusion | flops 54525952 | bytes 16777280 | tf_op jit(solution)/shard_map/yzag,zkgbw->ykabw/dot_general | solution.py:44
  328.2 9.6 %fusion.140 = (f32[1,2,2,128,2048]{4,2,0,3,1:T(2,128)}, f32[1,2,2,128,2048]{4,2,0,3,1:T(2,128)S(1)}) fusion(f32[2,2,2,128,2048]{4,2,0,3,1:T(2,128)} %fusion), kind=kLoop, calls=%fused_computation.277 | loop fusion | bytes 16777216 | tf_op jit(solution)/shard_map/slice | solution.py:31
  350.0 31.7 %all_to_all.88 = bf16[2,1,256,2048]{3,0,1,2:T(2,128)(2,1)S(1)} all-to-all(bf16[2,1,256,2048]{3,0,1,2:T(2,128)(2,1)S(1)} %copy.215), channel_id=1, replica_groups=mesh['dp'=4,'seq'=32] {'seq'}, dimensions={2} | all-to-all | bytes 4194304 | tf_op jit(solution)/shard_map/all_to_all | solution.py:153
  384.9 20.6 %all_to_all.89 = bf16[32,8,2048]{2,1,0:T(8,128)(2,1)S(1)} all-to-all(bf16[32,8,2048]{2,1,0:T(8,128)(2,1)S(1)} %copy.218), channel_id=1, replica_groups=mesh['dp'=4,'seq'=32] {'seq'}, dimensions={0} | all-to-all | bytes 2097152 | tf_op jit(solution)/shard_map/all_to_all | solution.py:162
  410.9 8.0 %all-to-all-start.10 = ((bf16[4,2,256,128]{3,1,2,0:T(2,128)(2,1)}), bf16[4,2,256,128]{3,1,2,0:T(2,128)(2,1)S(1)}, u32[]{:S(2)}, u32[]{:S(2)}) async-start(bf16[4,2,256,128]{3,1,2,0:T(2,128)(2,1)} %bitcast.249), calls=%async_computation.10 | async-start | bytes 1048576 | tf_op jit(solution)/shard_map/all_to_all | solution.py:234
  434.1 9.3 %all-to-all-start.8 = ((f32[128,49,128]{2,1,0:T(8,128)}), f32[128,49,128]{2,1,0:T(8,128)}, u32[]{:S(2)}, u32[]{:S(2)}) async-start(f32[128,49,128]{2,1,0:T(8,128)} %pad_maximum_fusion), calls=%async_computation.8 | async-start | bytes 7340032 | tf_op jit(solution)/shard_map/all_to_all | solution.py:274
  446.0 44.6 %all-to-all-done.8 = f32[128,49,128]{2,1,0:T(8,128)} async-done(((f32[128,49,128]{2,1,0:T(8,128)}), f32[128,49,128]{2,1,0:T(8,128)}, u32[]{:S(2)}, u32[]{:S(2)}) %all-to-all-start.8) | async-done | bytes 3211296 | tf_op jit(solution)/shard_map/all_to_all | solution.py:274
  499.2 9.3 %all-to-all-done.9 = f32[128,1,36]{2,1,0:T(1,128)S(1)} async-done(((f32[128,1,36]{2,1,0:T(1,128)}), f32[128,1,36]{2,1,0:T(1,128)S(1)}, u32[]{:S(2)}, u32[]{:S(2)}) %all-to-all-start.9) | async-done | bytes 18464 | tf_op jit(solution)/shard_map/all_to_all | solution.py:284
  (251 shorter events, 162.4 us)
Async XLA Ops:
  3.6 5.3 %collective-permute-start = (bf16[2,1536]{1,0:T(2,128)(2,1)S(1)}, bf16[2,1536]{1,0:T(2,128)(2,1)S(1)}, u32[]{:S(2)}, u32[]{:S(2)}) collective-permute-start(bf16[2,1536]{1,0:T(2,128)(2,1)S(1)} %slice.426), channel_id=1, source_target_pairs={{0,1},{1,2},{2,3},{3,4},{4,5},{5,6},{6,7},{7,8},{8,9},{9,10},{10,1... | collective-permute-start | bytes 18440 | tf_op jit(solution)/shard_map/ppermute | solution.py:15
  12.0 22.5 %all-to-all-start = ((bf16[32,8,2048]{2,1,0:T(8,128)(2,1)}), bf16[32,8,2048]{2,1,0:T(8,128)(2,1)S(1)}, u32[]{:S(2)}, u32[]{:S(2)}) async-start(bf16[32,8,2048]{2,1,0:T(8,128)(2,1)} %pad_maximum_fusion.4), calls=%async_computation | async-start | bytes 2097152 | tf_op jit(solution)/shard_map/all_to_all | solution.py:104
  40.4 33.7 %all-to-all-start.1 = ((bf16[2,32,8,2048]{3,2,0,1:T(8,128)(2,1)}), bf16[2,32,8,2048]{3,2,0,1:T(8,128)(2,1)}, u32[]{:S(2)}, u32[]{:S(2)}) async-start(bf16[2,32,8,2048]{3,2,0,1:T(8,128)(2,1)} %copy.175), calls=%async_computation.1 | async-start | bytes 4194304 | tf_op jit(solution)/shard_map/all_to_all | solution.py:124
  47.6 42.8 %copy-start.50 = (f32[1,2,2,2]{1,2,3,0:T(2,128)}, f32[1,2,2,2]{1,2,3,0:T(2,128)S(1)}, u32[]{:S(2)}) copy-start(f32[1,2,2,2]{1,2,3,0:T(2,128)S(1)} %copy.182) | copy-start | bytes 100
  47.7 42.7 %copy-start.52 = (f32[1,2,2,2]{1,2,3,0:T(2,128)}, f32[1,2,2,2]{1,2,3,0:T(2,128)S(1)}, u32[]{:S(2)}) copy-start(f32[1,2,2,2]{1,2,3,0:T(2,128)S(1)} %copy.183) | copy-start | bytes 100
  47.7 92.7 %copy-start.39 = (f32[2,128]{1,0:T(2,128)}, f32[2,128]{1,0:T(2,128)S(1)}, u32[]{:S(2)}) copy-start(f32[2,128]{1,0:T(2,128)S(1)} %get-tuple-element.141) | copy-start | bytes 3076
  47.7 92.7 %copy-start.42 = (f32[2,128]{1,0:T(2,128)}, f32[2,128]{1,0:T(2,128)S(1)}, u32[]{:S(2)}) copy-start(f32[2,128]{1,0:T(2,128)S(1)} %get-tuple-element.140) | copy-start | bytes 3076
  47.8 62.4 %copy-start.15 = (f32[2,128]{0,1:T(8,128)}, f32[2,128]{0,1:T(8,128)S(1)}, u32[]{:S(2)}) copy-start(f32[2,128]{0,1:T(8,128)S(1)} %copy.184) | copy-start | bytes 3076
  48.1 102.5 %copy-start.37 = (f32[1,2,2,2]{1,2,3,0:T(2,128)}, f32[1,2,2,2]{1,2,3,0:T(2,128)S(1)}, u32[]{:S(2)}) copy-start(f32[1,2,2,2]{1,2,3,0:T(2,128)S(1)} %copy.189) | copy-start | bytes 100
  48.2 102.4 %copy-start.38 = (f32[1,2,2,2]{1,2,3,0:T(2,128)}, f32[1,2,2,2]{1,2,3,0:T(2,128)S(1)}, u32[]{:S(2)}) copy-start(f32[1,2,2,2]{1,2,3,0:T(2,128)S(1)} %copy.190) | copy-start | bytes 100
  48.5 27.2 %copy-start.43 = (f32[256]{0:T(256)}, f32[256]{0:T(256)S(1)}, u32[]{:S(2)}) copy-start(f32[256]{0:T(256)S(1)} %get-tuple-element.136) | copy-start | bytes 3076
  48.5 27.2 %copy-start.44 = (f32[256]{0:T(256)}, f32[256]{0:T(256)S(1)}, u32[]{:S(2)}) copy-start(f32[256]{0:T(256)S(1)} %get-tuple-element.137) | copy-start | bytes 3076
  49.1 71.2 %copy-start.8 = (f32[1,2,128,128]{3,2,1,0:T(8,128)}, f32[1,2,128,128]{3,2,1,0:T(8,128)S(1)}, u32[]{:S(2)}) copy-start(f32[1,2,128,128]{3,2,1,0:T(8,128)S(1)} %get-tuple-element.117) | copy-start | bytes 393220
  49.1 71.2 %copy-start.10 = (f32[1,2,128,128]{3,2,1,0:T(8,128)}, f32[1,2,128,128]{3,2,1,0:T(8,128)S(1)}, u32[]{:S(2)}) copy-start(f32[1,2,128,128]{3,2,1,0:T(8,128)S(1)} %get-tuple-element.120) | copy-start | bytes 393220
  49.1 87.3 %copy-start.6 = (f32[1,2,128,128]{3,2,1,0:T(8,128)}, f32[1,2,128,128]{3,2,1,0:T(8,128)S(1)}, u32[]{:S(2)}) copy-start(f32[1,2,128,128]{3,2,1,0:T(8,128)S(1)} %get-tuple-element.121) | copy-start | bytes 393220
  49.2 115.6 %copy-start.33 = (f32[2,256]{1,0:T(2,128)}, f32[2,256]{1,0:T(2,128)S(1)}, u32[]{:S(2)}) copy-start(f32[2,256]{1,0:T(2,128)S(1)} %get-tuple-element.130) | copy-start | bytes 6148
  49.3 115.6 %copy-start.35 = (f32[2,256]{1,0:T(2,128)}, f32[2,256]{1,0:T(2,128)S(1)}, u32[]{:S(2)}) copy-start(f32[2,256]{1,0:T(2,128)S(1)} %get-tuple-element.131) | copy-start | bytes 6148
  167.7 20.3 %all-to-all-start.2 = ((bf16[2,1,256,1024]{3,0,1,2:T(2,128)(2,1)}), bf16[2,1,256,1024]{3,0,1,2:T(2,128)(2,1)S(1)}, u32[]{:S(2)}, u32[]{:S(2)}) async-start(bf16[2,1,256,1024]{3,0,1,2:T(2,128)(2,1)} %copy.194), calls=%async_computation.2 | async-start | bytes 2097152 | tf_op jit(solution)/shard_map/all_to_all | solution.py:153
  224.3 19.5 %all-to-all-start.5 = ((bf16[2,32,8,1024]{3,2,0,1:T(8,128)(2,1)}), bf16[2,32,8,1024]{3,2,0,1:T(8,128)(2,1)S(1)}, u32[]{:S(2)}, u32[]{:S(2)}) async-start(bf16[2,32,8,1024]{3,2,0,1:T(8,128)(2,1)} %copy.199), calls=%async_computation.5 | async-start | bytes 2097152 | tf_op jit(solution)/shard_map/all_to_all | solution.py:124
  384.9 21.5 %copy-start.4 = (bf16[256,512]{1,0:T(8,128)(2,1)S(1)}, bf16[256,512]{1,0:T(8,128)(2,1)}, u32[]{:S(2)}) copy-start(bf16[256,512]{1,0:T(8,128)(2,1)} %get-tuple-element.115) | copy-start | bytes 786436
  407.7 11.2 %collective-permute-start.1 = (bf16[2,1536]{1,0:T(2,128)(2,1)S(1)}, bf16[2,1536]{1,0:T(2,128)(2,1)S(1)}, u32[]{:S(2)}, u32[]{:S(2)}) collective-permute-start(bf16[2,1536]{1,0:T(2,128)(2,1)S(1)} %slice.473), channel_id=1, source_target_pairs={{1,0},{2,1},{3,2},{4,3},{5,4},{6,5},{7,6},{8,7},{9,8},{10,9},{11,1... | collective-permute-start | bytes 18440 | tf_op jit(solution)/shard_map/ppermute | solution.py:15
  410.9 23.2 %all-to-all-start.10 = ((bf16[4,2,256,128]{3,1,2,0:T(2,128)(2,1)}), bf16[4,2,256,128]{3,1,2,0:T(2,128)(2,1)S(1)}, u32[]{:S(2)}, u32[]{:S(2)}) async-start(bf16[4,2,256,128]{3,1,2,0:T(2,128)(2,1)} %bitcast.249), calls=%async_computation.10 | async-start | bytes 1048576 | tf_op jit(solution)/shard_map/all_to_all | solution.py:234
  434.1 56.6 %all-to-all-start.8 = ((f32[128,49,128]{2,1,0:T(8,128)}), f32[128,49,128]{2,1,0:T(8,128)}, u32[]{:S(2)}, u32[]{:S(2)}) async-start(f32[128,49,128]{2,1,0:T(8,128)} %pad_maximum_fusion), calls=%async_computation.8 | async-start | bytes 7340032 | tf_op jit(solution)/shard_map/all_to_all | solution.py:274
  493.7 14.8 %all-to-all-start.9 = ((f32[128,1,36]{2,1,0:T(1,128)}), f32[128,1,36]{2,1,0:T(1,128)S(1)}, u32[]{:S(2)}, u32[]{:S(2)}) async-start(f32[128,1,36]{2,1,0:T(1,128)} %broadcast_in_dim.27), calls=%async_computation.9 | async-start | bytes 131072 | tf_op jit(solution)/shard_map/all_to_all | solution.py:284
  (41 other events, 286.7 us)

commit v7 on v6

--- a/solution.py
+++ b/solution.py
@@ -69,7 +69,7 @@
 
 def local_forward(stacked):
     local_freqs, frames, channels = (stacked.shape[1], stacked.shape[2], stacked.shape[3])
-    inner_len = math.gcd(frames, 128)
+    inner_len = frames
     outer_len = frames // inner_len
     data = stacked.reshape(2, local_freqs, outer_len, inner_len, channels)
     cosine_table, sine_table = angle_table(outer_len, outer_len, outer_len)
@@ -83,7 +83,7 @@
 
 def local_inverse(stacked):
     local_freqs, frames, channels = (stacked.shape[1], stacked.shape[2], stacked.shape[3])
-    inner_len = math.gcd(frames, 128)
+    inner_len = frames
     outer_len = frames // inner_len
     data = stacked.reshape(2, local_freqs, outer_len, inner_len, channels)
     cosine_table, sine_table = angle_table(inner_len, inner_len, inner_len)

time: 517 us -> 525 us (1.015)
  other arithmetic: 65.8 us -> 97.1 us
  local copies, waits for them, and re-layouts: 94.4 us -> 64.5 us
  blocking collectives: 82.4 us -> 102 us
    another operation x6 -> x10, other arithmetic: 5.32 us -> 36 us
    all_to_all x0 -> x1, blocking collectives: none -> 19.3 us  [forward_transform(): lax.all_to_all(stacked, 'seq', split_axis=1, concat_axis=2, tiled=True)]
    slice x6 -> x1, local copies, waits for them, and re-layouts: 19.5 us -> 3.43 us  [forward_transform(): data[1]]
    dot_general x2, local copies, waits for them, and re-layouts: 21 us -> 6.21 us  [dft_pair(): jnp.einsum('yz' + table_part + ',z' + data_part + '->y' + result_side, bl...]
    select_n x2, other arithmetic: 0.55 us -> 14.7 us  [inverse_transform(): jnp.where(device == 0, jnp.stack([back[0, 0], back[0, 1]]), back[:, 0])]
    another operation x9 -> x2, local copies, waits for them, and re-layouts: 8.25 us -> 20.8 us  [the longest x4 6.47 us: forward_transform(): jnp.stack([jnp.cos(angles) * data[1], -jnp.sin(angles) * data[1]])]
    all_to_all x2 -> x1, waiting for transfers between devices: 35.1 us -> 23.1 us  [forward_transform(): lax.all_to_all(stacked, 'seq', split_axis=1, concat_axis=2, tiled=True)]
    sub x4, other arithmetic: 15.1 us -> 3.68 us  [rotate_stacked(): stacked[0] * cosine_table - direction * stacked[1] * sine_table]
  transfers between devices with their start and end apart: 9 -> 8, of which waited for: 6 -> 6; matrix products, arithmetic and copies ran while one was open for 7% -> 5% of each run, Pallas kernels for 0% -> 0%
where the time goes in v7:
time: 525 us; the launch traced here: 518 us
  waiting for transfers between devices  105 us (20%)
  blocking collectives  102 us (19%)
  matrix products  97.9 us (19%)
  other arithmetic  97.1 us (18%)
  local copies, waits for them, and re-layouts  64.5 us (12%)
  starting transfers between devices  49.4 us (9%)
    dot_general x8, matrix products, dft_pair(): jnp.einsum('yz' + table_part + ',z' + data_part + '->y' + result_side, bl...  84.2 us
    all_to_all x1, waiting for transfers between devices, shards(): lax.all_to_all(jnp.concatenate([proj_flat, taps_row], axis=1), ('dp', 'se...  43.5 us
    all_to_all x2, blocking collectives, inverse_transform(): lax.all_to_all(values.astype(jnp.bfloat16), 'seq', split_axis=0, concat_a...  36.1 us
    all_to_all x1, blocking collectives, inverse_transform(): lax.all_to_all(packed[:, None], 'seq', split_axis=2, concat_axis=1, tiled...  31.8 us
    another operation x8, other arithmetic  30 us
    all_to_all x1, waiting for transfers between devices, forward_transform(): lax.all_to_all(stacked, 'seq', split_axis=1, concat_axis=2, tiled=True)  23.1 us
    another operation x2, local copies, waits for them, and re-layouts  20.8 us
    all_to_all x1, blocking collectives, forward_transform(): lax.all_to_all(stacked, 'seq', split_axis=1, concat_axis=2, tiled=True)  19.3 us
  transfers between devices with their start and end apart: 8, of which 6 were waited for; matrix products, arithmetic and copies ran while one was open for 5% of the time, Pallas kernels for 0%

profile of v7, /device:TPU:1, one launch (start us, length us, event | category | flops | bytes accessed | tf_op | source)
XLA Modules:
  0.0 518.1 jit_solution(6944775223095439139)
XLA Ops:
  12.9 8.4 %all-to-all-start = ((bf16[32,8,2048]{2,1,0:T(8,128)(2,1)}), bf16[32,8,2048]{2,1,0:T(8,128)(2,1)}, u32[]{:S(2)}, u32[]{:S(2)}) async-start(bf16[32,8,2048]{2,1,0:T(8,128)(2,1)} %pad_maximum_fusion.8), calls=%async_computation | async-start | bytes 2097152 | tf_op jit(solution)/shard_map/all_to_all | solution.py:104
  21.6 13.9 %all-to-all-done = bf16[32,8,2048]{2,1,0:T(8,128)(2,1)} async-done(((bf16[32,8,2048]{2,1,0:T(8,128)(2,1)}), bf16[32,8,2048]{2,1,0:T(8,128)(2,1)}, u32[]{:S(2)}, u32[]{:S(2)}) %all-to-all-start) | async-done | bytes 1048608 | tf_op jit(solution)/shard_map/all_to_all | solution.py:104
  53.0 23.1 %all-to-all-done.1 = bf16[2,32,8,2048]{3,2,0,1:T(8,128)(2,1)} async-done(((bf16[2,32,8,2048]{3,2,0,1:T(8,128)(2,1)}), bf16[2,32,8,2048]{3,2,0,1:T(8,128)(2,1)}, u32[]{:S(2)}, u32[]{:S(2)}) %all-to-all-start.1) | async-done | bytes 2097184 | tf_op jit(solution)/shard_map/all_to_all | solution.py:124
  82.0 9.5 %select_select_fusion = (f32[2,1,256,2048]{3,0,2,1:T(2,128)S(1)}, f32[2,1,256,2048]{3,0,2,1:T(2,128)S(1)}) fusion(f32[2,1,256,2048]{3,2,0,1:T(8,128)S(1)} %get-tuple-element.103, pred[2]{0:T(512)(128)(4,1)S(1)} %copy-done.38, pred[]{:T(512)S(6)} %eq.64, f32[1,1,256,2048]{3,0,2,1:T(1,128)S(1)} %get-tuple-element.106, ...), kind=kLoop, calls=%fused_computation.24 | loop fusion | flops 4194304 | bytes 16777220 | tf_op jit(solution)/shard_map/jit(_where)/select_n | solution.py:130
  91.5 15.9 %fusion.17 = f32[2,256,2048,2]{2,3,1,0:T(2,128)S(1)} fusion(f32[2,2,1,1]{1,0,3,2:T(2,128)S(1)} %copy-done.39, f32[2,1,256,2048]{3,0,2,1:T(2,128)S(1)} %get-tuple-element.127, f32[2,1,256,2048]{3,0,2,1:T(2,128)S(1)} %get-tuple-element.126), kind=kOutput, calls=%fused_computation.23 | convolution fusion | flops 27262976 | bytes 16777232 | tf_op jit(solution)/shard_map/yzga,zkabw->ykgbw/dot_general | solution.py:44
  114.2 14.6 %fusion.19 = f32[2,2,256,2048]{2,3,0,1:T(8,128)S(1)} fusion(f32[1,2,256,256]{3,2,1,0:T(8,128)S(1)} %copy-done.4, f32[1,2,256,256]{3,2,1,0:T(8,128)S(1)} %copy-done.6, f32[1,2,1,256,2048]{4,3,2,1,0:T(8,128)S(1)} %get-tuple-element.90, f32[1,2,1,256,2048]{4,3,2,1,0:T(8,128)S(1)} %get-tuple-element.89), kind=kOutput, calls=%fused_computation.26 | convolution fusion | flops 6444810240 | bytes 17825792 | tf_op jit(solution)/shard_map/yzfb,zkgbw->ykgfw/dot_general | solution.py:44
  138.5 7.4 %copy.114 = f32[2,2,256,1024]{3,0,2,1:T(2,128)} copy(f32[2,2,256,1024]{2,3,0,1:T(8,128)} %maximum_bitcast_fusion.8) | data formatting | bytes 8388608 | tf_op jit(solution)/shard_map/reshape.146
  145.9 8.7 %convolution_multiply_fusion = f32[2,256,1024,2]{2,3,1,0:T(2,128)S(1)} fusion(f32[2,2,256,1024]{3,0,2,1:T(2,128)} %copy.114, f32[2,2,1,1]{1,0,3,2:T(2,128)S(1)} %copy-done.36), kind=kOutput, calls=%fused_computation.54 | convolution fusion | flops 13631488 | bytes 8388624 | tf_op jit(solution)/shard_map/yzag,zkgbw->ykabw/dot_general | solution.py:44
  176.8 12.2 %all-to-all-done.2 = bf16[2,1,256,1024]{3,0,1,2:T(2,128)(2,1)} async-done(((bf16[2,1,256,1024]{3,0,1,2:T(2,128)(2,1)}), bf16[2,1,256,1024]{3,0,1,2:T(2,128)(2,1)}, u32[]{:S(2)}, u32[]{:S(2)}) %all-to-all-start.2) | async-done | bytes 1048608 | tf_op jit(solution)/shard_map/all_to_all | solution.py:153
  191.5 15.5 %all_to_all.86 = bf16[32,8,1024]{2,1,0:T(8,128)(2,1)S(1)} all-to-all(bf16[32,8,1024]{2,1,0:T(8,128)(2,1)S(1)} %copy.119), channel_id=1, replica_groups=mesh['dp'=4,'seq'=32] {'seq'}, dimensions={0} | all-to-all | bytes 1048576 | tf_op jit(solution)/shard_map/all_to_all | solution.py:162
  208.9 14.5 %all_to_all.87 = bf16[32,8,1024]{2,1,0:T(8,128)(2,1)S(1)} all-to-all(bf16[32,8,1024]{2,1,0:T(8,128)(2,1)S(1)} %maximum_bitcast_fusion.18), channel_id=1, replica_groups=mesh['dp'=4,'seq'=32] {'seq'}, dimensions={0} | all-to-all | bytes 1048576 | tf_op jit(solution)/shard_map/all_to_all | solution.py:104
  225.6 19.3 %all_to_all.88 = bf16[2,32,8,1024]{3,2,0,1:T(8,128)(2,1)S(1)} all-to-all(bf16[2,32,8,1024]{3,2,0,1:T(8,128)(2,1)S(1)} %copy.121), channel_id=1, replica_groups=mesh['dp'=4,'seq'=32] {'seq'}, dimensions={1} | all-to-all | bytes 2097152 | tf_op jit(solution)/shard_map/all_to_all | solution.py:124
  257.5 7.6 %fusion.31 = f32[2,256,1024,2]{2,3,1,0:T(2,128)S(1)} fusion(f32[2,2,1,1]{1,0,3,2:T(2,128)S(1)} %copy-done.39, f32[2,1,256,1024]{3,0,2,1:T(2,128)S(1)} %maximum_select_fusion.1, f32[2,1,256,1024]{3,0,2,1:T(2,128)S(1)} %select_select_fusion.1), kind=kOutput, calls=%fused_computation.50 | convolution fusion | flops 13631488 | bytes 8388624 | tf_op jit(solution)/shard_map/yzga,zkabw->ykgbw/dot_general | solution.py:44
  278.9 10.2 %fusion.18 = f32[2,2,1,256,2048]{3,4,0,1,2:T(8,128)S(1)} fusion(f32[1,2,256,512]{2,3,0,1:T(8,128)} %get-tuple-element.73, f32[1,2,256,512]{2,3,0,1:T(8,128)S(1)} %get-tuple-element.72, f32[1,2,256,512]{2,3,0,1:T(8,128)} %get-tuple-element.76, f32[1,2,256,512]{2,3,0,1:T(8,128)} %get-tuple-element.74, f32[1,2,256,512]{2,3,0,1:T(8,128)} %get-tuple-element.78, ...), kind=kOutput, calls=%fused_computation.25 | convolution fusion | flops 6457393152 | bytes 17825792 | tf_op jit(solution)/shard_map/yzbf,zkgfw->ykgbw/dot_general | solution.py:44
  293.7 13.4 %copy.125 = f32[2,2,256,2048]{3,0,2,1:T(2,128)} copy(f32[2,2,256,2048]{2,3,0,1:T(8,128)} %maximum_bitcast_fusion.3) | data formatting | bytes 16777216 | tf_op jit(solution)/shard_map/reshape.165
  307.1 16.9 %multiply_bitcast_fusion = f32[2,2,1,256,2048]{4,0,3,2,1:T(2,128)S(1)} fusion(f32[2,2,256,2048]{3,0,2,1:T(2,128)} %copy.125, f32[2,2,1,1]{1,0,3,2:T(2,128)S(1)} %copy-done.37), kind=kOutput, calls=%fused_computation.22 | convolution fusion | flops 27262976 | bytes 16777232 | tf_op jit(solution)/shard_map/yzag,zkgbw->ykabw/dot_general | solution.py:44
  324.0 13.6 %subtract_convert_fusion = (bf16[1,2,256,2048]{3,0,2,1:T(2,128)(2,1)S(1)}, bf16[1,2,256,2048]{3,0,2,1:T(2,128)(2,1)S(1)}) fusion(f32[2,2,1,256,2048]{4,0,3,2,1:T(2,128)S(1)} %multiply_bitcast_fusion, f32[2,256]{1,0:T(2,128)S(1)} %copy-done.34, f32[2,256]{1,0:T(2,128)S(1)} %get-tuple-element.122), kind=kLoop, calls=%fused_computation.45 | loop fusion | flops 8388608 | bytes 12587008 | tf_op jit(solution)/shard_map/convert.10
  342.0 9.3 %fusion.37 = bf16[2,1,256,2048]{3,0,1,2:T(2,128)(2,1)S(1)} fusion(pred[]{:T(512)S(6)} %eq.64, bf16[1,2,256,2048]{3,0,2,1:T(2,128)(2,1)S(1)} %get-tuple-element.80, bf16[1,2,256,2048]{3,0,2,1:T(2,128)(2,1)S(1)} %get-tuple-element.79, bf16[1,1,256,2048]{3,0,2,1:T(2,128)(2,1)S(1)} %get-tuple-element.94, bf16[1,1,256,2048]{3,0,2,1:T(2,128)(2,1)S(1)} %get-tuple-element.93), kind=kLoop, calls=%fused_computation.64 | loop fusion | flops 9437184 | bytes 8388609 | tf_op jit(solution)/shard_map/jit(_where)/select_n | solution.py:152
  351.4 31.8 %all_to_all.89 = bf16[2,1,256,2048]{3,0,1,2:T(2,128)(2,1)S(1)} all-to-all(bf16[2,1,256,2048]{3,0,1,2:T(2,128)(2,1)S(1)} %fusion.37), channel_id=1, replica_groups=mesh['dp'=4,'seq'=32] {'seq'}, dimensions={2} | all-to-all | bytes 4194304 | tf_op jit(solution)/shard_map/all_to_all | solution.py:153
  385.6 20.6 %all_to_all.90 = bf16[32,8,2048]{2,1,0:T(8,128)(2,1)S(1)} all-to-all(bf16[32,8,2048]{2,1,0:T(8,128)(2,1)S(1)} %copy.129), channel_id=1, replica_groups=mesh['dp'=4,'seq'=32] {'seq'}, dimensions={0} | all-to-all | bytes 2097152 | tf_op jit(solution)/shard_map/all_to_all | solution.py:162
  412.2 8.0 %all-to-all-start.10 = ((bf16[4,2,256,128]{3,1,2,0:T(2,128)(2,1)}), bf16[4,2,256,128]{3,1,2,0:T(2,128)(2,1)}, u32[]{:S(2)}, u32[]{:S(2)}) async-start(bf16[4,2,256,128]{3,1,2,0:T(2,128)(2,1)} %bitcast.222), calls=%async_computation.10 | async-start | bytes 1048576 | tf_op jit(solution)/shard_map/all_to_all | solution.py:234
  441.7 9.9 %all-to-all-start.8 = ((f32[128,49,128]{2,1,0:T(8,128)}), f32[128,49,128]{2,1,0:T(8,128)}, u32[]{:S(2)}, u32[]{:S(2)}) async-start(f32[128,49,128]{2,1,0:T(8,128)} %pad_maximum_fusion.4), calls=%async_computation.8 | async-start | bytes 7340032 | tf_op jit(solution)/shard_map/all_to_all | solution.py:274
  455.4 43.5 %all-to-all-done.8 = f32[128,49,128]{2,1,0:T(8,128)} async-done(((f32[128,49,128]{2,1,0:T(8,128)}), f32[128,49,128]{2,1,0:T(8,128)}, u32[]{:S(2)}, u32[]{:S(2)}) %all-to-all-start.8) | async-done | bytes 3211296 | tf_op jit(solution)/shard_map/all_to_all | solution.py:274
  507.4 9.3 %all-to-all-done.9 = f32[128,1,36]{2,1,0:T(1,128)S(1)} async-done(((f32[128,1,36]{2,1,0:T(1,128)}), f32[128,1,36]{2,1,0:T(1,128)S(1)}, u32[]{:S(2)}, u32[]{:S(2)}) %all-to-all-start.9) | async-done | bytes 18464 | tf_op jit(solution)/shard_map/all_to_all | solution.py:284
  (194 shorter events, 158.8 us)
Async XLA Ops:
  3.6 5.3 %collective-permute-start = (bf16[2,1536]{1,0:T(2,128)(2,1)S(1)}, bf16[2,1536]{1,0:T(2,128)(2,1)S(1)}, u32[]{:S(2)}, u32[]{:S(2)}) collective-permute-start(bf16[2,1536]{1,0:T(2,128)(2,1)S(1)} %slice.426), channel_id=1, source_target_pairs={{0,1},{1,2},{2,3},{3,4},{4,5},{5,6},{6,7},{7,8},{8,9},{9,10},{10,1... | collective-permute-start | bytes 18440 | tf_op jit(solution)/shard_map/ppermute | solution.py:15
  12.9 22.7 %all-to-all-start = ((bf16[32,8,2048]{2,1,0:T(8,128)(2,1)}), bf16[32,8,2048]{2,1,0:T(8,128)(2,1)}, u32[]{:S(2)}, u32[]{:S(2)}) async-start(bf16[32,8,2048]{2,1,0:T(8,128)(2,1)} %pad_maximum_fusion.8), calls=%async_computation | async-start | bytes 2097152 | tf_op jit(solution)/shard_map/all_to_all | solution.py:104
  42.7 33.5 %all-to-all-start.1 = ((bf16[2,32,8,2048]{3,2,0,1:T(8,128)(2,1)}), bf16[2,32,8,2048]{3,2,0,1:T(8,128)(2,1)}, u32[]{:S(2)}, u32[]{:S(2)}) async-start(bf16[2,32,8,2048]{3,2,0,1:T(8,128)(2,1)} %copy.105), calls=%async_computation.1 | async-start | bytes 4194304 | tf_op jit(solution)/shard_map/all_to_all | solution.py:124
  53.0 101.7 %copy-start.33 = (f32[2,256]{1,0:T(2,128)}, f32[2,256]{1,0:T(2,128)S(1)}, u32[]{:S(2)}) copy-start(f32[2,256]{1,0:T(2,128)S(1)} %get-tuple-element.123) | copy-start | bytes 6148
  82.0 9.6 %copy-start.39 = (f32[2,2,1,1]{1,0,3,2:T(2,128)S(1)}, f32[2,2,1,1]{1,0,3,2:T(2,128)}, u32[]{:S(2)}) copy-start(f32[2,2,1,1]{1,0,3,2:T(2,128)} %constant.381) | copy-start | bytes 52
  138.5 7.4 %copy-start.36 = (f32[2,2,1,1]{1,0,3,2:T(2,128)S(1)}, f32[2,2,1,1]{1,0,3,2:T(2,128)}, u32[]{:S(2)}) copy-start(f32[2,2,1,1]{1,0,3,2:T(2,128)} %constant.382) | copy-start | bytes 52
  168.5 20.5 %all-to-all-start.2 = ((bf16[2,1,256,1024]{3,0,1,2:T(2,128)(2,1)}), bf16[2,1,256,1024]{3,0,1,2:T(2,128)(2,1)}, u32[]{:S(2)}, u32[]{:S(2)}) async-start(bf16[2,1,256,1024]{3,0,1,2:T(2,128)(2,1)} %fusion.47), calls=%async_computation.2 | async-start | bytes 2097152 | tf_op jit(solution)/shard_map/all_to_all | solution.py:153
  176.5 32.3 %copy-start.25 = (f32[1,32,32]{2,1,0:T(8,128)}, f32[1,32,32]{2,1,0:T(8,128)S(1)}, u32[]{:S(2)}) copy-start(f32[1,32,32]{2,1,0:T(8,128)S(1)} %scatter.10) | copy-start | bytes 12292
  176.8 32.1 %copy-start.23 = (f32[1,32,32]{2,1,0:T(8,128)}, f32[1,32,32]{2,1,0:T(8,128)S(1)}, u32[]{:S(2)}) copy-start(f32[1,32,32]{2,1,0:T(8,128)S(1)} %scatter.11) | copy-start | bytes 12292
  266.5 7.9 %slice-start = ((s8[8388608]{0:T(1024)(128)(4,1)}), s8[4194304]{0:T(1024)(128)(4,1)S(1)}, s32[]{:S(2)}) async-start(s8[8388608]{0:T(1024)(128)(4,1)} %bitcast.224), calls=%async_computation.11 | async-start | bytes 8388608
  293.7 13.4 %copy-start.37 = (f32[2,2,1,1]{1,0,3,2:T(2,128)S(1)}, f32[2,2,1,1]{1,0,3,2:T(2,128)}, u32[]{:S(2)}) copy-start(f32[2,2,1,1]{1,0,3,2:T(2,128)} %constant.382) | copy-start | bytes 52
  307.1 16.9 %copy-start.34 = (f32[2,256]{1,0:T(2,128)S(1)}, f32[2,256]{1,0:T(2,128)}, u32[]{:S(2)}) copy-start(f32[2,256]{1,0:T(2,128)} %copy-done.33) | copy-start | bytes 6148
  351.4 31.8 %copy-start.24 = (f32[1,32,32]{2,1,0:T(8,128)S(1)}, f32[1,32,32]{2,1,0:T(8,128)}, u32[]{:S(2)}) copy-start(f32[1,32,32]{2,1,0:T(8,128)} %copy-done.23) | copy-start | bytes 12292
  351.4 31.8 %copy-start.26 = (f32[1,32,32]{2,1,0:T(8,128)S(1)}, f32[1,32,32]{2,1,0:T(8,128)}, u32[]{:S(2)}) copy-start(f32[1,32,32]{2,1,0:T(8,128)} %copy-done.25) | copy-start | bytes 12292
  385.0 21.2 %copy-start.16 = (bf16[1,256,512]{2,1,0:T(8,128)(2,1)S(1)}, bf16[1,256,512]{2,1,0:T(8,128)(2,1)}, u32[]{:S(2)}) copy-start(bf16[1,256,512]{2,1,0:T(8,128)(2,1)} %param.21) | copy-start | bytes 786436
  385.6 23.3 %copy-start.10 = (bf16[256,512]{1,0:T(8,128)(2,1)S(1)}, bf16[256,512]{1,0:T(8,128)(2,1)}, u32[]{:S(2)}) copy-start(bf16[256,512]{1,0:T(8,128)(2,1)} %get-tuple-element.113) | copy-start | bytes 786436
  412.2 14.0 %copy-start.28 = (f32[1536]{0:T(1024)S(1)}, f32[1536]{0:T(1024)}, u32[]{:S(2)}) copy-start(f32[1536]{0:T(1024)} %copy-done.27) | copy-start | bytes 18436
  412.2 14.0 %copy-start.30 = (f32[1536]{0:T(1024)S(1)}, f32[1536]{0:T(1024)}, u32[]{:S(2)}) copy-start(f32[1536]{0:T(1024)} %copy-done.29) | copy-start | bytes 18436
  412.2 14.0 %copy-start.32 = (f32[1536]{0:T(1024)S(1)}, f32[1536]{0:T(1024)}, u32[]{:S(2)}) copy-start(f32[1536]{0:T(1024)} %copy-done.31) | copy-start | bytes 18436
  412.2 29.5 %all-to-all-start.10 = ((bf16[4,2,256,128]{3,1,2,0:T(2,128)(2,1)}), bf16[4,2,256,128]{3,1,2,0:T(2,128)(2,1)}, u32[]{:S(2)}, u32[]{:S(2)}) async-start(bf16[4,2,256,128]{3,1,2,0:T(2,128)(2,1)} %bitcast.222), calls=%async_computation.10 | async-start | bytes 1048576 | tf_op jit(solution)/shard_map/all_to_all | solution.py:234
  420.2 4.8 collective-permute-start.1
  441.7 9.9 %copy-start.13 = (bf16[256,1536]{1,0:T(8,128)(2,1)S(1)}, bf16[256,1536]{1,0:T(8,128)(2,1)}, u32[]{:S(2)}) copy-start(bf16[256,1536]{1,0:T(8,128)(2,1)} %copy-done.12) | copy-start | bytes 2359300
  441.7 57.2 %all-to-all-start.8 = ((f32[128,49,128]{2,1,0:T(8,128)}), f32[128,49,128]{2,1,0:T(8,128)}, u32[]{:S(2)}, u32[]{:S(2)}) async-start(f32[128,49,128]{2,1,0:T(8,128)} %pad_maximum_fusion.4), calls=%async_computation.8 | async-start | bytes 7340032 | tf_op jit(solution)/shard_map/all_to_all | solution.py:274
  501.8 14.9 %all-to-all-start.9 = ((f32[128,1,36]{2,1,0:T(1,128)}), f32[128,1,36]{2,1,0:T(1,128)S(1)}, u32[]{:S(2)}, u32[]{:S(2)}) async-start(f32[128,1,36]{2,1,0:T(1,128)} %broadcast_in_dim.27), calls=%async_computation.9 | async-start | bytes 131072 | tf_op jit(solution)/shard_map/all_to_all | solution.py:284
  (26 other events, 72.3 us)

commit v8 on v6

--- a/solution.py
+++ b/solution.py
@@ -95,19 +95,29 @@
     return data.reshape(2, local_freqs, frames, channels) / frames
 
 
-def forward_transform(field):
+def forward_gather(field):
     seq_devices = lax.axis_size("seq")
     frames, channels = field.shape
     block_rows = frames // seq_devices
-    freq_rows = 2 * seq_devices
-    fft_length = freq_rows * frames
-    received = lax.all_to_all(
+    return lax.all_to_all(
         field.reshape(seq_devices, block_rows, channels),
         "seq",
         split_axis=0,
         concat_axis=0,
         tiled=True,
     )
+
+
+def forward_transform(field):
+    return forward_core(forward_gather(field))
+
+
+def forward_core(received):
+    seq_devices = lax.axis_size("seq")
+    block_rows = received.shape[1]
+    frames = seq_devices * block_rows
+    freq_rows = 2 * seq_devices
+    fft_length = freq_rows * frames
     values = received.astype(jnp.float32)
     cosine_table, sine_table = angle_table(seq_devices, seq_devices, freq_rows)
     alternating = jnp.where(jnp.arange(seq_devices) % 2 == 0, 1.0, -1.0).astype(jnp.float32)
@@ -136,7 +146,7 @@
     return local_forward(jnp.stack([row_low, row_high], axis=1))
 
 
-def inverse_transform(spectra, keep_wide):
+def inverse_core(spectra):
     seq_devices = lax.axis_size("seq")
     local_freqs, frames, channels = (spectra.shape[1], spectra.shape[2], spectra.shape[3])
     block_rows = frames // seq_devices
@@ -158,11 +168,19 @@
     real_table = (2.0 * cosine_table).at[:, 0].set(1.0)
     imag_table = (-2.0 * sine_table).at[:, 0].set(alternating)
     part_table = jnp.stack([real_table, imag_table]) / freq_rows
-    values = jnp.einsum("zqk,zkrw->qrw", part_table, regrouped, precision=PRECISE)
+    return jnp.einsum("zqk,zkrw->qrw", part_table, regrouped, precision=PRECISE)
+
+
+def inverse_scatter(values):
+    seq_devices, block_rows, channels = values.shape
     returned = lax.all_to_all(
         values.astype(jnp.bfloat16), "seq", split_axis=0, concat_axis=1, tiled=True
     )
-    return returned.reshape(frames, channels)
+    return returned.reshape(seq_devices * block_rows, channels)
+
+
+def inverse_transform(spectra, keep_wide):
+    return inverse_scatter(inverse_core(spectra))
 
 
 def shards(frames_in, proj_weight, conv_taps, long_filters, out_grad):
@@ -190,28 +208,38 @@
     gate_two = mixed[:, 2 * channels :].astype(jnp.float32)
     upstream = out_grad[0].astype(jnp.float32)
     grad_two = (upstream * gate_two).astype(jnp.bfloat16)
-    opening = forward_transform(
-        jnp.concatenate([long_filters.reshape(frames, 2 * channels), value, grad_two], axis=1)
-    )
+    opening_rows = forward_gather(
+        jnp.concatenate(
+            [
+                long_filters.reshape(frames, 2 * channels),
+                value,
+                grad_two,
+                mixed[:, channels : 2 * channels],
+            ],
+            axis=1,
+        )
+    )
+    opening = forward_core(opening_rows[..., : 4 * channels])
+    gate_one_blocks = opening_rows[..., 4 * channels :].astype(jnp.float32)
     filter_one = opening[..., :channels]
     filter_two = opening[..., channels : 2 * channels]
     value_spectra = opening[..., 2 * channels : 3 * channels]
     two_spectra = opening[..., 3 * channels :]
-    middle_rows = inverse_transform(
+    middle_rows = inverse_core(
         jnp.concatenate(
             [
                 spectral_product(filter_one, value_spectra),
                 adjoint_product(filter_two, two_spectra),
             ],
             axis=3,
-        ),
-        False,
-    )
-    conv_one = middle_rows[:, :channels]
-    grad_first = middle_rows[:, channels:]
-    first = (gate_one * conv_one.astype(jnp.float32)).astype(jnp.bfloat16)
-    grad_one = (grad_first.astype(jnp.float32) * gate_one).astype(jnp.bfloat16)
-    second = forward_transform(jnp.concatenate([first, grad_one], axis=1))
+        )
+    ).astype(jnp.bfloat16)
+    conv_one_blocks = middle_rows[..., :channels].astype(jnp.float32)
+    grad_first_blocks = middle_rows[..., channels:].astype(jnp.float32)
+    first = (gate_one_blocks * conv_one_blocks).astype(jnp.bfloat16)
+    grad_one = (grad_first_blocks * gate_one_blocks).astype(jnp.bfloat16)
+    middle = inverse_scatter((grad_first_blocks * conv_one_blocks).astype(jnp.bfloat16))
+    second = forward_core(jnp.concatenate([first, grad_one], axis=2))
     first_spectra = second[..., :channels]
     one_spectra = second[..., channels:]
     closing = inverse_transform(
@@ -235,7 +263,6 @@
     grad_filters = (
         jnp.sum(tap_parts.astype(jnp.float32), axis=0).transpose(1, 0, 2) * grad_scale
     )
-    middle = (grad_first.astype(jnp.float32) * conv_one.astype(jnp.float32)).astype(jnp.bfloat16)
     layer_out = (gate_two * conv_two.astype(jnp.float32)).astype(jnp.bfloat16)
     grad_mixed = jnp.concatenate(
         [

time: 517 us -> 508 us (0.983)
  blocking collectives: 82.4 us -> 31.7 us
  waiting for transfers between devices: 110 us -> 132 us
  starting transfers between devices: 54.1 us -> 67.9 us
    all_to_all x4 -> x1, blocking collectives: 82.4 us -> 31.7 us  [inverse_core(): lax.all_to_all(packed[:, None], 'seq', split_axis=2, concat_axis=1, tiled...]
    all_to_all x4 -> x6, waiting for transfers between devices: 56.3 us -> 78.1 us  [the longest x2 33.8 us: forward_core(): lax.all_to_all(stacked, 'seq', split_axis=1, concat_axis=2, tiled=True)]
    all_to_all x4 -> x6, starting transfers between devices: 26.6 us -> 42.1 us  [the longest x2 13.9 us: forward_core(): lax.all_to_all(stacked, 'seq', split_axis=1, concat_axis=2, tiled=True)]
  transfers between devices with their start and end apart: 9 -> 11, of which waited for: 6 -> 9; matrix products, arithmetic and copies ran while one was open for 7% -> 8% of each run, Pallas kernels for 0% -> 0%
where the time goes in v8:
time: 508 us; the launch traced here: 500 us
  waiting for transfers between devices  132 us (26%)
  matrix products  99.9 us (20%)
  local copies, waits for them, and re-layouts  95.7 us (19%)
  other arithmetic  70.6 us (14%)
  starting transfers between devices  67.9 us (13%)
  blocking collectives  31.7 us (6%)
    dot_general x8, matrix products, dft_pair(): jnp.einsum('yz' + table_part + ',z' + data_part + '->y' + result_side, bl...  87.8 us
    all_to_all x1, waiting for transfers between devices, shards(): lax.all_to_all(jnp.concatenate([proj_flat, taps_row], axis=1), ('dp', 'se...  44.6 us
    all_to_all x2, waiting for transfers between devices, forward_core(): lax.all_to_all(stacked, 'seq', split_axis=1, concat_axis=2, tiled=True)  33.8 us
    all_to_all x1, blocking collectives, inverse_core(): lax.all_to_all(packed[:, None], 'seq', split_axis=2, concat_axis=1, tiled...  31.7 us
    dot_general x2, local copies, waits for them, and re-layouts, dft_pair(): jnp.einsum('yz' + table_part + ',z' + data_part + '->y' + result_side, bl...  21 us
    all_to_all x2, waiting for transfers between devices, inverse_scatter(): lax.all_to_all(values.astype(jnp.bfloat16), 'seq', split_axis=0, concat_a...  17.9 us
    slice x4, local copies, waits for them, and re-layouts, rotate_stacked(): stacked[0] * cosine_table - direction * stacked[1] * sine_table  16.4 us
    all_to_all x1, waiting for transfers between devices, forward_gather(): lax.all_to_all(field.reshape(seq_devices, block_rows, channels), 'seq', s...  16.1 us
  transfers between devices with their start and end apart: 11, of which 9 were waited for; matrix products, arithmetic and copies ran while one was open for 8% of the time, Pallas kernels for 0%

profile of v8, /device:TPU:1, one launch (start us, length us, event | category | flops | bytes accessed | tf_op | source)
XLA Modules:
  0.0 500.2 jit_solution(688472203435162591)
XLA Ops:
  11.9 8.8 %all-to-all-start = ((bf16[32,8,2560]{2,1,0:T(8,128)(2,1)}), bf16[32,8,2560]{2,1,0:T(8,128)(2,1)S(1)}, u32[]{:S(2)}, u32[]{:S(2)}) async-start(bf16[32,8,2560]{2,1,0:T(8,128)(2,1)} %pad_maximum_fusion.3), calls=%async_computation | async-start | bytes 2621440 | tf_op jit(solution)/shard_map/all_to_all | solution.py:102
  21.2 16.1 %all-to-all-done = bf16[32,8,2560]{2,1,0:T(8,128)(2,1)S(1)} async-done(((bf16[32,8,2560]{2,1,0:T(8,128)(2,1)}), bf16[32,8,2560]{2,1,0:T(8,128)(2,1)S(1)}, u32[]{:S(2)}, u32[]{:S(2)}) %all-to-all-start) | async-done | bytes 1310752 | tf_op jit(solution)/shard_map/all_to_all | solution.py:102
  43.3 7.5 %all-to-all-start.1 = ((bf16[2,32,8,2048]{3,2,0,1:T(8,128)(2,1)}), bf16[2,32,8,2048]{3,2,0,1:T(8,128)(2,1)}, u32[]{:S(2)}, u32[]{:S(2)}) async-start(bf16[2,32,8,2048]{3,2,0,1:T(8,128)(2,1)} %copy.175), calls=%async_computation.1 | async-start | bytes 4194304 | tf_op jit(solution)/shard_map/all_to_all | solution.py:134
  54.8 22.8 %all-to-all-done.1 = bf16[2,32,8,2048]{3,2,0,1:T(8,128)(2,1)} async-done(((bf16[2,32,8,2048]{3,2,0,1:T(8,128)(2,1)}), bf16[2,32,8,2048]{3,2,0,1:T(8,128)(2,1)}, u32[]{:S(2)}, u32[]{:S(2)}) %all-to-all-start.1) | async-done | bytes 2097184 | tf_op jit(solution)/shard_map/all_to_all | solution.py:134
  93.8 19.8 %fusion.7 = f32[2,2,2,128,2048]{4,2,0,3,1:T(2,128)S(1)} fusion(f32[2,1,2,128,2048]{4,0,2,3,1:T(2,128)S(1)} %maximum_select_fusion, f32[2,1,2,128,2048]{4,0,2,3,1:T(2,128)S(1)} %select_select_fusion, f32[1,2,2,2]{1,2,3,0:T(2,128)S(1)} %copy-done.43, f32[1,2,2,2]{1,2,3,0:T(2,128)S(1)} %copy-done.41), kind=kOutput, calls=%fused_computation.12 | convolution fusion | flops 52428816 | bytes 16777280 | tf_op jit(solution)/shard_map/yzga,zkabw->ykgbw/dot_general | solution.py:44
  123.7 11.2 %fusion.8 = f32[2,2,2,128,2048]{4,3,0,2,1:T(8,128)S(1)} fusion(f32[2,2,2,128,2048,1]{4,2,0,3,1,5:T(2,128)S(1)} %maximum_bitcast_fusion.1, f32[1,2,128,128]{3,2,1,0:T(8,128)S(1)} %get-tuple-element.119, f32[1,2,128,128]{3,2,1,0:T(8,128)S(1)} %get-tuple-element.122), kind=kOutput, calls=%fused_computation.14 | convolution fusion | flops 3221291008 | bytes 17039360 | tf_op jit(solution)/shard_map/yzfb,zkgbw->ykgfw/dot_general | solution.py:44
  146.6 7.4 %copy.231 = f32[2,2,2,128,1024,1]{4,0,2,5,3,1:T(2,128)} copy(f32[2,2,2,128,1024,1]{3,4,0,2,1,5:T(8,128)} %maximum_bitcast_fusion.9) | data formatting | bytes 8388608 | tf_op jit(solution)/shard_map/stack | solution.py:29
  154.0 11.4 %fusion.21 = f32[2,2,2,128,1024]{4,2,0,3,1:T(2,128)S(1)} fusion(f32[2,2,2,128,1024,1]{4,0,2,5,3,1:T(2,128)} %copy.231, f32[1,2,2,2]{1,2,3,0:T(2,128)S(1)} %copy.191, f32[1,2,2,2]{1,2,3,0:T(2,128)S(1)} %copy.190), kind=kOutput, calls=%fused_computation.33 | convolution fusion | flops 26214416 | bytes 8388672 | tf_op jit(solution)/shard_map/yzag,zkgbw->ykabw/dot_general | solution.py:44
  181.3 10.3 %all-to-all-done.2 = bf16[2,1,256,1024]{3,0,1,2:T(2,128)(2,1)} async-done(((bf16[2,1,256,1024]{3,0,1,2:T(2,128)(2,1)}), bf16[2,1,256,1024]{3,0,1,2:T(2,128)(2,1)}, u32[]{:S(2)}, u32[]{:S(2)}) %all-to-all-start.2) | async-done | bytes 1048608 | tf_op jit(solution)/shard_map/all_to_all | solution.py:163
  207.5 11.0 %all-to-all-done.3 = bf16[2,32,8,1024]{3,2,0,1:T(8,128)(2,1)S(1)} async-done(((bf16[2,32,8,1024]{3,2,0,1:T(8,128)(2,1)}), bf16[2,32,8,1024]{3,2,0,1:T(8,128)(2,1)S(1)}, u32[]{:S(2)}, u32[]{:S(2)}) %all-to-all-start.3) | async-done | bytes 1048608 | tf_op jit(solution)/shard_map/all_to_all | solution.py:134
  226.4 9.6 %fusion.25 = f32[2,128,1024,2,2]{2,4,3,1,0:T(2,128)} fusion(f32[2,1,2,128,1024]{4,0,2,3,1:T(2,128)S(1)} %maximum_select_fusion.1, f32[2,1,2,128,1024]{4,0,2,3,1:T(2,128)S(1)} %select_select_fusion.1, f32[1,2,2,2]{1,2,3,0:T(2,128)S(1)} %copy-done.44, f32[1,2,2,2]{1,2,3,0:T(2,128)S(1)} %copy-done.42), kind=kOutput, calls=%fused_computation.42 | convolution fusion | flops 26214416 | bytes 8388672 | tf_op jit(solution)/shard_map/yzga,zkabw->ykgbw/dot_general | solution.py:44
  236.0 7.7 %copy.205 = f32[2,128,1024,2,2]{1,2,3,4,0:T(8,128)} copy(f32[2,128,1024,2,2]{2,4,3,1,0:T(2,128)} %fusion.25) | data formatting | bytes 8388608 | tf_op jit(solution)/shard_map/yzga,zkabw->ykgbw/dot_general | solution.py:44
  252.5 9.0 %fusion.11 = f32[2,2,2048,2,128]{4,2,3,1,0:T(8,128)} fusion(f32[2,2,2,128,2048,1]{4,3,2,1,0,5:T(8,128)S(1)} %bitcast.258, f32[1,2,128,128]{3,2,1,0:T(8,128)S(1)} %get-tuple-element.123, f32[1,2,128,128]{3,2,1,0:T(8,128)S(1)} %get-tuple-element.118), kind=kOutput, calls=%fused_computation.15 | convolution fusion | flops 3221291008 | bytes 17039360 | tf_op jit(solution)/shard_map/yzbf,zkgfw->ykgbw/dot_general | solution.py:44
  261.5 13.3 %copy.209 = f32[2,2,2048,2,128]{2,1,3,4,0:T(2,128)} copy(f32[2,2,2048,2,128]{4,2,3,1,0:T(8,128)} %fusion.11) | data formatting | bytes 16777216 | tf_op jit(solution)/shard_map/yzbf,zkgfw->ykgbw/dot_general | solution.py:44
  274.8 7.1 %multiply_subtract_fusion = (f32[1,2,2,128,2048]{4,2,0,3,1:T(2,128)S(1)}, f32[1,2,2,128,2048]{4,2,0,3,1:T(2,128)S(1)}) fusion(f32[2,2,2,128,2048]{4,2,0,3,1:T(2,128)} %bitcast.259, f32[2,128]{0,1:T(8,128)S(1)} %copy.210, f32[2,128]{0,1:T(8,128)S(1)} %copy.184), kind=kLoop, calls=%fused_computation.37 | loop fusion | flops 6291456 | bytes 16779264 | tf_op jit(solution)/shard_map/sub | solution.py:31
  281.8 21.0 %fusion = f32[2,2,2,128,2048]{4,2,0,3,1:T(2,128)} fusion(f32[2,2,2,2,1,1]{3,2,1,0,5,4:T(2,128)S(1)} %copy-done.38, f32[1,2,2,128,2048]{4,2,0,3,1:T(2,128)S(1)} %get-tuple-element.80, f32[1,2,2,128,2048]{4,2,0,3,1:T(2,128)S(1)} %get-tuple-element.79), kind=kOutput, calls=%fused_computation.5 | convolution fusion | flops 54525952 | bytes 16777280 | tf_op jit(solution)/shard_map/yzag,zkgbw->ykabw/dot_general | solution.py:44
  302.9 9.6 %fusion.139 = (f32[1,2,2,128,2048]{4,2,0,3,1:T(2,128)}, f32[1,2,2,128,2048]{4,2,0,3,1:T(2,128)S(1)}) fusion(f32[2,2,2,128,2048]{4,2,0,3,1:T(2,128)} %fusion), kind=kLoop, calls=%fused_computation.278 | loop fusion | bytes 16777216 | tf_op jit(solution)/shard_map/slice | solution.py:31
  324.6 31.7 %all_to_all.81 = bf16[2,1,256,2048]{3,0,1,2:T(2,128)(2,1)S(1)} all-to-all(bf16[2,1,256,2048]{3,0,1,2:T(2,128)(2,1)S(1)} %copy.214), channel_id=1, replica_groups=mesh['dp'=4,'seq'=32] {'seq'}, dimensions={2} | all-to-all | bytes 4194304 | tf_op jit(solution)/shard_map/all_to_all | solution.py:163
  359.7 6.6 %all-to-all-start.5 = ((bf16[32,8,2048]{2,1,0:T(8,128)(2,1)}), bf16[32,8,2048]{2,1,0:T(8,128)(2,1)}, u32[]{:S(2)}, u32[]{:S(2)}) async-start(bf16[32,8,2048]{2,1,0:T(8,128)(2,1)} %copy.217), calls=%async_computation.5 | async-start | bytes 2097152 | tf_op jit(solution)/shard_map/all_to_all | solution.py:176
  367.2 13.4 %all-to-all-done.5 = bf16[32,8,2048]{2,1,0:T(8,128)(2,1)} async-done(((bf16[32,8,2048]{2,1,0:T(8,128)(2,1)}), bf16[32,8,2048]{2,1,0:T(8,128)(2,1)}, u32[]{:S(2)}, u32[]{:S(2)}) %all-to-all-start.5) | async-done | bytes 1048608 | tf_op jit(solution)/shard_map/all_to_all | solution.py:176
  402.2 7.2 %all-to-all-start.9 = ((bf16[4,2,256,128]{3,1,2,0:T(2,128)(2,1)}), bf16[4,2,256,128]{3,1,2,0:T(2,128)(2,1)S(1)}, u32[]{:S(2)}, u32[]{:S(2)}) async-start(bf16[4,2,256,128]{3,1,2,0:T(2,128)(2,1)} %bitcast.249), calls=%async_computation.9 | async-start | bytes 1048576 | tf_op jit(solution)/shard_map/all_to_all | solution.py:262
  425.7 8.3 %all-to-all-start.7 = ((f32[128,49,128]{2,1,0:T(8,128)}), f32[128,49,128]{2,1,0:T(8,128)}, u32[]{:S(2)}, u32[]{:S(2)}) async-start(f32[128,49,128]{2,1,0:T(8,128)} %pad_maximum_fusion), calls=%async_computation.7 | async-start | bytes 7340032 | tf_op jit(solution)/shard_map/all_to_all | solution.py:301
  436.7 44.6 %all-to-all-done.7 = f32[128,49,128]{2,1,0:T(8,128)} async-done(((f32[128,49,128]{2,1,0:T(8,128)}), f32[128,49,128]{2,1,0:T(8,128)}, u32[]{:S(2)}, u32[]{:S(2)}) %all-to-all-start.7) | async-done | bytes 3211296 | tf_op jit(solution)/shard_map/all_to_all | solution.py:301
  489.8 9.3 %all-to-all-done.8 = f32[128,1,36]{2,1,0:T(1,128)S(1)} async-done(((f32[128,1,36]{2,1,0:T(1,128)}), f32[128,1,36]{2,1,0:T(1,128)S(1)}, u32[]{:S(2)}, u32[]{:S(2)}) %all-to-all-start.8) | async-done | bytes 18464 | tf_op jit(solution)/shard_map/all_to_all | solution.py:311
  (235 shorter events, 173.5 us)
Async XLA Ops:
  3.6 4.8 collective-permute-start
  11.9 25.3 %all-to-all-start = ((bf16[32,8,2560]{2,1,0:T(8,128)(2,1)}), bf16[32,8,2560]{2,1,0:T(8,128)(2,1)S(1)}, u32[]{:S(2)}, u32[]{:S(2)}) async-start(bf16[32,8,2560]{2,1,0:T(8,128)(2,1)} %pad_maximum_fusion.3), calls=%async_computation | async-start | bytes 2621440 | tf_op jit(solution)/shard_map/all_to_all | solution.py:102
  20.9 18.8 %copy-start.13 = (f32[1,32,32]{2,1,0:T(8,128)}, f32[1,32,32]{2,1,0:T(8,128)S(1)}, u32[]{:S(2)}) copy-start(f32[1,32,32]{2,1,0:T(8,128)S(1)} %scatter.14) | copy-start | bytes 12292
  21.0 18.7 %copy-start.11 = (f32[1,32,32]{2,1,0:T(8,128)}, f32[1,32,32]{2,1,0:T(8,128)S(1)}, u32[]{:S(2)}) copy-start(f32[1,32,32]{2,1,0:T(8,128)S(1)} %fusion.91) | copy-start | bytes 12292
  21.1 18.5 %copy-start.21 = (f32[32,8]{0,1:T(8,128)}, f32[32,8]{0,1:T(8,128)S(1)}, u32[]{:S(2)}) copy-start(f32[32,8]{0,1:T(8,128)S(1)} %get-tuple-element.134) | copy-start | bytes 3076
  21.1 18.5 %copy-start.23 = (f32[32,8]{0,1:T(8,128)}, f32[32,8]{0,1:T(8,128)S(1)}, u32[]{:S(2)}) copy-start(f32[32,8]{0,1:T(8,128)S(1)} %get-tuple-element.135) | copy-start | bytes 3076
  43.3 34.3 %all-to-all-start.1 = ((bf16[2,32,8,2048]{3,2,0,1:T(8,128)(2,1)}), bf16[2,32,8,2048]{3,2,0,1:T(8,128)(2,1)}, u32[]{:S(2)}, u32[]{:S(2)}) async-start(bf16[2,32,8,2048]{3,2,0,1:T(8,128)(2,1)} %copy.175), calls=%async_computation.1 | async-start | bytes 4194304 | tf_op jit(solution)/shard_map/all_to_all | solution.py:134
  53.2 100.8 %copy-start.29 = (f32[1,2,2,2]{1,2,3,0:T(2,128)}, f32[1,2,2,2]{1,2,3,0:T(2,128)S(1)}, u32[]{:S(2)}) copy-start(f32[1,2,2,2]{1,2,3,0:T(2,128)S(1)} %copy.190) | copy-start | bytes 100
  53.3 100.7 %copy-start.30 = (f32[1,2,2,2]{1,2,3,0:T(2,128)}, f32[1,2,2,2]{1,2,3,0:T(2,128)S(1)}, u32[]{:S(2)}) copy-start(f32[1,2,2,2]{1,2,3,0:T(2,128)S(1)} %copy.191) | copy-start | bytes 100
  54.7 113.5 %copy-start.25 = (f32[2,256]{1,0:T(2,128)}, f32[2,256]{1,0:T(2,128)S(1)}, u32[]{:S(2)}) copy-start(f32[2,256]{1,0:T(2,128)S(1)} %get-tuple-element.132) | copy-start | bytes 6148
  54.7 113.5 %copy-start.27 = (f32[2,256]{1,0:T(2,128)}, f32[2,256]{1,0:T(2,128)S(1)}, u32[]{:S(2)}) copy-start(f32[2,256]{1,0:T(2,128)S(1)} %get-tuple-element.133) | copy-start | bytes 6148
  171.2 20.5 %all-to-all-start.2 = ((bf16[2,1,256,1024]{3,0,1,2:T(2,128)(2,1)}), bf16[2,1,256,1024]{3,0,1,2:T(2,128)(2,1)}, u32[]{:S(2)}, u32[]{:S(2)}) async-start(bf16[2,1,256,1024]{3,0,1,2:T(2,128)(2,1)} %copy.195), calls=%async_computation.2 | async-start | bytes 2097152 | tf_op jit(solution)/shard_map/all_to_all | solution.py:163
  177.5 17.6 %copy-start.12 = (f32[1,32,32]{2,1,0:T(8,128)S(1)}, f32[1,32,32]{2,1,0:T(8,128)}, u32[]{:S(2)}) copy-start(f32[1,32,32]{2,1,0:T(8,128)} %copy-done.11) | copy-start | bytes 12292
  177.5 17.6 %copy-start.14 = (f32[1,32,32]{2,1,0:T(8,128)S(1)}, f32[1,32,32]{2,1,0:T(8,128)}, u32[]{:S(2)}) copy-start(f32[1,32,32]{2,1,0:T(8,128)} %copy-done.13) | copy-start | bytes 12292
  180.4 15.4 %copy-start.9 = (f32[1,32,32]{2,1,0:T(8,128)}, f32[1,32,32]{2,1,0:T(8,128)S(1)}, u32[]{:S(2)}) copy-start(f32[1,32,32]{2,1,0:T(8,128)S(1)} %scatter.10) | copy-start | bytes 12292
  197.8 20.8 %all-to-all-start.3 = ((bf16[2,32,8,1024]{3,2,0,1:T(8,128)(2,1)}), bf16[2,32,8,1024]{3,2,0,1:T(8,128)(2,1)S(1)}, u32[]{:S(2)}, u32[]{:S(2)}) async-start(bf16[2,32,8,1024]{3,2,0,1:T(8,128)(2,1)} %copy.198), calls=%async_computation.3 | async-start | bytes 2097152 | tf_op jit(solution)/shard_map/all_to_all | solution.py:134
  324.6 31.7 %copy-start.10 = (f32[1,32,32]{2,1,0:T(8,128)S(1)}, f32[1,32,32]{2,1,0:T(8,128)}, u32[]{:S(2)}) copy-start(f32[1,32,32]{2,1,0:T(8,128)} %copy-done.9) | copy-start | bytes 12292
  359.7 20.8 %all-to-all-start.5 = ((bf16[32,8,2048]{2,1,0:T(8,128)(2,1)}), bf16[32,8,2048]{2,1,0:T(8,128)(2,1)}, u32[]{:S(2)}, u32[]{:S(2)}) async-start(bf16[32,8,2048]{2,1,0:T(8,128)(2,1)} %copy.217), calls=%async_computation.5 | async-start | bytes 2097152 | tf_op jit(solution)/shard_map/all_to_all | solution.py:176
  367.2 29.1 %copy-start.3 = (f32[258,1536]{1,0:T(8,128)S(1)}, f32[258,1536]{1,0:T(8,128)}, u32[]{:S(2)}) copy-start(f32[258,1536]{1,0:T(8,128)} %copy-done.2) | copy-start | bytes 4755460
  380.6 14.6 %all-to-all-start.6 = ((bf16[32,8,512]{2,1,0:T(8,128)(2,1)}), bf16[32,8,512]{2,1,0:T(8,128)(2,1)}, u32[]{:S(2)}, u32[]{:S(2)}) async-start(bf16[32,8,512]{2,1,0:T(8,128)(2,1)} %copy.218), calls=%async_computation.6 | async-start | bytes 524288 | tf_op jit(solution)/shard_map/all_to_all | solution.py:176
  398.0 11.5 %collective-permute-start.1 = (bf16[2,1536]{1,0:T(2,128)(2,1)S(1)}, bf16[2,1536]{1,0:T(2,128)(2,1)S(1)}, u32[]{:S(2)}, u32[]{:S(2)}) collective-permute-start(bf16[2,1536]{1,0:T(2,128)(2,1)S(1)} %slice.483), channel_id=1, source_target_pairs={{1,0},{2,1},{3,2},{4,3},{5,4},{6,5},{7,6},{8,7},{9,8},{10,9},{11,1... | collective-permute-start | bytes 18440 | tf_op jit(solution)/shard_map/ppermute | solution.py:15
  402.2 23.5 %all-to-all-start.9 = ((bf16[4,2,256,128]{3,1,2,0:T(2,128)(2,1)}), bf16[4,2,256,128]{3,1,2,0:T(2,128)(2,1)S(1)}, u32[]{:S(2)}, u32[]{:S(2)}) async-start(bf16[4,2,256,128]{3,1,2,0:T(2,128)(2,1)} %bitcast.249), calls=%async_computation.9 | async-start | bytes 1048576 | tf_op jit(solution)/shard_map/all_to_all | solution.py:262
  425.7 55.6 %all-to-all-start.7 = ((f32[128,49,128]{2,1,0:T(8,128)}), f32[128,49,128]{2,1,0:T(8,128)}, u32[]{:S(2)}, u32[]{:S(2)}) async-start(f32[128,49,128]{2,1,0:T(8,128)} %pad_maximum_fusion), calls=%async_computation.7 | async-start | bytes 7340032 | tf_op jit(solution)/shard_map/all_to_all | solution.py:301
  484.3 14.8 %all-to-all-start.8 = ((f32[128,1,36]{2,1,0:T(1,128)}), f32[128,1,36]{2,1,0:T(1,128)S(1)}, u32[]{:S(2)}, u32[]{:S(2)}) async-start(f32[128,1,36]{2,1,0:T(1,128)} %broadcast_in_dim.27), calls=%async_computation.8 | async-start | bytes 131072 | tf_op jit(solution)/shard_map/all_to_all | solution.py:311
  (34 other events, 134.3 us)

commit v9 on v8

--- a/solution.py
+++ b/solution.py
@@ -242,7 +242,7 @@
     second = forward_core(jnp.concatenate([first, grad_one], axis=2))
     first_spectra = second[..., :channels]
     one_spectra = second[..., channels:]
-    closing = inverse_transform(
+    closing = inverse_core(
         jnp.concatenate(
             [
                 spectral_product(filter_two, first_spectra),
@@ -251,18 +251,23 @@
                 adjoint_product(first_spectra, two_spectra),
             ],
             axis=3,
-        ),
-        False,
-    )
-    conv_two = closing[:, :channels]
-    grad_value = closing[:, channels : 2 * channels]
-    tap_rows = closing[:, 2 * channels :]
+        )
+    )
+    closing_rows = inverse_scatter(closing[..., : 2 * channels])
+    conv_two = closing_rows[:, :channels]
+    grad_value = closing_rows[:, channels:]
     block = channels // data_devices
-    tap_blocks = tap_rows.reshape(frames, 2, data_devices, block).transpose(2, 1, 0, 3)
+    tap_blocks = (
+        closing[..., 2 * channels :]
+        .astype(jnp.bfloat16)
+        .reshape(seq_devices, frames // seq_devices, 2, data_devices, block)
+        .transpose(3, 0, 1, 2, 4)
+        .reshape(data_devices, seq_devices, frames // seq_devices, 2 * block)
+    )
     tap_parts = lax.all_to_all(tap_blocks, "dp", split_axis=0, concat_axis=0, tiled=True)
-    grad_filters = (
-        jnp.sum(tap_parts.astype(jnp.float32), axis=0).transpose(1, 0, 2) * grad_scale
-    )
+    tap_sums = jnp.sum(tap_parts.astype(jnp.float32), axis=0)
+    tap_rows = lax.all_to_all(tap_sums, "seq", split_axis=0, concat_axis=1, tiled=True)
+    grad_filters = tap_rows.reshape(frames, 2, block) * grad_scale
     layer_out = (gate_two * conv_two.astype(jnp.float32)).astype(jnp.bfloat16)
     grad_mixed = jnp.concatenate(
         [

time: 508 us -> 522 us (1.028)
  starting transfers between devices: 67.9 us -> 76.1 us
  waiting for transfers between devices: 132 us -> 140 us
    all_to_all x1, waiting for transfers between devices: 0.01 us -> 8.22 us  [shards(): lax.all_to_all(tap_blocks, 'dp', split_axis=0, concat_axis=0, tiled=True)]
    all_to_all x1, starting transfers between devices: 8.32 us -> 14.5 us  [shards(): lax.all_to_all(jnp.concatenate([proj_flat, taps_row], axis=1), ('dp', 'se...]
    all_to_all x2, waiting for transfers between devices: 17.9 us -> 12.2 us  [inverse_scatter(): lax.all_to_all(values.astype(jnp.bfloat16), 'seq', split_axis=0, concat_a...]
  transfers between devices with their start and end apart: 11 -> 12, of which waited for: 9 -> 11; matrix products, arithmetic and copies ran while one was open for 8% -> 7% of each run, Pallas kernels for 0% -> 0%
where the time goes in v9:
time: 522 us; the launch traced here: 514 us
  waiting for transfers between devices  140 us (27%)
  matrix products  99.9 us (19%)
  local copies, waits for them, and re-layouts  94.2 us (18%)
  starting transfers between devices  76.1 us (15%)
  other arithmetic  70.1 us (13%)
  blocking collectives  31.7 us (6%)
    dot_general x8, matrix products, dft_pair(): jnp.einsum('yz' + table_part + ',z' + data_part + '->y' + result_side, bl...  87.8 us
    all_to_all x1, waiting for transfers between devices, shards(): lax.all_to_all(jnp.concatenate([proj_flat, taps_row], axis=1), ('dp', 'se...  44.2 us
    all_to_all x2, waiting for transfers between devices, forward_core(): lax.all_to_all(stacked, 'seq', split_axis=1, concat_axis=2, tiled=True)  34.7 us
    all_to_all x1, blocking collectives, inverse_core(): lax.all_to_all(packed[:, None], 'seq', split_axis=2, concat_axis=1, tiled...  31.7 us
    dot_general x2, local copies, waits for them, and re-layouts, dft_pair(): jnp.einsum('yz' + table_part + ',z' + data_part + '->y' + result_side, bl...  21 us
    slice x4, local copies, waits for them, and re-layouts, rotate_stacked(): stacked[0] * cosine_table - direction * stacked[1] * sine_table  16.4 us
    all_to_all x1, waiting for transfers between devices, forward_gather(): lax.all_to_all(field.reshape(seq_devices, block_rows, channels), 'seq', s...  16.1 us
    sub x4, other arithmetic, rotate_stacked(): stacked[0] * cosine_table - direction * stacked[1] * sine_table  15.1 us
  transfers between devices with their start and end apart: 12, of which 11 were waited for; matrix products, arithmetic and copies ran while one was open for 7% of the time, Pallas kernels for 0%

profile of v9, /device:TPU:1, one launch (start us, length us, event | category | flops | bytes accessed | tf_op | source)
XLA Modules:
  0.0 513.9 jit_solution(443549525706023669)
XLA Ops:
  11.9 8.8 %all-to-all-start = ((bf16[32,8,2560]{2,1,0:T(8,128)(2,1)}), bf16[32,8,2560]{2,1,0:T(8,128)(2,1)S(1)}, u32[]{:S(2)}, u32[]{:S(2)}) async-start(bf16[32,8,2560]{2,1,0:T(8,128)(2,1)} %pad_maximum_fusion.3), calls=%async_computation | async-start | bytes 2621440 | tf_op jit(solution)/shard_map/all_to_all | solution.py:102
  21.1 16.1 %all-to-all-done = bf16[32,8,2560]{2,1,0:T(8,128)(2,1)S(1)} async-done(((bf16[32,8,2560]{2,1,0:T(8,128)(2,1)}), bf16[32,8,2560]{2,1,0:T(8,128)(2,1)S(1)}, u32[]{:S(2)}, u32[]{:S(2)}) %all-to-all-start) | async-done | bytes 1310752 | tf_op jit(solution)/shard_map/all_to_all | solution.py:102
  43.3 7.5 %all-to-all-start.1 = ((bf16[2,32,8,2048]{3,2,0,1:T(8,128)(2,1)}), bf16[2,32,8,2048]{3,2,0,1:T(8,128)(2,1)}, u32[]{:S(2)}, u32[]{:S(2)}) async-start(bf16[2,32,8,2048]{3,2,0,1:T(8,128)(2,1)} %copy.176), calls=%async_computation.1 | async-start | bytes 4194304 | tf_op jit(solution)/shard_map/all_to_all | solution.py:134
  56.9 20.6 %all-to-all-done.1 = bf16[2,32,8,2048]{3,2,0,1:T(8,128)(2,1)} async-done(((bf16[2,32,8,2048]{3,2,0,1:T(8,128)(2,1)}), bf16[2,32,8,2048]{3,2,0,1:T(8,128)(2,1)}, u32[]{:S(2)}, u32[]{:S(2)}) %all-to-all-start.1) | async-done | bytes 2097184 | tf_op jit(solution)/shard_map/all_to_all | solution.py:134
  93.8 19.8 %fusion.7 = f32[2,2,2,128,2048]{4,2,0,3,1:T(2,128)S(1)} fusion(f32[2,1,2,128,2048]{4,0,2,3,1:T(2,128)S(1)} %maximum_select_fusion, f32[2,1,2,128,2048]{4,0,2,3,1:T(2,128)S(1)} %select_select_fusion, f32[1,2,2,2]{1,2,3,0:T(2,128)S(1)} %copy-done.44, f32[1,2,2,2]{1,2,3,0:T(2,128)S(1)} %copy-done.42), kind=kOutput, calls=%fused_computation.12 | convolution fusion | flops 52428816 | bytes 16777280 | tf_op jit(solution)/shard_map/yzga,zkabw->ykgbw/dot_general | solution.py:44
  123.7 11.2 %fusion.8 = f32[2,2,2,128,2048]{4,3,0,2,1:T(8,128)S(1)} fusion(f32[2,2,2,128,2048,1]{4,2,0,3,1,5:T(2,128)S(1)} %maximum_bitcast_fusion.1, f32[1,2,128,128]{3,2,1,0:T(8,128)S(1)} %get-tuple-element.121, f32[1,2,128,128]{3,2,1,0:T(8,128)S(1)} %get-tuple-element.124), kind=kOutput, calls=%fused_computation.14 | convolution fusion | flops 3221291008 | bytes 17039360 | tf_op jit(solution)/shard_map/yzfb,zkgbw->ykgfw/dot_general | solution.py:44
  146.6 7.4 %copy.232 = f32[2,2,2,128,1024,1]{4,0,2,5,3,1:T(2,128)} copy(f32[2,2,2,128,1024,1]{3,4,0,2,1,5:T(8,128)} %maximum_bitcast_fusion.9) | data formatting | bytes 8388608 | tf_op jit(solution)/shard_map/stack | solution.py:29
  154.0 11.3 %fusion.21 = f32[2,2,2,128,1024]{4,2,0,3,1:T(2,128)S(1)} fusion(f32[2,2,2,128,1024,1]{4,0,2,5,3,1:T(2,128)} %copy.232, f32[1,2,2,2]{1,2,3,0:T(2,128)S(1)} %copy-done.28, f32[1,2,2,2]{1,2,3,0:T(2,128)S(1)} %copy-done.26), kind=kOutput, calls=%fused_computation.33 | convolution fusion | flops 26214416 | bytes 8388672 | tf_op jit(solution)/shard_map/yzag,zkgbw->ykabw/dot_general | solution.py:44
  180.2 11.5 %all-to-all-done.2 = bf16[2,1,256,1024]{3,0,1,2:T(2,128)(2,1)} async-done(((bf16[2,1,256,1024]{3,0,1,2:T(2,128)(2,1)}), bf16[2,1,256,1024]{3,0,1,2:T(2,128)(2,1)}, u32[]{:S(2)}, u32[]{:S(2)}) %all-to-all-start.2) | async-done | bytes 1048608 | tf_op jit(solution)/shard_map/all_to_all | solution.py:163
  205.2 14.1 %all-to-all-done.3 = bf16[2,32,8,1024]{3,2,0,1:T(8,128)(2,1)S(1)} async-done(((bf16[2,32,8,1024]{3,2,0,1:T(8,128)(2,1)}), bf16[2,32,8,1024]{3,2,0,1:T(8,128)(2,1)S(1)}, u32[]{:S(2)}, u32[]{:S(2)}) %all-to-all-start.3) | async-done | bytes 1048608 | tf_op jit(solution)/shard_map/all_to_all | solution.py:134
  226.5 9.6 %fusion.25 = f32[2,128,1024,2,2]{2,4,3,1,0:T(2,128)} fusion(f32[2,1,2,128,1024]{4,0,2,3,1:T(2,128)S(1)} %maximum_select_fusion.1, f32[2,1,2,128,1024]{4,0,2,3,1:T(2,128)S(1)} %select_select_fusion.1, f32[1,2,2,2]{1,2,3,0:T(2,128)S(1)} %copy-done.45, f32[1,2,2,2]{1,2,3,0:T(2,128)S(1)} %copy-done.43), kind=kOutput, calls=%fused_computation.42 | convolution fusion | flops 26214416 | bytes 8388672 | tf_op jit(solution)/shard_map/yzga,zkabw->ykgbw/dot_general | solution.py:44
  236.1 7.7 %copy.206 = f32[2,128,1024,2,2]{1,2,3,4,0:T(8,128)} copy(f32[2,128,1024,2,2]{2,4,3,1,0:T(2,128)} %fusion.25) | data formatting | bytes 8388608 | tf_op jit(solution)/shard_map/yzga,zkabw->ykgbw/dot_general | solution.py:44
  252.6 9.0 %fusion.11 = f32[2,2,2048,2,128]{4,2,3,1,0:T(8,128)} fusion(f32[2,2,2,128,2048,1]{4,3,2,1,0,5:T(8,128)S(1)} %bitcast.260, f32[1,2,128,128]{3,2,1,0:T(8,128)S(1)} %get-tuple-element.125, f32[1,2,128,128]{3,2,1,0:T(8,128)S(1)} %get-tuple-element.120), kind=kOutput, calls=%fused_computation.15 | convolution fusion | flops 3221291008 | bytes 17039360 | tf_op jit(solution)/shard_map/yzbf,zkgfw->ykgbw/dot_general | solution.py:44
  261.6 13.3 %copy.210 = f32[2,2,2048,2,128]{2,1,3,4,0:T(2,128)} copy(f32[2,2,2048,2,128]{4,2,3,1,0:T(8,128)} %fusion.11) | data formatting | bytes 16777216 | tf_op jit(solution)/shard_map/yzbf,zkgfw->ykgbw/dot_general | solution.py:44
  274.9 7.1 %multiply_subtract_fusion = (f32[1,2,2,128,2048]{4,2,0,3,1:T(2,128)S(1)}, f32[1,2,2,128,2048]{4,2,0,3,1:T(2,128)S(1)}) fusion(f32[2,2,2,128,2048]{4,2,0,3,1:T(2,128)} %bitcast.261, f32[2,128]{0,1:T(8,128)S(1)} %copy.211, f32[2,128]{0,1:T(8,128)S(1)} %copy.185), kind=kLoop, calls=%fused_computation.37 | loop fusion | flops 6291456 | bytes 16779264 | tf_op jit(solution)/shard_map/sub | solution.py:31
  282.0 21.0 %fusion = f32[2,2,2,128,2048]{4,2,0,3,1:T(2,128)} fusion(f32[2,2,2,2,1,1]{3,2,1,0,5,4:T(2,128)S(1)} %copy.243, f32[1,2,2,128,2048]{4,2,0,3,1:T(2,128)S(1)} %get-tuple-element.80, f32[1,2,2,128,2048]{4,2,0,3,1:T(2,128)S(1)} %get-tuple-element.79), kind=kOutput, calls=%fused_computation.5 | convolution fusion | flops 54525952 | bytes 16777280 | tf_op jit(solution)/shard_map/yzag,zkgbw->ykabw/dot_general | solution.py:44
  303.0 9.6 %fusion.139 = (f32[1,2,2,128,2048]{4,2,0,3,1:T(2,128)}, f32[1,2,2,128,2048]{4,2,0,3,1:T(2,128)S(1)}) fusion(f32[2,2,2,128,2048]{4,2,0,3,1:T(2,128)} %fusion), kind=kLoop, calls=%fused_computation.278 | loop fusion | bytes 16777216 | tf_op jit(solution)/shard_map/slice | solution.py:31
  324.8 31.7 %all_to_all.90 = bf16[2,1,256,2048]{3,0,1,2:T(2,128)(2,1)S(1)} all-to-all(bf16[2,1,256,2048]{3,0,1,2:T(2,128)(2,1)S(1)} %copy.215), channel_id=1, replica_groups=mesh['dp'=4,'seq'=32] {'seq'}, dimensions={2} | all-to-all | bytes 4194304 | tf_op jit(solution)/shard_map/all_to_all | solution.py:163
  359.9 8.0 %all-to-all-start.9 = ((bf16[4,32,8,256]{3,2,1,0:T(8,128)(2,1)}), bf16[4,32,8,256]{3,2,1,0:T(8,128)(2,1)S(1)}, u32[]{:S(2)}, u32[]{:S(2)}) async-start(bf16[4,32,8,256]{3,2,1,0:T(8,128)(2,1)} %bitcast.251), calls=%async_computation.9 | async-start | bytes 1048576 | tf_op jit(solution)/shard_map/all_to_all | solution.py:267
  369.0 8.2 %all-to-all-done.9 = bf16[4,32,8,256]{3,2,1,0:T(8,128)(2,1)S(1)} async-done(((bf16[4,32,8,256]{3,2,1,0:T(8,128)(2,1)}), bf16[4,32,8,256]{3,2,1,0:T(8,128)(2,1)S(1)}, u32[]{:S(2)}, u32[]{:S(2)}) %all-to-all-start.9) | async-done | bytes 524320 | tf_op jit(solution)/shard_map/all_to_all | solution.py:267
  382.3 8.6 %all-to-all-done.5 = bf16[32,8,1024]{2,1,0:T(8,128)(2,1)S(1)} async-done(((bf16[32,8,1024]{2,1,0:T(8,128)(2,1)}), bf16[32,8,1024]{2,1,0:T(8,128)(2,1)S(1)}, u32[]{:S(2)}, u32[]{:S(2)}) %all-to-all-start.5) | async-done | bytes 524320 | tf_op jit(solution)/shard_map/all_to_all | solution.py:176
  433.1 14.5 %all-to-all-start.7 = ((f32[128,49,128]{2,1,0:T(8,128)}), f32[128,49,128]{2,1,0:T(8,128)}, u32[]{:S(2)}, u32[]{:S(2)}) async-start(f32[128,49,128]{2,1,0:T(8,128)} %pad_maximum_fusion), calls=%async_computation.7 | async-start | bytes 7340032 | tf_op jit(solution)/shard_map/all_to_all | solution.py:306
  450.7 44.2 %all-to-all-done.7 = f32[128,49,128]{2,1,0:T(8,128)} async-done(((f32[128,49,128]{2,1,0:T(8,128)}), f32[128,49,128]{2,1,0:T(8,128)}, u32[]{:S(2)}, u32[]{:S(2)}) %all-to-all-start.7) | async-done | bytes 3211296 | tf_op jit(solution)/shard_map/all_to_all | solution.py:306
  503.4 9.3 %all-to-all-done.8 = f32[128,1,36]{2,1,0:T(1,128)S(1)} async-done(((f32[128,1,36]{2,1,0:T(1,128)}), f32[128,1,36]{2,1,0:T(1,128)S(1)}, u32[]{:S(2)}, u32[]{:S(2)}) %all-to-all-start.8) | async-done | bytes 18464 | tf_op jit(solution)/shard_map/all_to_all | solution.py:316
  (240 shorter events, 181.7 us)
Async XLA Ops:
  3.6 4.8 collective-permute-start
  11.9 25.3 %all-to-all-start = ((bf16[32,8,2560]{2,1,0:T(8,128)(2,1)}), bf16[32,8,2560]{2,1,0:T(8,128)(2,1)S(1)}, u32[]{:S(2)}, u32[]{:S(2)}) async-start(bf16[32,8,2560]{2,1,0:T(8,128)(2,1)} %pad_maximum_fusion.3), calls=%async_computation | async-start | bytes 2621440 | tf_op jit(solution)/shard_map/all_to_all | solution.py:102
  20.9 18.8 %copy-start.10 = (f32[1,32,32]{2,1,0:T(8,128)}, f32[1,32,32]{2,1,0:T(8,128)S(1)}, u32[]{:S(2)}) copy-start(f32[1,32,32]{2,1,0:T(8,128)S(1)} %scatter.14) | copy-start | bytes 12292
  21.1 18.5 %copy-start.18 = (f32[32,8]{0,1:T(8,128)}, f32[32,8]{0,1:T(8,128)S(1)}, u32[]{:S(2)}) copy-start(f32[32,8]{0,1:T(8,128)S(1)} %get-tuple-element.136) | copy-start | bytes 3076
  21.1 18.5 %copy-start.20 = (f32[32,8]{0,1:T(8,128)}, f32[32,8]{0,1:T(8,128)S(1)}, u32[]{:S(2)}) copy-start(f32[32,8]{0,1:T(8,128)S(1)} %get-tuple-element.137) | copy-start | bytes 3076
  43.3 34.3 %all-to-all-start.1 = ((bf16[2,32,8,2048]{3,2,0,1:T(8,128)(2,1)}), bf16[2,32,8,2048]{3,2,0,1:T(8,128)(2,1)}, u32[]{:S(2)}, u32[]{:S(2)}) async-start(bf16[2,32,8,2048]{3,2,0,1:T(8,128)(2,1)} %copy.176), calls=%async_computation.1 | async-start | bytes 4194304 | tf_op jit(solution)/shard_map/all_to_all | solution.py:134
  171.2 20.5 %all-to-all-start.2 = ((bf16[2,1,256,1024]{3,0,1,2:T(2,128)(2,1)}), bf16[2,1,256,1024]{3,0,1,2:T(2,128)(2,1)}, u32[]{:S(2)}, u32[]{:S(2)}) async-start(bf16[2,1,256,1024]{3,0,1,2:T(2,128)(2,1)} %copy.196), calls=%async_computation.2 | async-start | bytes 2097152 | tf_op jit(solution)/shard_map/all_to_all | solution.py:163
  177.5 18.3 %copy-start.11 = (f32[1,32,32]{2,1,0:T(8,128)S(1)}, f32[1,32,32]{2,1,0:T(8,128)}, u32[]{:S(2)}) copy-start(f32[1,32,32]{2,1,0:T(8,128)} %copy-done.10) | copy-start | bytes 12292
  196.9 8.0 %copy-start.35 = (f32[2,128]{1,0:T(2,128)S(1)}, f32[2,128]{1,0:T(2,128)}, u32[]{:S(2)}) copy-start(f32[2,128]{1,0:T(2,128)} %get-tuple-element.144) | copy-start | bytes 3076
  196.9 8.1 %copy-start.27 = (f32[1,2,2,2]{1,2,3,0:T(2,128)S(1)}, f32[1,2,2,2]{1,2,3,0:T(2,128)}, u32[]{:S(2)}) copy-start(f32[1,2,2,2]{1,2,3,0:T(2,128)} %copy.191) | copy-start | bytes 100
  197.0 8.1 %copy-start.29 = (f32[1,2,2,2]{1,2,3,0:T(2,128)S(1)}, f32[1,2,2,2]{1,2,3,0:T(2,128)}, u32[]{:S(2)}) copy-start(f32[1,2,2,2]{1,2,3,0:T(2,128)} %copy.192) | copy-start | bytes 100
  197.0 22.3 %copy-start.36 = (f32[256]{0:T(256)S(1)}, f32[256]{0:T(256)}, u32[]{:S(2)}) copy-start(f32[256]{0:T(256)} %get-tuple-element.140) | copy-start | bytes 3076
  197.0 22.3 %copy-start.37 = (f32[256]{0:T(256)S(1)}, f32[256]{0:T(256)}, u32[]{:S(2)}) copy-start(f32[256]{0:T(256)} %get-tuple-element.141) | copy-start | bytes 3076
  198.5 20.8 %all-to-all-start.3 = ((bf16[2,32,8,1024]{3,2,0,1:T(8,128)(2,1)}), bf16[2,32,8,1024]{3,2,0,1:T(8,128)(2,1)S(1)}, u32[]{:S(2)}, u32[]{:S(2)}) async-start(bf16[2,32,8,1024]{3,2,0,1:T(8,128)(2,1)} %copy.199), calls=%async_computation.3 | async-start | bytes 2097152 | tf_op jit(solution)/shard_map/all_to_all | solution.py:134
  236.1 7.7 %copy-start.39 = (f32[2,128]{1,0:T(2,128)S(1)}, f32[2,128]{1,0:T(2,128)}, u32[]{:S(2)}) copy-start(f32[2,128]{1,0:T(2,128)} %copy-done.38) | copy-start | bytes 3076
  358.8 22.7 %copy-start.8 = (bf16[32,8,512]{2,0,1:T(8,128)(2,1)S(1)}, bf16[32,8,512]{2,0,1:T(8,128)(2,1)}, u32[]{:S(2)}) copy-start(bf16[32,8,512]{2,0,1:T(8,128)(2,1)} %get-tuple-element.117) | copy-start | bytes 786436
  359.9 17.3 %all-to-all-start.9 = ((bf16[4,32,8,256]{3,2,1,0:T(8,128)(2,1)}), bf16[4,32,8,256]{3,2,1,0:T(8,128)(2,1)S(1)}, u32[]{:S(2)}, u32[]{:S(2)}) async-start(bf16[4,32,8,256]{3,2,1,0:T(8,128)(2,1)} %bitcast.251), calls=%async_computation.9 | async-start | bytes 1048576 | tf_op jit(solution)/shard_map/all_to_all | solution.py:267
  377.2 13.6 %all-to-all-start.5 = ((bf16[32,8,1024]{2,1,0:T(8,128)(2,1)}), bf16[32,8,1024]{2,1,0:T(8,128)(2,1)S(1)}, u32[]{:S(2)}, u32[]{:S(2)}) async-start(bf16[32,8,1024]{2,1,0:T(8,128)(2,1)} %copy.218), calls=%async_computation.5 | async-start | bytes 1048576 | tf_op jit(solution)/shard_map/all_to_all | solution.py:176
  390.8 13.8 %all-to-all-start.6 = ((bf16[32,8,512]{2,1,0:T(8,128)(2,1)}), bf16[32,8,512]{2,1,0:T(8,128)(2,1)}, u32[]{:S(2)}, u32[]{:S(2)}) async-start(bf16[32,8,512]{2,1,0:T(8,128)(2,1)} %copy.219), calls=%async_computation.6 | async-start | bytes 524288 | tf_op jit(solution)/shard_map/all_to_all | solution.py:176
  397.3 13.0 %copy-start.3 = (f32[258,1536]{1,0:T(8,128)S(1)}, f32[258,1536]{1,0:T(8,128)}, u32[]{:S(2)}) copy-start(f32[258,1536]{1,0:T(8,128)} %copy-done.2) | copy-start | bytes 4755460
  404.6 28.4 %all-to-all-start.10 = ((f32[32,8,256]{2,1,0:T(8,128)}), f32[32,8,256]{2,1,0:T(8,128)}, u32[]{:S(2)}, u32[]{:S(2)}) async-start(f32[32,8,256]{2,1,0:T(8,128)} %convert_reduce_fusion), calls=%async_computation.10 | async-start | bytes 524288 | tf_op jit(solution)/shard_map/all_to_all | solution.py:269
  412.0 4.8 collective-permute-start.1
  433.1 61.8 %all-to-all-start.7 = ((f32[128,49,128]{2,1,0:T(8,128)}), f32[128,49,128]{2,1,0:T(8,128)}, u32[]{:S(2)}, u32[]{:S(2)}) async-start(f32[128,49,128]{2,1,0:T(8,128)} %pad_maximum_fusion), calls=%async_computation.7 | async-start | bytes 7340032 | tf_op jit(solution)/shard_map/all_to_all | solution.py:306
  497.9 14.8 %all-to-all-start.8 = ((f32[128,1,36]{2,1,0:T(1,128)}), f32[128,1,36]{2,1,0:T(1,128)S(1)}, u32[]{:S(2)}, u32[]{:S(2)}) async-start(f32[128,1,36]{2,1,0:T(1,128)} %broadcast_in_dim.27), calls=%async_computation.8 | async-start | bytes 131072 | tf_op jit(solution)/shard_map/all_to_all | solution.py:316
  (36 other events, 121.4 us)
